TPU v7x, 256 devices: a whole 4x4x8 slice. The times are simulated.
256 devices in a mesh: dp: 128 (over y, z, x_lo, core), rows: 2 (over x_hi).
Axes of the slice: x: 4 (x_hi: 2, x_lo: 2; x = x_hi * 2 + x_lo), y: 4, z: 8, core: 2. Of those that a mesh axis runs over, the one named last changes fastest.
Arguments:
- features: bfloat16 [128, 32, 32, 768], P('dp', 'rows'), may hold values from -24 to 24
- bucket: int32 [128], P('dp'), may hold values from 0 to 16, as said below
- kernel: float32 [7, 7, 768], replicated, may hold values from -0.875 to 0.875
- up_weight: bfloat16 [768, 2816], P('dp'), may hold values from -0.21875 to 0.21875
- down_weight: bfloat16 [2816, 768], P('dp'), may hold values from -0.109375 to 0.109375
- cotangent: bfloat16 [128, 32, 32, 768], P('dp', 'rows'), may hold values from -6 to 6
Outputs:
- block_out: bfloat16 [128, 32, 32, 768], P('dp', 'rows')
- feature_grad: bfloat16 [128, 32, 32, 768], P('dp', 'rows')
- up_grad: float32 [768, 2816], P('dp')
- down_grad: float32 [2816, 768], P('dp')
- kernel_grad: float32 [7, 7, 768], replicated
Inputs may be any that keep to these rules, and one draw needn't show every extreme that they name: `bucket`: both ends of the range occur in every draw.
All inputs are finite; a program needn't handle non-finite values.
Results may differ from a plain program's by a relative error of at most 0.0075.
Values may be sent and summed in bfloat16 or wider, within the bound.
No kernel may reach another device: no remote copies, remote signals or barrier semaphores. Data moves between devices by JAX's collectives and lax.ppermute only.
A program may use at most 128 MiB of HBM per device.

v0:
```python
import jax
import jax.numpy as jnp
from jax import lax
from jax.sharding import Mesh
from jax.sharding import PartitionSpec as P

INV_ROOT_TWO = 0.7071067811865476
INV_ROOT_TAU = 0.3989422804014327
EPSILON = 1e-06

AXES = ("y", "z", "xl", "c", "rows")
SIZES = (4, 8, 2, 2, 2)
DP = AXES[:4]
SIZE = dict(zip(AXES, SIZES))


def ring_scatter(x, axis, wire):
    n = SIZE[axis]
    me = lax.axis_index(axis)
    dim = AXES.index(axis)

    def block(j):
        return lax.dynamic_slice_in_dim(x, j % n, 1, dim)

    if n == 2:
        got = lax.ppermute(block(me + 1).astype(wire), axis, [(0, 1), (1, 0)])
        return block(me) + got.astype(jnp.float32)
    half = x.shape[-1] // 2
    acc_r = block(me - 1)[..., :half]
    acc_l = block(me + 1)[..., half:]
    for s in range(1, n):
        got_r = lax.ppermute(acc_r.astype(wire), axis, [(i, (i + 1) % n) for i in range(n)])
        got_l = lax.ppermute(acc_l.astype(wire), axis, [(i, (i - 1) % n) for i in range(n)])
        j_r, j_l = (me - s - 1, me + s + 1) if s < n - 1 else (me, me)
        acc_r = got_r.astype(jnp.float32) + block(j_r)[..., :half]
        acc_l = got_l.astype(jnp.float32) + block(j_l)[..., half:]
    return jnp.concatenate([acc_r, acc_l], axis=-1)


def ring_gather_rows(x, axis):
    n = SIZE[axis]
    me = lax.axis_index(axis)
    m = x.shape[0]
    out = jnp.zeros((n * m,) + x.shape[1:], x.dtype)
    out = lax.dynamic_update_slice_in_dim(out, x, me * m, 0)
    right = n // 2
    left = n - 1 - right
    cur = x
    for s in range(1, right + 1):
        cur = lax.ppermute(cur, axis, [(i, (i + 1) % n) for i in range(n)])
        out = lax.dynamic_update_slice_in_dim(out, cur, ((me - s) % n) * m, 0)
    cur = x
    for s in range(1, left + 1):
        cur = lax.ppermute(cur, axis, [(i, (i - 1) % n) for i in range(n)])
        out = lax.dynamic_update_slice_in_dim(out, cur, ((me + s) % n) * m, 0)
    return out


def gather_weight(shard):
    for axis in ("c", "xl", "y", "z"):
        shard = ring_gather_rows(shard, axis)
    shard = shard.reshape(SIZE["z"], SIZE["y"], -1, shard.shape[1]).transpose(1, 0, 2, 3)
    return shard.reshape(-1, shard.shape[3])


def reduce_weight_grad(term, order):
    rows = term.shape[0] // 128
    view = term.reshape(*SIZES[:4], 1, rows, term.shape[1])
    for axis in order:
        view = ring_scatter(view, axis, jnp.bfloat16)
    tiles = view.reshape(rows, term.shape[1])
    return tiles + lax.ppermute(tiles, "rows", [(0, 1), (1, 0)])


def butterfly_sum(x):
    for axis, n in zip(AXES, SIZES):
        d = 1
        while d < n:
            x = x + lax.ppermute(x, axis, [(i, i ^ d) for i in range(n)])
            d *= 2
    return x


def padded_2(block, sides, width):
    for axis, dim in sides:
        count = lax.axis_size(axis)
        forward = [(i, i + 1) for i in range(count - 1)]
        backward = [(target, source) for source, target in forward]
        low = lax.ppermute(
            lax.slice_in_dim(block, block.shape[dim] - width, None, axis=dim), axis, forward
        )
        high = lax.ppermute(lax.slice_in_dim(block, 0, width, axis=dim), axis, backward)
        block = jnp.concatenate([low, block, high], axis=dim)
    return block


def gelu_parts(pre_act):
    normal_cdf = 0.5 * (1.0 + lax.erf(pre_act * INV_ROOT_TWO))
    density = jnp.exp(-0.5 * pre_act * pre_act) * INV_ROOT_TAU
    return (pre_act * normal_cdf, normal_cdf + pre_act * density)


def depthwise(padded, kernel, out_rows, out_cols, flipped):
    span = kernel.shape[0]
    result = jnp.zeros(padded.shape[:-3] + (out_rows, out_cols, padded.shape[-1]), jnp.float32)
    for offset_row in range(span):
        for offset_col in range(span):
            start_row = span - 1 - offset_row if flipped else offset_row
            start_col = span - 1 - offset_col if flipped else offset_col
            result = (
                result
                + kernel[offset_row, offset_col]
                * padded[..., start_row : start_row + out_rows, start_col : start_col + out_cols, :]
            )
    return result


def kernel_terms(grad_conv, padded, span):
    reduce_axes = tuple(range(grad_conv.ndim - 1))
    rows_out = grad_conv.shape[-3]
    cols_out = grad_conv.shape[-2]
    kernel_rows = []
    for offset_row in range(span):
        kernel_row = []
        for offset_col in range(span):
            window = padded[
                ..., offset_row : offset_row + rows_out, offset_col : offset_col + cols_out, :
            ]
            kernel_row.append(jnp.sum(grad_conv * window, axis=reduce_axes))
        kernel_rows.append(jnp.stack(kernel_row))
    return jnp.stack(kernel_rows)


def layer_norm(convolved):
    centered = convolved - jnp.mean(convolved, axis=-1, keepdims=True)
    inv_std = lax.rsqrt(jnp.mean(centered * centered, axis=-1, keepdims=True) + EPSILON)
    return (centered * inv_std, inv_std)


def norm_backward(grad_norm, unit_norm, inv_std):
    first_mean = jnp.mean(grad_norm, axis=-1, keepdims=True)
    second_mean = jnp.mean(grad_norm * unit_norm, axis=-1, keepdims=True)
    return inv_std * (grad_norm - first_mean - unit_norm * second_mean)


def on_device(features, bucket, kernel, up_weight, down_weight, cotangent):
    images, strip_rows, canvas_cols, channels = features.shape
    rows_count = lax.axis_size("rows")
    row_index = lax.axis_index("rows")
    canvas_rows = strip_rows * rows_count
    area_cells = canvas_rows * canvas_cols // 2
    reach = kernel.shape[0] // 2
    grad_scale = 1.0 / (images * lax.axis_size(DP))
    heights = canvas_rows // 2 + bucket
    widths = jnp.minimum(canvas_cols, area_cells // heights)
    row_ids = row_index * strip_rows + lax.iota(jnp.int32, strip_rows)
    col_ids = lax.iota(jnp.int32, canvas_cols)
    inside = (row_ids[None, :, None] < heights[:, None, None]) & (
        col_ids[None, None, :] < widths[:, None, None]
    )
    inside_cells = inside[..., None]
    masked = jnp.where(inside_cells, features, jnp.zeros((), features.dtype))
    masked_cot = jnp.where(inside_cells, cotangent, jnp.zeros((), cotangent.dtype))
    up_full = gather_weight(up_weight)
    down_full = gather_weight(down_weight)
    rimmed = padded_2(masked, (("rows", 1),), reach)
    padded = jnp.pad(rimmed, ((0, 0), (0, 0), (reach, reach), (0, 0)))
    convolved = jnp.where(
        inside_cells, depthwise(padded, kernel, strip_rows, canvas_cols, False), 0.0
    )
    unit_norm, inv_std = layer_norm(convolved)
    normed = unit_norm.astype(jnp.bfloat16)
    tokens = normed.reshape(images * strip_rows * canvas_cols, channels)
    cot_rows = masked_cot.reshape(images * strip_rows * canvas_cols, channels)

    pre_act = jnp.dot(tokens, up_full, preferred_element_type=jnp.float32)
    hidden, derivative = gelu_parts(pre_act)
    activation = hidden.astype(jnp.bfloat16)
    down_term = lax.dot_general(
        activation, cot_rows, (((0,), (0,)), ((), ())), preferred_element_type=jnp.float32
    )
    down_grad = reduce_weight_grad(down_term * grad_scale, ("c", "y", "z", "xl"))
    branch = jnp.dot(activation, down_full, preferred_element_type=jnp.float32)
    grad_act = lax.dot_general(
        cot_rows, down_full, (((1,), (1,)), ((), ())), preferred_element_type=jnp.float32
    )
    grad_pre = (grad_act * derivative).astype(jnp.bfloat16)
    up_term = lax.dot_general(
        tokens, grad_pre, (((0,), (0,)), ((), ())), preferred_element_type=jnp.float32
    )
    up_grad = reduce_weight_grad(up_term * grad_scale, ("c", "z", "y", "xl"))
    grad_rows = lax.dot_general(
        grad_pre, up_full, (((1,), (1,)), ((), ())), preferred_element_type=jnp.float32
    )

    branch = branch.reshape(features.shape)
    grad_norm = grad_rows.reshape(features.shape)
    block_out = (masked + branch).astype(jnp.bfloat16)
    grad_conv = jnp.where(inside_cells, norm_backward(grad_norm, unit_norm, inv_std), 0.0)
    kernel_grad = butterfly_sum(kernel_terms(grad_conv, padded, kernel.shape[0]) * grad_scale)
    grad_rimmed = padded_2(grad_conv.astype(jnp.bfloat16), (("rows", 1),), reach).astype(
        grad_conv.dtype
    )
    grad_padded = jnp.pad(grad_rimmed, ((0, 0), (0, 0), (reach, reach), (0, 0)))
    feature_grad = jnp.where(
        inside_cells,
        masked_cot + depthwise(grad_padded, kernel, strip_rows, canvas_cols, True),
        0.0,
    ).astype(jnp.bfloat16)
    return (block_out, feature_grad, up_grad, down_grad, kernel_grad)


def solution(mesh):
    torus = Mesh(mesh.devices.reshape(SIZES), AXES)
    strips = P(DP, "rows", None, None)
    return jax.shard_map(
        on_device,
        mesh=torus,
        in_specs=(strips, P(DP), P(), P(DP, None), P(DP, None), strips),
        out_specs=(strips, strips, P(DP, None), P(DP, None), P()),
        check_vma=False,
    )
```

profile of v0, /device:TPU:2, one launch (start us, length us, event | category | flops | bytes accessed | tf_op | source)
XLA Modules:
  0.0 394.7 jit_solution(846783701808002252)
XLA Ops:
  4.5 4.2 %collective-permute-start = (bf16[1,3,32,768]{3,2,1,0:T(8,128)(2,1)S(1)}, bf16[1,3,32,768]{3,2,1,0:T(8,128)(2,1)S(1)}, u32[]{:S(2)}, u32[]{:S(2)}) collective-permute-start(bf16[1,3,32,768]{3,2,1,0:T(8,128)(2,1)S(1)} %get-tuple-element.136), channel_id=1, source_target_pairs={{0,1},{2,3},{4,5},{6,7},{8,9},{10,11},{12,13},{14,15},{16,17},{18,... | collective-permute-start | bytes 442376 | tf_op jit(solution)/shard_map/ppermute | solution.py:89
  18.4 3.1 collective-permute-start.18
  22.1 3.3 collective-permute-start.6
  27.4 16.3 %fusion.294 = (f32[16,32]{1,0:T(8,128)S(1)}, f32[1,16,32,768]{3,2,1,0:T(8,128)S(1)}) fusion(bf16[1,22,38,768]{3,2,1,0:T(8,128)(2,1)S(1)} %fusion.203, f32[768]{0:T(1024)S(1)} %copy-done.82, f32[768]{0:T(1024)S(1)} %copy-done.84, f32[768]{0:T(1024)S(1)} %copy-done.28, bf16[1,3,32,768]{3,2,1,0:T(8,128)(2,1)S(1)} %collective-permute-done.1, ...), kind=kLoop, calls=%fused_computation.640 | loop fusion | flops 60554752 | bytes 35837440 | tf_op jit(solution)/shard_map/reduce_sum | solution.py:135
  46.1 4.1 %collective-permute-done.17 = bf16[88,768]{1,0:T(8,128)(2,1)S(1)} collective-permute-done((bf16[88,768]{1,0:T(8,128)(2,1)}, bf16[88,768]{1,0:T(8,128)(2,1)S(1)}, u32[]{:S(2)}, u32[]{:S(2)}) %collective-permute-start.17) | collective-permute-done | bytes 135200 | tf_op jit(solution)/shard_map/ppermute | solution.py:50
  60.0 10.2 %collective-permute-done.19 = bf16[352,768]{1,0:T(8,128)(2,1)S(1)} collective-permute-done((bf16[352,768]{1,0:T(8,128)(2,1)S(1)}, bf16[352,768]{1,0:T(8,128)(2,1)S(1)}, u32[]{:S(2)}, u32[]{:S(2)}) %collective-permute-start.19) | collective-permute-done | bytes 540704 | tf_op jit(solution)/shard_map/ppermute | solution.py:50
  70.4 11.3 %collective-permute-done.7 = bf16[96,2816]{1,0:T(8,128)(2,1)S(1)} collective-permute-done((bf16[96,2816]{1,0:T(8,128)(2,1)S(1)}, bf16[96,2816]{1,0:T(8,128)(2,1)S(1)}, u32[]{:S(2)}, u32[]{:S(2)}) %collective-permute-start.7) | collective-permute-done | bytes 540704 | tf_op jit(solution)/shard_map/ppermute | solution.py:50
  82.1 15.9 %collective-permute-start.12 = (bf16[96,2816]{1,0:T(8,128)(2,1)S(1)}, bf16[96,2816]{1,0:T(8,128)(2,1)S(1)}, u32[]{:S(2)}, u32[]{:S(2)}) collective-permute-start(bf16[96,2816]{1,0:T(8,128)(2,1)S(1)} %collective-permute-done.11), channel_id=1, source_target_pairs={{0,56},{8,0},{16,8},{24,16},{32,24},{40,32},{48,40},{56,48},{1,57}... | collective-permute-start | bytes 1622024 | tf_op jit(solution)/shard_map/ppermute | solution.py:54
  100.5 4.5 %collective-permute-done.8 = bf16[96,2816]{1,0:T(8,128)(2,1)S(1)} collective-permute-done((bf16[96,2816]{1,0:T(8,128)(2,1)S(1)}, bf16[96,2816]{1,0:T(8,128)(2,1)S(1)}, u32[]{:S(2)}, u32[]{:S(2)}) %collective-permute-start.8) | collective-permute-done | bytes 540704 | tf_op jit(solution)/shard_map/ppermute | solution.py:50
  105.0 5.7 %collective-permute-done.12 = bf16[96,2816]{1,0:T(8,128)(2,1)S(1)} collective-permute-done((bf16[96,2816]{1,0:T(8,128)(2,1)S(1)}, bf16[96,2816]{1,0:T(8,128)(2,1)S(1)}, u32[]{:S(2)}, u32[]{:S(2)}) %collective-permute-start.12) | collective-permute-done | bytes 540704 | tf_op jit(solution)/shard_map/ppermute | solution.py:54
  110.7 3.7 collective-permute-start.13
  114.4 7.9 %collective-permute-done.24 = bf16[352,768]{1,0:T(8,128)(2,1)S(1)} collective-permute-done((bf16[352,768]{1,0:T(8,128)(2,1)S(1)}, bf16[352,768]{1,0:T(8,128)(2,1)S(1)}, u32[]{:S(2)}, u32[]{:S(2)}) %collective-permute-start.24) | collective-permute-done | bytes 540704 | tf_op jit(solution)/shard_map/ppermute | solution.py:54
  122.3 3.7 collective-permute-start.25
  128.2 13.3 %collective-permute-done.22 = bf16[352,768]{1,0:T(8,128)(2,1)S(1)} collective-permute-done((bf16[352,768]{1,0:T(8,128)(2,1)S(1)}, bf16[352,768]{1,0:T(8,128)(2,1)S(1)}, u32[]{:S(2)}, u32[]{:S(2)}) %collective-permute-start.22) | collective-permute-done | bytes 540704 | tf_op jit(solution)/shard_map/ppermute | solution.py:50
  142.1 5.3 %collective-permute-done.10 = bf16[96,2816]{1,0:T(8,128)(2,1)S(1)} collective-permute-done((bf16[96,2816]{1,0:T(8,128)(2,1)S(1)}, bf16[96,2816]{1,0:T(8,128)(2,1)S(1)}, u32[]{:S(2)}, u32[]{:S(2)}) %collective-permute-start.10) | collective-permute-done | bytes 540704 | tf_op jit(solution)/shard_map/ppermute | solution.py:50
  147.9 4.3 %multiply_convert_fusion = (bf16[512,2816]{1,0:T(8,128)(2,1)}, f32[512,2816]{1,0:T(8,128)S(1)}) fusion(bf16[512,768]{1,0:T(8,128)(2,1)S(1)} %bitcast.65, bf16[768,2816]{1,0:T(8,128)(2,1)S(1)} %bitcast.61), kind=kOutput, calls=%fused_computation.52 | convolution fusion | flops 2221801472 | bytes 13762560 | tf_op jit(solution)/shard_map/dot_general | solution.py:176
  152.2 3.7 fusion.5
  155.9 3.6 fusion.298
  161.6 4.7 %fusion.102 = (f32[768]{0:T(1024)S(1)}, f32[768]{0:T(1024)S(1)}, f32[768]{0:T(1024)S(1)}, f32[768]{0:T(1024)S(1)}, f32[768]{0:T(1024)S(1)}, /*index=5*/f32[768]{...) fusion(bf16[1,22,38,768]{3,2,1,0:T(8,128)(2,1)S(1)} %fusion.203, ...), kind=kLoop, calls=%fused_computation.284 | loop fusion | flops 23972352 | bytes 18938368 | tf_op jit(solution)/shard_map/reduce_sum | solution.py:129
  167.6 4.0 %fusion.81 = (f32[768]{0:T(1024)S(1)}, f32[768]{0:T(1024)S(1)}, f32[768]{0:T(1024)S(1)}, f32[768]{0:T(1024)S(1)}, f32[768]{0:T(1024)S(1)}, /*index=5*/f32[768]{0...) fusion(f32[1,16,32,768]{3,2,1,0:T(8,128)S(1)} %get-tuple-elemen, ...), kind=kLoop, calls=%fused_computation.263 | loop fusion | flops 21613056 | bytes 16570368 | tf_op jit(solution)/shard_map/reduce_sum | solution.py:129
  171.7 5.8 %convolution_multiply_fusion.1 = f32[768,2816]{1,0:T(8,128)} fusion(bf16[512,768]{1,0:T(8,128)(2,1)S(1)} %bitcast.66, bf16[512,2816]{1,0:T(8,128)(2,1)S(1)} %copy-done.11), kind=kOutput, calls=%fused_computation.44 | convolution fusion | flops 2216755200 | bytes 12320768 | tf_op jit(solution)/shard_map/dot_general | solution.py:188
  180.3 9.8 %reshape.362 = f32[4,8,2,2,1,6,2816]{6,5,3,2,1,0,4:T(8,128)} reshape(f32[768,2816]{1,0:T(8,128)} %convolution_multiply_fusion.1) | data formatting | bytes 17301504 | tf_op jit(solution)/shard_map/reshape | solution.py:68
  195.1 3.2 collective-permute-start.75
  198.3 5.1 %collective-permute-done.75 = f32[7,7,768]{2,1,0:T(8,128)S(1)} collective-permute-done((f32[7,7,768]{2,1,0:T(8,128)S(1)}, f32[7,7,768]{2,1,0:T(8,128)S(1)}, u32[]{:S(2)}, u32[]{:S(2)}) %collective-permute-start.75) | collective-permute-done | bytes 150560 | tf_op jit(solution)/shard_map/ppermute | solution.py:79
  203.6 7.6 %convolution_multiply_fusion = f32[2816,768]{1,0:T(8,128)} fusion(bf16[512,2816]{1,0:T(8,128)(2,1)} %get-tuple-element.148, bf16[512,768]{1,0:T(8,128)(2,1)S(1)} %bitcast.64), kind=kOutput, calls=%fused_computation.43 | convolution fusion | flops 2216755200 | bytes 12320768 | tf_op jit(solution)/shard_map/dot_general | solution.py:179
  211.2 9.4 %reshape.364 = f32[4,8,2,2,1,22,768]{6,5,3,2,1,0,4:T(8,128)} reshape(f32[2816,768]{1,0:T(8,128)} %convolution_multiply_fusion) | data formatting | bytes 17301504 | tf_op jit(solution)/shard_map/reshape | solution.py:68
  227.1 4.2 %collective-permute-done.77 = f32[7,7,768]{2,1,0:T(8,128)S(1)} collective-permute-done((f32[7,7,768]{2,1,0:T(8,128)S(1)}, f32[7,7,768]{2,1,0:T(8,128)S(1)}, u32[]{:S(2)}, u32[]{:S(2)}) %collective-permute-start.77) | collective-permute-done | bytes 150560 | tf_op jit(solution)/shard_map/ppermute | solution.py:79
  231.3 4.4 %collective-permute-start.78 = (f32[7,7,768]{2,1,0:T(8,128)S(1)}, f32[7,7,768]{2,1,0:T(8,128)S(1)}, u32[]{:S(2)}, u32[]{:S(2)}) collective-permute-start(f32[7,7,768]{2,1,0:T(8,128)S(1)} %add.1210), channel_id=1, source_target_pairs={{0,32},{8,40},{16,48},{24,56},{32,0},{40,8},{48,16},{56,24},{1,33}... | collective-permute-start | bytes 451592 | tf_op jit(solution)/shard_map/ppermute | solution.py:79
  235.7 5.8 %collective-permute-start.26 = (bf16[1,3,32,768]{3,2,1,0:T(8,128)(2,1)S(1)}, bf16[1,3,32,768]{3,2,1,0:T(8,128)(2,1)S(1)}, u32[]{:S(2)}, u32[]{:S(2)}) collective-permute-start(bf16[1,3,32,768]{3,2,1,0:T(8,128)(2,1)S(1)} %get-tuple-element.134), channel_id=1, source_target_pairs={{0,1},{2,3},{4,5},{6,7},{8,9},{10,11},{12,13},{14,15},{16,17},{18,... | collective-permute-start | bytes 442376 | tf_op jit(solution)/shard_map/ppermute | solution.py:89
  245.7 5.7 %fusion.103 = bf16[1,16,32,768]{3,2,1,0:T(8,128)(2,1)} fusion(bf16[1,16,32,768]{3,2,1,0:T(8,128)(2,1)S(1)} %copy-done.1, bf16[16,32,2816]{2,1,0:T(8,128)(2,1)S(1)} %bitcast.67, bf16[2816,768,1]{1,0,2:T(8,128)(2,1)} %bitcast.60), kind=kOutput, calls=%fused_computation.285 | convolution fusion | flops 2215772160 | bytes 8781824 | tf_op jit(solution)/shard_map/dot_general | solution.py:183
  253.0 3.5 collective-permute-start.81
  256.5 5.2 %convert_add_fusion = f32[4,8,2,1,1,6,2816]{6,5,3,2,1,0,4:T(8,128)} fusion(f32[4,8,2,2,1,6,2816]{6,5,3,2,1,0,4:T(8,128)S(1)} %bitcast.51, s32[]{:T(128)S(6)} %select_n.496, bf16[4,8,2,1,1,6,2816]{6,1,5,4,3,2,0:T(8,128)(2,1)} %collective-permute-done.28), kind=kLoop, calls=%fused_computation.51 | loop fusion | flops 2162688 | bytes 10813444 | tf_op jit(solution)/shard_map/add | solution.py:27
  265.0 3.0 convert_add_fusion.1
  272.1 4.3 %collective-permute-done.55 = bf16[1,8,2,1,1,22,384]{6,5,3,2,1,0,4:T(8,128)(2,1)S(1)} collective-permute-done((bf16[1,8,2,1,1,22,384]{6,5,3,2,1,0,4:T(8,128)(2,1)S(1)}, bf16[1,8,2,1,1,22,384]{6,5,3,2,1,0,4:T(8,128)(2,1)S(1)}, u32[]{:S(2)}, u32[]{:S(2)}) %collective-permute-start.55) | collective-permute-done | bytes 270368 | tf_op jit(solution)/shard_map/ppermute | solution.py:33
  284.2 3.7 collective-permute-start.57
  292.2 3.7 collective-permute-done.53
  299.0 5.2 %collective-permute-done.54 = bf16[1,8,2,1,1,22,384]{6,5,3,2,1,0,4:T(8,128)(2,1)S(1)} collective-permute-done((bf16[1,8,2,1,1,22,384]{6,5,3,2,1,0,4:T(8,128)(2,1)S(1)}, bf16[1,8,2,1,1,22,384]{6,5,3,2,1,0,4:T(8,128)(2,1)S(1)}, u32[]{:S(2)}, u32[]{:S(2)}) %collective-permute-start.54) | collective-permute-done | bytes 270368 | tf_op jit(solution)/shard_map/ppermute | solution.py:32
  308.6 3.2 collective-permute-start.66
  322.8 3.3 collective-permute-start.68
  326.1 3.4 collective-permute-done.35
  333.6 3.3 collective-permute-start.70
  340.4 5.1 %collective-permute-done.59 = bf16[1,1,2,1,1,22,384]{6,5,3,2,1,0,4:T(8,128)(2,1)S(1)} collective-permute-done((bf16[1,1,2,1,1,22,384]{6,5,3,2,1,0,4:T(8,128)(2,1)S(1)}, bf16[1,1,2,1,1,22,384]{6,5,3,2,1,0,4:T(8,128)(2,1)S(1)}, u32[]{:S(2)}, u32[]{:S(2)}) %collective-permute-start.59) | collective-permute-done | bytes 33824 | tf_op jit(solution)/shard_map/ppermute | solution.py:32
  345.7 3.3 collective-permute-start.47
  351.3 3.3 collective-permute-start.48
  356.7 3.2 collective-permute-done.44
  365.2 3.3 collective-permute-start.71
  370.5 3.2 collective-permute-done.64
  379.9 12.6 %fusion.194 = bf16[1,16,32,768]{3,2,1,0:T(8,128)(2,1)} fusion(f32[1,22,32,768]{3,2,1,0:T(8,128)S(1)} %maximum_convert_fusion, f32[768]{0:T(1024)S(1)} %copy-done.83, f32[768]{0:T(1024)S(1)} %copy-done.85, f32[768]{0:T(1024)S(1)} %copy-done.29, f32[768]{0:T(1024)S(1)} %copy-done.31, f32[768]{0:T(1024)S(1)} %copy-done.33, f32[768]{0:T(1024)S(1)} %copy-done.35, ...), kind=kLoop, calls=%fused_computation.376 | loop fusion | flops 40108032 | bytes 14948352 | tf_op jit(solution)/shard_map/convert_element_type | solution.py:209
  (502 shorter events, 121.0 us)
Async XLA Ops:
  0.6 11.8 %collective-permute-start.14 = (bf16[22,768]{1,0:T(8,128)(2,1)}, bf16[22,768]{1,0:T(8,128)(2,1)S(1)}, u32[]{:S(2)}, u32[]{:S(2)}) collective-permute-start(bf16[22,768]{1,0:T(8,128)(2,1)} %param.10), channel_id=1, source_target_pairs={{0,2},{2,0},{1,3},{3,1},{4,6},{6,4},{5,7},{7,5},{8,10},{10,8},{9,1... | collective-permute-start | bytes 101384 | tf_op jit(solution)/shard_map/ppermute | solution.py:50
  0.7 13.7 %collective-permute-start.2 = (bf16[6,2816]{1,0:T(8,128)(2,1)}, bf16[6,2816]{1,0:T(8,128)(2,1)S(1)}, u32[]{:S(2)}, u32[]{:S(2)}) collective-permute-start(bf16[6,2816]{1,0:T(8,128)(2,1)} %param.9), channel_id=1, source_target_pairs={{0,2},{2,0},{1,3},{3,1},{4,6},{6,4},{5,7},{7,5},{8,10},{10,8},{9,1... | collective-permute-start | bytes 101384 | tf_op jit(solution)/shard_map/ppermute | solution.py:50
  4.5 21.4 %collective-permute-start = (bf16[1,3,32,768]{3,2,1,0:T(8,128)(2,1)S(1)}, bf16[1,3,32,768]{3,2,1,0:T(8,128)(2,1)S(1)}, u32[]{:S(2)}, u32[]{:S(2)}) collective-permute-start(bf16[1,3,32,768]{3,2,1,0:T(8,128)(2,1)S(1)} %get-tuple-element.136), channel_id=1, source_target_pairs={{0,1},{2,3},{4,5},{6,7},{8,9},{10,11},{12,13},{14,15},{16,17},{18,... | collective-permute-start | bytes 442376 | tf_op jit(solution)/shard_map/ppermute | solution.py:89
  8.7 17.7 %collective-permute-start.1 = (bf16[1,3,32,768]{3,2,1,0:T(8,128)(2,1)S(1)}, bf16[1,3,32,768]{3,2,1,0:T(8,128)(2,1)S(1)}, u32[]{:S(2)}, u32[]{:S(2)}) collective-permute-start(bf16[1,3,32,768]{3,2,1,0:T(8,128)(2,1)S(1)} %get-tuple-element.137), channel_id=1, source_target_pairs={{1,0},{3,2},{5,4},{7,6},{9,8},{11,10},{13,12},{15,14},{17,16},{19,... | collective-permute-start | bytes 442376 | tf_op jit(solution)/shard_map/ppermute | solution.py:92
  18.4 31.8 %collective-permute-start.18 = (bf16[88,768]{1,0:T(8,128)(2,1)S(1)}, bf16[88,768]{1,0:T(8,128)(2,1)}, u32[]{:S(2)}, u32[]{:S(2)}) collective-permute-start(bf16[88,768]{1,0:T(8,128)(2,1)S(1)} %dynamic_update_slice.115), channel_id=1, source_target_pairs={{0,192},{64,0},{128,64},{192,128},{1,193},{65,1},{129,65},{193,129... | collective-permute-start | bytes 405512 | tf_op jit(solution)/shard_map/ppermute | solution.py:54
  21.5 22.1 %collective-permute-start.16 = (bf16[88,768]{1,0:T(8,128)(2,1)S(1)}, bf16[88,768]{1,0:T(8,128)(2,1)}, u32[]{:S(2)}, u32[]{:S(2)}) collective-permute-start(bf16[88,768]{1,0:T(8,128)(2,1)S(1)} %dynamic_update_slice.115), channel_id=1, source_target_pairs={{0,64},{64,128},{128,192},{192,0},{1,65},{65,129},{129,193},{193,1... | collective-permute-start | bytes 405512 | tf_op jit(solution)/shard_map/ppermute | solution.py:50
  22.1 31.0 %collective-permute-start.6 = (bf16[24,2816]{1,0:T(8,128)(2,1)S(1)}, bf16[24,2816]{1,0:T(8,128)(2,1)S(1)}, u32[]{:S(2)}, u32[]{:S(2)}) collective-permute-start(bf16[24,2816]{1,0:T(8,128)(2,1)S(1)} %dynamic_update_slice.99), channel_id=1, source_target_pairs={{0,192},{64,0},{128,64},{192,128},{1,193},{65,1},{129,65},{193,129... | collective-permute-start | bytes 405512 | tf_op jit(solution)/shard_map/ppermute | solution.py:54
  25.9 17.8 %collective-permute-start.4 = (bf16[24,2816]{1,0:T(8,128)(2,1)S(1)}, bf16[24,2816]{1,0:T(8,128)(2,1)S(1)}, u32[]{:S(2)}, u32[]{:S(2)}) collective-permute-start(bf16[24,2816]{1,0:T(8,128)(2,1)S(1)} %dynamic_update_slice.99), channel_id=1, source_target_pairs={{0,64},{64,128},{128,192},{192,0},{1,65},{65,129},{129,193},{193,1... | collective-permute-start | bytes 405512 | tf_op jit(solution)/shard_map/ppermute | solution.py:50
  43.7 9.4 %collective-permute-start.5 = (bf16[24,2816]{1,0:T(8,128)(2,1)S(1)}, bf16[24,2816]{1,0:T(8,128)(2,1)S(1)}, u32[]{:S(2)}, u32[]{:S(2)}) collective-permute-start(bf16[24,2816]{1,0:T(8,128)(2,1)S(1)} %collective-permute-done.4), channel_id=1, source_target_pairs={{0,64},{64,128},{128,192},{192,0},{1,65},{65,129},{129,193},{193,1... | collective-permute-start | bytes 405512 | tf_op jit(solution)/shard_map/ppermute | solution.py:50
  51.1 19.1 %collective-permute-start.19 = (bf16[352,768]{1,0:T(8,128)(2,1)S(1)}, bf16[352,768]{1,0:T(8,128)(2,1)S(1)}, u32[]{:S(2)}, u32[]{:S(2)}) collective-permute-start(bf16[352,768]{1,0:T(8,128)(2,1)S(1)} %constant_dynamic-update-slice_fusion.8), channel_id=1, source_target_pairs={{0,8},{8,16},{16,24},{24,32},{32,40},{40,48},{48,56},{56,0},{1,9},... | collective-permute-start | bytes 1622024 | tf_op jit(solution)/shard_map/ppermute | solution.py:50
  53.1 28.7 %collective-permute-start.7 = (bf16[96,2816]{1,0:T(8,128)(2,1)S(1)}, bf16[96,2816]{1,0:T(8,128)(2,1)S(1)}, u32[]{:S(2)}, u32[]{:S(2)}) collective-permute-start(bf16[96,2816]{1,0:T(8,128)(2,1)S(1)} %constant_dynamic-update-slice_fusion.20), channel_id=1, source_target_pairs={{0,8},{8,16},{16,24},{24,32},{32,40},{40,48},{48,56},{56,0},{1,9},... | collective-permute-start | bytes 1622024 | tf_op jit(solution)/shard_map/ppermute | solution.py:50
  55.5 26.7 %collective-permute-start.11 = (bf16[96,2816]{1,0:T(8,128)(2,1)S(1)}, bf16[96,2816]{1,0:T(8,128)(2,1)S(1)}, u32[]{:S(2)}, u32[]{:S(2)}) collective-permute-start(bf16[96,2816]{1,0:T(8,128)(2,1)S(1)} %constant_dynamic-update-slice_fusion.20), channel_id=1, source_target_pairs={{0,56},{8,0},{16,8},{24,16},{32,24},{40,32},{48,40},{56,48},{1,57}... | collective-permute-start | bytes 1622024 | tf_op jit(solution)/shard_map/ppermute | solution.py:54
  58.0 40.0 %collective-permute-start.23 = (bf16[352,768]{1,0:T(8,128)(2,1)S(1)}, bf16[352,768]{1,0:T(8,128)(2,1)S(1)}, u32[]{:S(2)}, u32[]{:S(2)}) collective-permute-start(bf16[352,768]{1,0:T(8,128)(2,1)S(1)} %constant_dynamic-update-slice_fusion.8), channel_id=1, source_target_pairs={{0,56},{8,0},{16,8},{24,16},{32,24},{40,32},{48,40},{56,48},{1,57}... | collective-permute-start | bytes 1622024 | tf_op jit(solution)/shard_map/ppermute | solution.py:54
  70.2 29.0 %collective-permute-start.20 = (bf16[352,768]{1,0:T(8,128)(2,1)S(1)}, bf16[352,768]{1,0:T(8,128)(2,1)S(1)}, u32[]{:S(2)}, u32[]{:S(2)}) collective-permute-start(bf16[352,768]{1,0:T(8,128)(2,1)S(1)} %collective-permute-done.19), channel_id=1, source_target_pairs={{0,8},{8,16},{16,24},{24,32},{32,40},{40,48},{48,56},{56,0},{1,9},... | collective-permute-start | bytes 1622024 | tf_op jit(solution)/shard_map/ppermute | solution.py:50
  81.8 23.2 %collective-permute-start.8 = (bf16[96,2816]{1,0:T(8,128)(2,1)S(1)}, bf16[96,2816]{1,0:T(8,128)(2,1)S(1)}, u32[]{:S(2)}, u32[]{:S(2)}) collective-permute-start(bf16[96,2816]{1,0:T(8,128)(2,1)S(1)} %collective-permute-done.7), channel_id=1, source_target_pairs={{0,8},{8,16},{16,24},{24,32},{32,40},{40,48},{48,56},{56,0},{1,9},... | collective-permute-start | bytes 1622024 | tf_op jit(solution)/shard_map/ppermute | solution.py:50
  82.1 28.6 %collective-permute-start.12 = (bf16[96,2816]{1,0:T(8,128)(2,1)S(1)}, bf16[96,2816]{1,0:T(8,128)(2,1)S(1)}, u32[]{:S(2)}, u32[]{:S(2)}) collective-permute-start(bf16[96,2816]{1,0:T(8,128)(2,1)S(1)} %collective-permute-done.11), channel_id=1, source_target_pairs={{0,56},{8,0},{16,8},{24,16},{32,24},{40,32},{48,40},{56,48},{1,57}... | collective-permute-start | bytes 1622024 | tf_op jit(solution)/shard_map/ppermute | solution.py:54
  98.0 24.3 %collective-permute-start.24 = (bf16[352,768]{1,0:T(8,128)(2,1)S(1)}, bf16[352,768]{1,0:T(8,128)(2,1)S(1)}, u32[]{:S(2)}, u32[]{:S(2)}) collective-permute-start(bf16[352,768]{1,0:T(8,128)(2,1)S(1)} %collective-permute-done.23), channel_id=1, source_target_pairs={{0,56},{8,0},{16,8},{24,16},{32,24},{40,32},{48,40},{56,48},{1,57}... | collective-permute-start | bytes 1622024 | tf_op jit(solution)/shard_map/ppermute | solution.py:54
  99.2 26.9 %collective-permute-start.21 = (bf16[352,768]{1,0:T(8,128)(2,1)S(1)}, bf16[352,768]{1,0:T(8,128)(2,1)S(1)}, u32[]{:S(2)}, u32[]{:S(2)}) collective-permute-start(bf16[352,768]{1,0:T(8,128)(2,1)S(1)} %collective-permute-done.20), channel_id=1, source_target_pairs={{0,8},{8,16},{16,24},{24,32},{32,40},{40,48},{48,56},{56,0},{1,9},... | collective-permute-start | bytes 1622024 | tf_op jit(solution)/shard_map/ppermute | solution.py:50
  105.0 23.2 %collective-permute-start.9 = (bf16[96,2816]{1,0:T(8,128)(2,1)S(1)}, bf16[96,2816]{1,0:T(8,128)(2,1)S(1)}, u32[]{:S(2)}, u32[]{:S(2)}) collective-permute-start(bf16[96,2816]{1,0:T(8,128)(2,1)S(1)} %collective-permute-done.8), channel_id=1, source_target_pairs={{0,8},{8,16},{16,24},{24,32},{32,40},{40,48},{48,56},{56,0},{1,9},... | collective-permute-start | bytes 1622024 | tf_op jit(solution)/shard_map/ppermute | solution.py:50
  110.7 36.8 %collective-permute-start.13 = (bf16[96,2816]{1,0:T(8,128)(2,1)S(1)}, bf16[96,2816]{1,0:T(8,128)(2,1)S(1)}, u32[]{:S(2)}, u32[]{:S(2)}) collective-permute-start(bf16[96,2816]{1,0:T(8,128)(2,1)S(1)} %collective-permute-done.12), channel_id=1, source_target_pairs={{0,56},{8,0},{16,8},{24,16},{32,24},{40,32},{48,40},{56,48},{1,57}... | collective-permute-start | bytes 1622024 | tf_op jit(solution)/shard_map/ppermute | solution.py:54
  122.3 19.4 %collective-permute-start.25 = (bf16[352,768]{1,0:T(8,128)(2,1)S(1)}, bf16[352,768]{1,0:T(8,128)(2,1)S(1)}, u32[]{:S(2)}, u32[]{:S(2)}) collective-permute-start(bf16[352,768]{1,0:T(8,128)(2,1)S(1)} %collective-permute-done.24), channel_id=1, source_target_pairs={{0,56},{8,0},{16,8},{24,16},{32,24},{40,32},{48,40},{56,48},{1,57}... | collective-permute-start | bytes 1622024 | tf_op jit(solution)/shard_map/ppermute | solution.py:54
  126.1 15.5 %collective-permute-start.22 = (bf16[352,768]{1,0:T(8,128)(2,1)S(1)}, bf16[352,768]{1,0:T(8,128)(2,1)S(1)}, u32[]{:S(2)}, u32[]{:S(2)}) collective-permute-start(bf16[352,768]{1,0:T(8,128)(2,1)S(1)} %collective-permute-done.21), channel_id=1, source_target_pairs={{0,8},{8,16},{16,24},{24,32},{32,40},{40,48},{48,56},{56,0},{1,9},... | collective-permute-start | bytes 1622024 | tf_op jit(solution)/shard_map/ppermute | solution.py:50
  128.1 19.2 %collective-permute-start.10 = (bf16[96,2816]{1,0:T(8,128)(2,1)S(1)}, bf16[96,2816]{1,0:T(8,128)(2,1)S(1)}, u32[]{:S(2)}, u32[]{:S(2)}) collective-permute-start(bf16[96,2816]{1,0:T(8,128)(2,1)S(1)} %collective-permute-done.9), channel_id=1, source_target_pairs={{0,8},{8,16},{16,24},{24,32},{32,40},{40,48},{48,56},{56,0},{1,9},... | collective-permute-start | bytes 1622024 | tf_op jit(solution)/shard_map/ppermute | solution.py:50
  179.8 15.2 %collective-permute-start.74 = (f32[7,7,768]{2,1,0:T(8,128)S(1)}, f32[7,7,768]{2,1,0:T(8,128)S(1)}, u32[]{:S(2)}, u32[]{:S(2)}) collective-permute-start(f32[7,7,768]{2,1,0:T(8,128)S(1)} %broadcast_multiply_fusion), channel_id=1, source_target_pairs={{0,64},{64,0},{128,192},{192,128},{1,65},{65,1},{129,193},{193,129... | collective-permute-start | bytes 451592 | tf_op jit(solution)/shard_map/ppermute | solution.py:79
  195.0 61.5 %collective-permute-start.28 = (bf16[4,8,2,1,1,6,2816]{6,1,5,4,3,2,0:T(8,128)(2,1)}, bf16[4,8,2,1,1,6,2816]{6,1,5,4,3,2,0:T(8,128)(2,1)}, u32[]{:S(2)}, u32[]{:S(2)}) collective-permute-start(bf16[4,8,2,1,1,6,2816]{6,1,5,4,3,2,0:T(8,128)(2,1)} %copy.36), channel_id=1, source_target_pairs={{0,2},{2,0},{1,3},{3,1},{4,6},{6,4},{5,7},{7,5},{8,10},{10,8},{9,1... | collective-permute-start | bytes 6488072 | tf_op jit(solution)/shard_map/ppermute | solution.py:26
  195.1 8.4 %collective-permute-start.75 = (f32[7,7,768]{2,1,0:T(8,128)S(1)}, f32[7,7,768]{2,1,0:T(8,128)S(1)}, u32[]{:S(2)}, u32[]{:S(2)}) collective-permute-start(f32[7,7,768]{2,1,0:T(8,128)S(1)} %fusion.293), channel_id=1, source_target_pairs={{0,128},{64,192},{128,0},{192,64},{1,129},{65,193},{129,1},{193,65... | collective-permute-start | bytes 451592 | tf_op jit(solution)/shard_map/ppermute | solution.py:79
  203.5 17.1 %collective-permute-start.76 = (f32[7,7,768]{2,1,0:T(8,128)S(1)}, f32[7,7,768]{2,1,0:T(8,128)S(1)}, u32[]{:S(2)}, u32[]{:S(2)}) collective-permute-start(f32[7,7,768]{2,1,0:T(8,128)S(1)} %add.1208), channel_id=1, source_target_pairs={{0,8},{8,0},{16,24},{24,16},{32,40},{40,32},{48,56},{56,48},{1,9},... | collective-permute-start | bytes 451592 | tf_op jit(solution)/shard_map/ppermute | solution.py:79
  220.6 10.7 %collective-permute-start.77 = (f32[7,7,768]{2,1,0:T(8,128)S(1)}, f32[7,7,768]{2,1,0:T(8,128)S(1)}, u32[]{:S(2)}, u32[]{:S(2)}) collective-permute-start(f32[7,7,768]{2,1,0:T(8,128)S(1)} %add.1209), channel_id=1, source_target_pairs={{0,16},{8,24},{16,0},{24,8},{32,48},{40,56},{48,32},{56,40},{1,17}... | collective-permute-start | bytes 451592 | tf_op jit(solution)/shard_map/ppermute | solution.py:79
  227.1 37.9 %collective-permute-start.51 = (bf16[4,8,2,1,1,22,768]{6,1,5,4,3,2,0:T(8,128)(2,1)}, bf16[4,8,2,1,1,22,768]{6,1,5,4,3,2,0:T(8,128)(2,1)}, u32[]{:S(2)}, u32[]{:S(2)}) collective-permute-start(bf16[4,8,2,1,1,22,768]{6,1,5,4,3,2,0:T(8,128)(2,1)} %copy.35), channel_id=1, source_target_pairs={{0,2},{2,0},{1,3},{3,1},{4,6},{6,4},{5,7},{7,5},{8,10},{10,8},{9,1... | collective-permute-start | bytes 6488072 | tf_op jit(solution)/shard_map/ppermute | solution.py:26
  231.3 12.8 %collective-permute-start.78 = (f32[7,7,768]{2,1,0:T(8,128)S(1)}, f32[7,7,768]{2,1,0:T(8,128)S(1)}, u32[]{:S(2)}, u32[]{:S(2)}) collective-permute-start(f32[7,7,768]{2,1,0:T(8,128)S(1)} %add.1210), channel_id=1, source_target_pairs={{0,32},{8,40},{16,48},{24,56},{32,0},{40,8},{48,16},{56,24},{1,33}... | collective-permute-start | bytes 451592 | tf_op jit(solution)/shard_map/ppermute | solution.py:79
  235.7 15.8 %collective-permute-start.26 = (bf16[1,3,32,768]{3,2,1,0:T(8,128)(2,1)S(1)}, bf16[1,3,32,768]{3,2,1,0:T(8,128)(2,1)S(1)}, u32[]{:S(2)}, u32[]{:S(2)}) collective-permute-start(bf16[1,3,32,768]{3,2,1,0:T(8,128)(2,1)S(1)} %get-tuple-element.134), channel_id=1, source_target_pairs={{0,1},{2,3},{4,5},{6,7},{8,9},{10,11},{12,13},{14,15},{16,17},{18,... | collective-permute-start | bytes 442376 | tf_op jit(solution)/shard_map/ppermute | solution.py:89
  241.5 10.1 %collective-permute-start.27 = (bf16[1,3,32,768]{3,2,1,0:T(8,128)(2,1)S(1)}, bf16[1,3,32,768]{3,2,1,0:T(8,128)(2,1)S(1)}, u32[]{:S(2)}, u32[]{:S(2)}) collective-permute-start(bf16[1,3,32,768]{3,2,1,0:T(8,128)(2,1)S(1)} %get-tuple-element.135), channel_id=1, source_target_pairs={{1,0},{3,2},{5,4},{7,6},{9,8},{11,10},{13,12},{15,14},{17,16},{19,... | collective-permute-start | bytes 442376 | tf_op jit(solution)/shard_map/ppermute | solution.py:92
  253.0 139.6 %collective-permute-start.81 = (f32[7,7,768]{2,1,0:T(8,128)S(1)}, f32[7,7,768]{2,1,0:T(8,128)S(1)}, u32[]{:S(2)}, u32[]{:S(2)}) collective-permute-start(f32[7,7,768]{2,1,0:T(8,128)S(1)} %add.1213), channel_id=1, source_target_pairs={{0,1},{1,0},{2,3},{3,2},{4,5},{5,4},{6,7},{7,6},{8,9},{9,8},{10,11... | collective-permute-start | bytes 451592 | tf_op jit(solution)/shard_map/ppermute | solution.py:79
  263.9 15.4 %collective-permute-start.29 = (bf16[4,1,2,1,1,6,1408]{6,5,3,2,1,0,4:T(8,128)(2,1)S(1)}, bf16[4,1,2,1,1,6,1408]{6,5,3,2,1,0,4:T(8,128)(2,1)S(1)}, u32[]{:S(2)}, u32[]{:S(2)}) collective-permute-start(bf16[4,1,2,1,1,6,1408]{6,5,3,2,1,0,4:T(8,128)(2,1)S(1)} %get-tuple-element.122), channel_id=1, source_target_pairs={{0,8},{8,16},{16,24},{24,32},{32,40},{40,48},{48,56},{56,0},{1,9},... | collective-permute-start | bytes 405512 | tf_op jit(solution)/shard_map/ppermute | solution.py:32
  268.1 8.4 %collective-permute-start.55 = (bf16[1,8,2,1,1,22,384]{6,5,3,2,1,0,4:T(8,128)(2,1)S(1)}, bf16[1,8,2,1,1,22,384]{6,5,3,2,1,0,4:T(8,128)(2,1)S(1)}, u32[]{:S(2)}, u32[]{:S(2)}) collective-permute-start(bf16[1,8,2,1,1,22,384]{6,5,3,2,1,0,4:T(8,128)(2,1)S(1)} %get-tuple-element.127), channel_id=1, source_target_pairs={{0,192},{64,0},{128,64},{192,128},{1,193},{65,1},{129,65},{193,129... | collective-permute-start | bytes 811016 | tf_op jit(solution)/shard_map/ppermute | solution.py:33
  269.9 11.7 %collective-permute-start.52 = (bf16[1,8,2,1,1,22,384]{6,5,3,2,1,0,4:T(8,128)(2,1)S(1)}, bf16[1,8,2,1,1,22,384]{6,5,3,2,1,0,4:T(8,128)(2,1)S(1)}, u32[]{:S(2)}, u32[]{:S(2)}) collective-permute-start(bf16[1,8,2,1,1,22,384]{6,5,3,2,1,0,4:T(8,128)(2,1)S(1)} %get-tuple-element.128), channel_id=1, source_target_pairs={{0,64},{64,128},{128,192},{192,0},{1,65},{65,129},{129,193},{193,1... | collective-permute-start | bytes 811016 | tf_op jit(solution)/shard_map/ppermute | solution.py:32
  270.3 9.0 %collective-permute-start.37 = (bf16[4,1,2,1,1,6,1408]{6,5,3,2,1,0,4:T(8,128)(2,1)S(1)}, bf16[4,1,2,1,1,6,1408]{6,5,3,2,1,0,4:T(8,128)(2,1)S(1)}, u32[]{:S(2)}, u32[]{:S(2)}) collective-permute-start(bf16[4,1,2,1,1,6,1408]{6,5,3,2,1,0,4:T(8,128)(2,1)S(1)} %fusion.218), channel_id=1, source_target_pairs={{0,56},{8,0},{16,8},{24,16},{32,24},{40,32},{48,40},{56,48},{1,57}... | collective-permute-start | bytes 405512 | tf_op jit(solution)/shard_map/ppermute | solution.py:33
  279.4 8.5 %collective-permute-start.38 = (bf16[4,1,2,1,1,6,1408]{6,5,3,2,1,0,4:T(8,128)(2,1)S(1)}, bf16[4,1,2,1,1,6,1408]{6,5,3,2,1,0,4:T(8,128)(2,1)S(1)}, u32[]{:S(2)}, u32[]{:S(2)}) collective-permute-start(bf16[4,1,2,1,1,6,1408]{6,5,3,2,1,0,4:T(8,128)(2,1)S(1)} %get-tuple-element.119), channel_id=1, source_target_pairs={{0,56},{8,0},{16,8},{24,16},{32,24},{40,32},{48,40},{56,48},{1,57}... | collective-permute-start | bytes 405512 | tf_op jit(solution)/shard_map/ppermute | solution.py:33
  296.0 8.2 %collective-permute-start.54 = (bf16[1,8,2,1,1,22,384]{6,5,3,2,1,0,4:T(8,128)(2,1)S(1)}, bf16[1,8,2,1,1,22,384]{6,5,3,2,1,0,4:T(8,128)(2,1)S(1)}, u32[]{:S(2)}, u32[]{:S(2)}) collective-permute-start(bf16[1,8,2,1,1,22,384]{6,5,3,2,1,0,4:T(8,128)(2,1)S(1)} %get-tuple-element.124), channel_id=1, source_target_pairs={{0,64},{64,128},{128,192},{192,0},{1,65},{65,129},{129,193},{193,1... | collective-permute-start | bytes 811016 | tf_op jit(solution)/shard_map/ppermute | solution.py:32
  296.9 9.5 %collective-permute-start.40 = (bf16[4,1,2,1,1,6,1408]{6,5,3,2,1,0,4:T(8,128)(2,1)S(1)}, bf16[4,1,2,1,1,6,1408]{6,5,3,2,1,0,4:T(8,128)(2,1)S(1)}, u32[]{:S(2)}, u32[]{:S(2)}) collective-permute-start(bf16[4,1,2,1,1,6,1408]{6,5,3,2,1,0,4:T(8,128)(2,1)S(1)} %get-tuple-element.115), channel_id=1, source_target_pairs={{0,56},{8,0},{16,8},{24,16},{32,24},{40,32},{48,40},{56,48},{1,57}... | collective-permute-start | bytes 405512 | tf_op jit(solution)/shard_map/ppermute | solution.py:33
  306.6 8.3 %collective-permute-start.33 = (bf16[4,1,2,1,1,6,1408]{6,5,3,2,1,0,4:T(8,128)(2,1)S(1)}, bf16[4,1,2,1,1,6,1408]{6,5,3,2,1,0,4:T(8,128)(2,1)S(1)}, u32[]{:S(2)}, u32[]{:S(2)}) collective-permute-start(bf16[4,1,2,1,1,6,1408]{6,5,3,2,1,0,4:T(8,128)(2,1)S(1)} %get-tuple-element.114), channel_id=1, source_target_pairs={{0,8},{8,16},{16,24},{24,32},{32,40},{40,48},{48,56},{56,0},{1,9},... | collective-permute-start | bytes 405512 | tf_op jit(solution)/shard_map/ppermute | solution.py:32
  308.6 8.5 %collective-permute-start.66 = (bf16[1,1,2,1,1,22,384]{6,5,3,2,1,0,4:T(8,128)(2,1)S(1)}, bf16[1,1,2,1,1,22,384]{6,5,3,2,1,0,4:T(8,128)(2,1)S(1)}, u32[]{:S(2)}, u32[]{:S(2)}) collective-permute-start(bf16[1,1,2,1,1,22,384]{6,5,3,2,1,0,4:T(8,128)(2,1)S(1)} %fusion.289), channel_id=1, source_target_pairs={{0,56},{8,0},{16,8},{24,16},{32,24},{40,32},{48,40},{56,48},{1,57}... | collective-permute-start | bytes 101384 | tf_op jit(solution)/shard_map/ppermute | solution.py:33
  331.7 8.5 %collective-permute-start.58 = (bf16[1,1,2,1,1,22,384]{6,5,3,2,1,0,4:T(8,128)(2,1)S(1)}, bf16[1,1,2,1,1,22,384]{6,5,3,2,1,0,4:T(8,128)(2,1)S(1)}, u32[]{:S(2)}, u32[]{:S(2)}) collective-permute-start(bf16[1,1,2,1,1,22,384]{6,5,3,2,1,0,4:T(8,128)(2,1)S(1)} %get-tuple-element.133), channel_id=1, source_target_pairs={{0,8},{8,16},{16,24},{24,32},{32,40},{40,48},{48,56},{56,0},{1,9},... | collective-permute-start | bytes 101384 | tf_op jit(solution)/shard_map/ppermute | solution.py:32
  336.9 8.7 %collective-permute-start.46 = (bf16[1,1,2,1,1,6,1408]{6,5,3,2,1,0,4:T(8,128)(2,1)S(1)}, bf16[1,1,2,1,1,6,1408]{6,5,3,2,1,0,4:T(8,128)(2,1)S(1)}, u32[]{:S(2)}, u32[]{:S(2)}) collective-permute-start(bf16[1,1,2,1,1,6,1408]{6,5,3,2,1,0,4:T(8,128)(2,1)S(1)} %get-tuple-element.140), channel_id=1, source_target_pairs={{0,192},{64,0},{128,64},{192,128},{1,193},{65,1},{129,65},{193,129... | collective-permute-start | bytes 101384 | tf_op jit(solution)/shard_map/ppermute | solution.py:33
  339.8 11.4 %collective-permute-start.43 = (bf16[1,1,2,1,1,6,1408]{6,5,3,2,1,0,4:T(8,128)(2,1)S(1)}, bf16[1,1,2,1,1,6,1408]{6,5,3,2,1,0,4:T(8,128)(2,1)S(1)}, u32[]{:S(2)}, u32[]{:S(2)}) collective-permute-start(bf16[1,1,2,1,1,6,1408]{6,5,3,2,1,0,4:T(8,128)(2,1)S(1)} %get-tuple-element.141), channel_id=1, source_target_pairs={{0,64},{64,128},{128,192},{192,0},{1,65},{65,129},{129,193},{193,1... | collective-permute-start | bytes 101384 | tf_op jit(solution)/shard_map/ppermute | solution.py:32
  351.3 11.0 %collective-permute-start.48 = (bf16[1,1,2,1,1,6,1408]{6,5,3,2,1,0,4:T(8,128)(2,1)S(1)}, bf16[1,1,2,1,1,6,1408]{6,5,3,2,1,0,4:T(8,128)(2,1)S(1)}, u32[]{:S(2)}, u32[]{:S(2)}) collective-permute-start(bf16[1,1,2,1,1,6,1408]{6,5,3,2,1,0,4:T(8,128)(2,1)S(1)} %get-tuple-element.138), channel_id=1, source_target_pairs={{0,192},{64,0},{128,64},{192,128},{1,193},{65,1},{129,65},{193,129... | collective-permute-start | bytes 101384 | tf_op jit(solution)/shard_map/ppermute | solution.py:33
  375.7 17.5 %collective-permute-start.50 = (f32[6,2816]{1,0:T(8,128)S(1)}, f32[6,2816]{1,0:T(8,128)S(1)}, u32[]{:S(2)}, u32[]{:S(2)}) collective-permute-start(f32[6,2816]{1,0:T(8,128)S(1)} %fusion.231), channel_id=1, source_target_pairs={{0,1},{1,0},{2,3},{3,2},{4,5},{5,4},{6,7},{7,6},{8,9},{9,8},{10,11... | collective-permute-start | bytes 202760 | tf_op jit(solution)/shard_map/ppermute | solution.py:72
  377.9 16.0 %collective-permute-start.73 = (f32[22,768]{1,0:T(8,128)S(1)}, f32[22,768]{1,0:T(8,128)S(1)}, u32[]{:S(2)}, u32[]{:S(2)}) collective-permute-start(f32[22,768]{1,0:T(8,128)S(1)} %fusion.252), channel_id=1, source_target_pairs={{0,1},{1,0},{2,3},{3,2},{4,5},{5,4},{6,7},{7,6},{8,9},{9,8},{10,11... | collective-permute-start | bytes 202760 | tf_op jit(solution)/shard_map/ppermute | solution.py:72
  (129 other events, 1231.6 us)
where the time goes:
time: 402 us; the launch traced here: 395 us
  starting transfers between devices  132 us (33%)
  waiting for transfers between devices  129 us (32%)
  other arithmetic  58 us (14%)
  local copies, waits for them, and re-layouts  41.1 us (10%)
  matrix products  30.7 us (8%)
  between operations  4.27 us (1%)
    ppermute x16, waiting for transfers between devices, ring_gather_rows(): cur = lax.ppermute(cur, axis, [(i, (i + 1) % n) for i in range(n)])  51.2 us
    ppermute x20, starting transfers between devices, ring_scatter(): lax.ppermute(acc_l.astype(wire), axis, [(i, (i - 1) % n) for i in range(n)])  46.2 us
    ppermute x20, waiting for transfers between devices, ring_scatter(): lax.ppermute(acc_r.astype(wire), axis, [(i, (i + 1) % n) for i in range(n)])  36.3 us
    ppermute x8, starting transfers between devices, ring_gather_rows(): cur = lax.ppermute(cur, axis, [(i, (i - 1) % n) for i in range(n)])  35 us
    reshape x2, local copies, waits for them, and re-layouts, reduce_weight_grad(): view = term.reshape(*SIZES[:4], 1, rows, term.shape[1])  19.1 us
    reduce_sum x1, other arithmetic, layer_norm(): centered = convolved - jnp.mean(convolved, axis=-1, keepdims=True)  16.3 us
    ppermute x8, starting transfers between devices, butterfly_sum(): x = x + lax.ppermute(x, axis, [(i, i ^ d) for i in range(n)])  15.1 us
    ppermute x20, waiting for transfers between devices, ring_scatter(): lax.ppermute(acc_l.astype(wire), axis, [(i, (i - 1) % n) for i in range(n)])  14.1 us
  transfers between devices with their start and end apart: 82, of which 35 were waited for; matrix products, arithmetic and copies ran while one was open for 25% of the time, Pallas kernels for 0%

commit v1 on v0

--- a/solution.py
+++ b/solution.py
@@ -18,23 +18,18 @@
     n = SIZE[axis]
     me = lax.axis_index(axis)
     dim = AXES.index(axis)
-
-    def block(j):
-        return lax.dynamic_slice_in_dim(x, j % n, 1, dim)
-
-    if n == 2:
-        got = lax.ppermute(block(me + 1).astype(wire), axis, [(0, 1), (1, 0)])
-        return block(me) + got.astype(jnp.float32)
-    half = x.shape[-1] // 2
-    acc_r = block(me - 1)[..., :half]
-    acc_l = block(me + 1)[..., half:]
-    for s in range(1, n):
-        got_r = lax.ppermute(acc_r.astype(wire), axis, [(i, (i + 1) % n) for i in range(n)])
-        got_l = lax.ppermute(acc_l.astype(wire), axis, [(i, (i - 1) % n) for i in range(n)])
-        j_r, j_l = (me - s - 1, me + s + 1) if s < n - 1 else (me, me)
-        acc_r = got_r.astype(jnp.float32) + block(j_r)[..., :half]
-        acc_l = got_l.astype(jnp.float32) + block(j_l)[..., half:]
-    return jnp.concatenate([acc_r, acc_l], axis=-1)
+    d = 1
+    while d < n:
+        shape = list(x.shape)
+        shape[dim : dim + 1] = [shape[dim] // 2, 2]
+        pairs = x.reshape(shape)
+        bit = (me // d) % 2
+        keep = lax.dynamic_index_in_dim(pairs, bit, dim + 1, keepdims=False)
+        send = lax.dynamic_index_in_dim(pairs, 1 - bit, dim + 1, keepdims=False)
+        got = lax.ppermute(send.astype(wire), axis, [(i, i ^ d) for i in range(n)])
+        x = keep + got.astype(jnp.float32)
+        d *= 2
+    return x
 
 
 def ring_gather_rows(x, axis):

time: 402 us -> 395 us (0.983)
  starting transfers between devices: 132 us -> 70.4 us
  waiting for transfers between devices: 129 us -> 158 us
  local copies, waits for them, and re-layouts: 41.1 us -> 59.4 us
  other arithmetic: 58 us -> 66.9 us
    ppermute x44 -> x14, starting transfers between devices: 56.9 us -> 14.8 us  [ring_scatter(): got = lax.ppermute(send.astype(wire), axis, [(i, i ^ d) for i in range(n)])]
    ppermute x16, waiting for transfers between devices: 51.2 us -> 81.6 us  [ring_gather_rows(): cur = lax.ppermute(cur, axis, [(i, (i + 1) % n) for i in range(n)])]
    another operation x2, local copies, waits for them, and re-layouts: 1.22 us -> 19.1 us  [ring_scatter(): pairs = x.reshape(shape)]
    ppermute x8, starting transfers between devices: 35 us -> 19.3 us  [ring_gather_rows(): cur = lax.ppermute(cur, axis, [(i, (i - 1) % n) for i in range(n)])]
    ppermute x8, waiting for transfers between devices: 13.6 us -> 0.02 us  [ring_gather_rows(): cur = lax.ppermute(cur, axis, [(i, (i - 1) % n) for i in range(n)])]
    reshape x2 -> x1, local copies, waits for them, and re-layouts: 19.1 us -> 6.03 us  [ring_scatter(): pairs = x.reshape(shape)]
    convert_element_type x0 -> x15, local copies, waits for them, and re-layouts: none -> 11.5 us  [ring_scatter(): got = lax.ppermute(send.astype(wire), axis, [(i, i ^ d) for i in range(n)])]
    add x8 -> x14, other arithmetic: 8.55 us -> 18.4 us  [ring_scatter(): x = keep + got.astype(jnp.float32)]
  transfers between devices with their start and end apart: 82 -> 52, of which waited for: 35 -> 27; matrix products, arithmetic and copies ran while one was open for 25% -> 32% of each run, Pallas kernels for 0% -> 0%
where the time goes in v1:
time: 395 us; the launch traced here: 388 us
  waiting for transfers between devices  158 us (40%)
  starting transfers between devices  70.4 us (18%)
  other arithmetic  66.9 us (17%)
  local copies, waits for them, and re-layouts  59.4 us (15%)
  matrix products  28.9 us (7%)
  between operations  4.62 us (1%)
    ppermute x16, waiting for transfers between devices, ring_gather_rows(): cur = lax.ppermute(cur, axis, [(i, (i + 1) % n) for i in range(n)])  81.6 us
    ppermute x14, waiting for transfers between devices, ring_scatter(): got = lax.ppermute(send.astype(wire), axis, [(i, i ^ d) for i in range(n)])  54.5 us
    ppermute x8, starting transfers between devices, ring_gather_rows(): cur = lax.ppermute(cur, axis, [(i, (i - 1) % n) for i in range(n)])  19.3 us
    another operation x2, local copies, waits for them, and re-layouts, ring_scatter(): pairs = x.reshape(shape)  19.1 us
    add x14, other arithmetic, ring_scatter(): x = keep + got.astype(jnp.float32)  18.4 us
    ppermute x8, waiting for transfers between devices, butterfly_sum(): x = x + lax.ppermute(x, axis, [(i, i ^ d) for i in range(n)])  16.8 us
    reduce_sum x1, other arithmetic, layer_norm(): centered = convolved - jnp.mean(convolved, axis=-1, keepdims=True)  16.2 us
    ppermute x14, starting transfers between devices, ring_scatter(): got = lax.ppermute(send.astype(wire), axis, [(i, i ^ d) for i in range(n)])  14.8 us
  transfers between devices with their start and end apart: 52, of which 27 were waited for; matrix products, arithmetic and copies ran while one was open for 32% of the time, Pallas kernels for 0%

profile of v1, /device:TPU:2, one launch (start us, length us, event | category | flops | bytes accessed | tf_op | source)
XLA Modules:
  0.0 388.2 jit_solution(2889242255390277701)
XLA Ops:
  4.5 4.2 %collective-permute-start = (bf16[1,3,32,768]{3,2,1,0:T(8,128)(2,1)S(1)}, bf16[1,3,32,768]{3,2,1,0:T(8,128)(2,1)S(1)}, u32[]{:S(2)}, u32[]{:S(2)}) collective-permute-start(bf16[1,3,32,768]{3,2,1,0:T(8,128)(2,1)S(1)} %get-tuple-element.112), channel_id=1, source_target_pairs={{0,1},{2,3},{4,5},{6,7},{8,9},{10,11},{12,13},{14,15},{16,17},{18,... | collective-permute-start | bytes 442376 | tf_op jit(solution)/shard_map/ppermute | solution.py:84
  18.4 3.1 collective-permute-start.18
  22.2 3.3 collective-permute-start.6
  27.6 16.2 %fusion.219 = (f32[16,32]{1,0:T(8,128)S(1)}, f32[1,16,32,768]{3,2,1,0:T(8,128)S(1)}) fusion(bf16[1,22,38,768]{3,2,1,0:T(8,128)(2,1)S(1)} %fusion.205, f32[768]{0:T(1024)S(1)} %copy-done.98, f32[768]{0:T(1024)S(1)} %copy-done.99, f32[768]{0:T(1024)S(1)} %copy-done.49, bf16[1,3,32,768]{3,2,1,0:T(8,128)(2,1)S(1)} %collective-permute-done.1, ...), kind=kLoop, calls=%fused_computation.515 | loop fusion | flops 60554752 | bytes 35837440 | tf_op jit(solution)/shard_map/reduce_sum | solution.py:130
  46.3 4.1 %collective-permute-done.17 = bf16[88,768]{1,0:T(8,128)(2,1)S(1)} collective-permute-done((bf16[88,768]{1,0:T(8,128)(2,1)}, bf16[88,768]{1,0:T(8,128)(2,1)S(1)}, u32[]{:S(2)}, u32[]{:S(2)}) %collective-permute-start.17) | collective-permute-done | bytes 135200 | tf_op jit(solution)/shard_map/ppermute | solution.py:45
  60.2 10.2 %collective-permute-done.19 = bf16[352,768]{1,0:T(8,128)(2,1)S(1)} collective-permute-done((bf16[352,768]{1,0:T(8,128)(2,1)S(1)}, bf16[352,768]{1,0:T(8,128)(2,1)S(1)}, u32[]{:S(2)}, u32[]{:S(2)}) %collective-permute-start.19) | collective-permute-done | bytes 540704 | tf_op jit(solution)/shard_map/ppermute | solution.py:45
  70.6 11.3 %collective-permute-done.7 = bf16[96,2816]{1,0:T(8,128)(2,1)S(1)} collective-permute-done((bf16[96,2816]{1,0:T(8,128)(2,1)S(1)}, bf16[96,2816]{1,0:T(8,128)(2,1)S(1)}, u32[]{:S(2)}, u32[]{:S(2)}) %collective-permute-start.7) | collective-permute-done | bytes 540704 | tf_op jit(solution)/shard_map/ppermute | solution.py:45
  82.3 3.5 collective-permute-start.12
  87.0 6.6 %collective-permute-done.20 = bf16[352,768]{1,0:T(8,128)(2,1)S(1)} collective-permute-done((bf16[352,768]{1,0:T(8,128)(2,1)S(1)}, bf16[352,768]{1,0:T(8,128)(2,1)S(1)}, u32[]{:S(2)}, u32[]{:S(2)}) %collective-permute-start.20) | collective-permute-done | bytes 540704 | tf_op jit(solution)/shard_map/ppermute | solution.py:45
  93.6 11.5 %collective-permute-done.8 = bf16[96,2816]{1,0:T(8,128)(2,1)S(1)} collective-permute-done((bf16[96,2816]{1,0:T(8,128)(2,1)S(1)}, bf16[96,2816]{1,0:T(8,128)(2,1)S(1)}, u32[]{:S(2)}, u32[]{:S(2)}) %collective-permute-start.8) | collective-permute-done | bytes 540704 | tf_op jit(solution)/shard_map/ppermute | solution.py:45
  105.2 3.3 collective-permute-start.13
  109.4 7.4 %collective-permute-done.21 = bf16[352,768]{1,0:T(8,128)(2,1)S(1)} collective-permute-done((bf16[352,768]{1,0:T(8,128)(2,1)S(1)}, bf16[352,768]{1,0:T(8,128)(2,1)S(1)}, u32[]{:S(2)}, u32[]{:S(2)}) %collective-permute-start.21) | collective-permute-done | bytes 540704 | tf_op jit(solution)/shard_map/ppermute | solution.py:45
  116.8 11.5 %collective-permute-done.9 = bf16[96,2816]{1,0:T(8,128)(2,1)S(1)} collective-permute-done((bf16[96,2816]{1,0:T(8,128)(2,1)S(1)}, bf16[96,2816]{1,0:T(8,128)(2,1)S(1)}, u32[]{:S(2)}, u32[]{:S(2)}) %collective-permute-start.9) | collective-permute-done | bytes 540704 | tf_op jit(solution)/shard_map/ppermute | solution.py:45
  128.6 11.3 %collective-permute-done.22 = bf16[352,768]{1,0:T(8,128)(2,1)S(1)} collective-permute-done((bf16[352,768]{1,0:T(8,128)(2,1)S(1)}, bf16[352,768]{1,0:T(8,128)(2,1)S(1)}, u32[]{:S(2)}, u32[]{:S(2)}) %collective-permute-start.22) | collective-permute-done | bytes 540704 | tf_op jit(solution)/shard_map/ppermute | solution.py:45
  140.5 7.1 %collective-permute-done.10 = bf16[96,2816]{1,0:T(8,128)(2,1)S(1)} collective-permute-done((bf16[96,2816]{1,0:T(8,128)(2,1)S(1)}, bf16[96,2816]{1,0:T(8,128)(2,1)S(1)}, u32[]{:S(2)}, u32[]{:S(2)}) %collective-permute-start.10) | collective-permute-done | bytes 540704 | tf_op jit(solution)/shard_map/ppermute | solution.py:45
  148.1 4.3 %multiply_convert_fusion = (bf16[512,2816]{1,0:T(8,128)(2,1)}, f32[512,2816]{1,0:T(8,128)S(1)}) fusion(bf16[512,768]{1,0:T(8,128)(2,1)S(1)} %bitcast.120, bf16[768,2816]{1,0:T(8,128)(2,1)S(1)} %bitcast.114), kind=kOutput, calls=%fused_computation.52 | convolution fusion | flops 2221801472 | bytes 13762560 | tf_op jit(solution)/shard_map/dot_general | solution.py:171
  152.4 3.7 fusion.5
  156.1 3.6 fusion.223
  161.8 4.7 %fusion.104 = (f32[768]{0:T(1024)S(1)}, f32[768]{0:T(1024)S(1)}, f32[768]{0:T(1024)S(1)}, f32[768]{0:T(1024)S(1)}, f32[768]{0:T(1024)S(1)}, /*index=5*/f32[768]{...) fusion(bf16[1,22,38,768]{3,2,1,0:T(8,128)(2,1)S(1)} %fusion.205, ...), kind=kLoop, calls=%fused_computation.260 | loop fusion | flops 23972352 | bytes 18938368 | tf_op jit(solution)/shard_map/reduce_sum | solution.py:124
  167.8 4.0 %fusion.83 = (f32[768]{0:T(1024)S(1)}, f32[768]{0:T(1024)S(1)}, f32[768]{0:T(1024)S(1)}, f32[768]{0:T(1024)S(1)}, f32[768]{0:T(1024)S(1)}, /*index=5*/f32[768]{0...) fusion(f32[1,16,32,768]{3,2,1,0:T(8,128)S(1)} %get-tuple-elemen, ...), kind=kLoop, calls=%fused_computation.239 | loop fusion | flops 21613056 | bytes 16570368 | tf_op jit(solution)/shard_map/reduce_sum | solution.py:124
  171.9 5.8 %convolution_multiply_fusion.1 = f32[768,2816]{1,0:T(8,128)} fusion(bf16[512,768]{1,0:T(8,128)(2,1)S(1)} %bitcast.121, bf16[512,2816]{1,0:T(8,128)(2,1)S(1)} %copy-done.12), kind=kOutput, calls=%fused_computation.44 | convolution fusion | flops 2216755200 | bytes 12320768 | tf_op jit(solution)/shard_map/dot_general | solution.py:183
  180.5 5.8 %collective-permute-start.26 = (bf16[1,3,32,768]{3,2,1,0:T(8,128)(2,1)S(1)}, bf16[1,3,32,768]{3,2,1,0:T(8,128)(2,1)S(1)}, u32[]{:S(2)}, u32[]{:S(2)}) collective-permute-start(bf16[1,3,32,768]{3,2,1,0:T(8,128)(2,1)S(1)} %get-tuple-element.110), channel_id=1, source_target_pairs={{0,1},{2,3},{4,5},{6,7},{8,9},{10,11},{12,13},{14,15},{16,17},{18,... | collective-permute-start | bytes 442376 | tf_op jit(solution)/shard_map/ppermute | solution.py:84
  187.6 9.8 %reshape_reshape.6 = f32[4,8,2,1,2,1,6,2816]{7,6,4,2,1,0,5,3:T(8,128)} reshape(f32[768,2816]{1,0:T(8,128)} %convolution_multiply_fusion.1) | data formatting | bytes 17301504 | tf_op jit(solution)/shard_map/reshape;reshape | solution.py:25
  197.4 3.0 fusion.6
  202.4 3.2 collective-permute-start.45
  205.6 5.8 %convolution_multiply_fusion = f32[2816,768]{1,0:T(8,128)} fusion(bf16[512,2816]{1,0:T(8,128)(2,1)S(1)} %copy-done.9, bf16[512,768]{1,0:T(8,128)(2,1)S(1)} %bitcast.119), kind=kOutput, calls=%fused_computation.43 | convolution fusion | flops 2216755200 | bytes 12320768 | tf_op jit(solution)/shard_map/dot_general | solution.py:174
  211.5 9.4 %reshape_reshape.7 = f32[4,8,2,1,2,1,22,768]{7,6,4,2,1,0,5,3:T(8,128)} reshape(f32[2816,768]{1,0:T(8,128)} %convolution_multiply_fusion) | data formatting | bytes 17301504 | tf_op jit(solution)/shard_map/reshape;reshape | solution.py:25
  221.0 2.8 fusion.8
  227.7 5.7 %fusion.105 = bf16[1,16,32,768]{3,2,1,0:T(8,128)(2,1)} fusion(bf16[1,16,32,768]{3,2,1,0:T(8,128)(2,1)S(1)} %copy-done.1, bf16[16,32,2816]{2,1,0:T(8,128)(2,1)S(1)} %bitcast.122, bf16[2816,768,1]{1,0,2:T(8,128)(2,1)} %bitcast.113), kind=kOutput, calls=%fused_computation.261 | convolution fusion | flops 2215772160 | bytes 8781824 | tf_op jit(solution)/shard_map/dot_general | solution.py:178
  233.3 4.5 %collective-permute-done.47 = f32[7,7,768]{2,1,0:T(8,128)S(1)} collective-permute-done((f32[7,7,768]{2,1,0:T(8,128)S(1)}, f32[7,7,768]{2,1,0:T(8,128)S(1)}, u32[]{:S(2)}, u32[]{:S(2)}) %collective-permute-start.47) | collective-permute-done | bytes 150560 | tf_op jit(solution)/shard_map/ppermute | solution.py:74
  237.9 4.4 %collective-permute-start.48 = (f32[7,7,768]{2,1,0:T(8,128)S(1)}, f32[7,7,768]{2,1,0:T(8,128)S(1)}, u32[]{:S(2)}, u32[]{:S(2)}) collective-permute-start(f32[7,7,768]{2,1,0:T(8,128)S(1)} %add.879), channel_id=1, source_target_pairs={{0,32},{8,40},{16,48},{24,56},{32,0},{40,8},{48,16},{56,24},{1,33}... | collective-permute-start | bytes 451592 | tf_op jit(solution)/shard_map/ppermute | solution.py:74
  242.8 8.2 %collective-permute-done.48 = f32[7,7,768]{2,1,0:T(8,128)S(1)} collective-permute-done((f32[7,7,768]{2,1,0:T(8,128)S(1)}, f32[7,7,768]{2,1,0:T(8,128)S(1)}, u32[]{:S(2)}, u32[]{:S(2)}) %collective-permute-start.48) | collective-permute-done | bytes 150560 | tf_op jit(solution)/shard_map/ppermute | solution.py:74
  258.2 4.2 %collective-permute-start.51 = (f32[7,7,768]{2,1,0:T(8,128)S(1)}, f32[7,7,768]{2,1,0:T(8,128)S(1)}, u32[]{:S(2)}, u32[]{:S(2)}) collective-permute-start(f32[7,7,768]{2,1,0:T(8,128)S(1)} %add.882), channel_id=1, source_target_pairs={{0,1},{1,0},{2,3},{3,2},{4,5},{5,4},{6,7},{7,6},{8,9},{9,8},{10,11... | collective-permute-start | bytes 451592 | tf_op jit(solution)/shard_map/ppermute | solution.py:74
  262.5 6.2 %bitcast_add_fusion.1 = f32[4,8,2,1,1,6,2816]{6,1,5,4,3,2,0:T(8,128)} fusion(f32[4,8,2,1,1,1,6,2816]{7,6,4,2,1,0,5,3:T(8,128)S(1)} %constant_dynamic-slice_fusion.4, bf16[4,8,2,1,1,6,2816]{6,1,5,4,3,2,0:T(8,128)(2,1)} %collective-permute-done.28), kind=kLoop, calls=%fused_computation.56 | loop fusion | flops 2162688 | bytes 10813440 | tf_op jit(solution)/shard_map/add | solution.py:30
  268.7 6.0 %reshape.520 = f32[4,4,2,2,1,1,6,2816]{7,2,1,6,3,0,5,4:T(2,128)} reshape(f32[4,8,2,1,1,6,2816]{6,1,5,4,3,2,0:T(8,128)} %bitcast_add_fusion.1) | data formatting | bytes 8650752 | tf_op jit(solution)/shard_map/reshape | solution.py:25
  274.7 4.2 %constant_dynamic-slice_fusion.2 = bf16[4,4,1,2,1,1,6,2816]{7,2,1,6,3,0,5,4:T(2,128)(2,1)S(1)} fusion(f32[4,4,2,2,1,1,6,2816]{7,2,1,6,3,0,5,4:T(2,128)} %reshape.520, s32[]{:T(128)S(6)} %select_n.381), kind=kLoop, calls=%fused_computation.429 | loop fusion | bytes 2162692 | tf_op jit(solution)/shard_map/jit(dynamic_index_in_dim)/dynamic_slice | solution.py:28
  281.2 13.1 %fusion.196 = bf16[1,16,32,768]{3,2,1,0:T(8,128)(2,1)} fusion(f32[1,22,32,768]{3,2,1,0:T(8,128)S(1)} %maximum_convert_fusion, f32[768]{0:T(1024)} %get-tuple-element.104, f32[768]{0:T(1024)} %get-tuple-element.105, f32[768]{0:T(1024)S(1)} %copy-done.50, f32[768]{0:T(1024)S(1)} %copy-done.52, f32[768]{0:T(1024)S(1)} %copy-done.54, f32[768]{0:T(1024)S(1)} %copy-done.56, ...), kind=kLoop, calls=%fused_computation.352 | loop fusion | flops 40108032 | bytes 14941184 | tf_op jit(solution)/shard_map/convert_element_type | solution.py:204
  295.0 6.0 %bitcast_add_fusion = f32[4,8,2,1,1,22,768]{6,1,5,4,3,2,0:T(8,128)S(1)} fusion(f32[4,8,2,1,1,1,22,768]{7,6,4,2,1,0,5,3:T(8,128)} %constant_dynamic-slice_fusion.1, bf16[4,8,2,1,1,22,768]{6,1,5,4,3,2,0:T(8,128)(2,1)} %collective-permute-done.36), kind=kLoop, calls=%fused_computation.55 | loop fusion | flops 2162688 | bytes 10813440 | tf_op jit(solution)/shard_map/add | solution.py:30
  308.8 18.9 %collective-permute-done.37 = bf16[2,8,2,1,1,22,768]{6,2,5,1,4,3,0:T(2,128)(2,1)S(1)} collective-permute-done((bf16[2,8,2,1,1,22,768]{6,2,5,1,4,3,0:T(2,128)(2,1)S(1)}, bf16[2,8,2,1,1,22,768]{6,2,5,1,4,3,0:T(2,128)(2,1)S(1)}, u32[]{:S(2)}, u32[]{:S(2)}) %collective-permute-start.37) | collective-permute-done | bytes 1081376 | tf_op jit(solution)/shard_map/ppermute | solution.py:29
  335.0 2.8 collective-permute-start.31
  337.8 7.3 %collective-permute-done.38 = bf16[1,8,2,1,1,22,768]{6,2,5,1,4,3,0:T(2,128)(2,1)S(1)} collective-permute-done((bf16[1,8,2,1,1,22,768]{6,2,5,1,4,3,0:T(2,128)(2,1)S(1)}, bf16[1,8,2,1,1,22,768]{6,2,5,1,4,3,0:T(2,128)(2,1)S(1)}, u32[]{:S(2)}, u32[]{:S(2)}) %collective-permute-start.38) | collective-permute-done | bytes 540704 | tf_op jit(solution)/shard_map/ppermute | solution.py:29
  347.3 5.2 %collective-permute-done.31 = bf16[4,1,2,1,1,6,2816]{6,2,5,1,0,4,3:T(2,128)(2,1)S(1)} collective-permute-done((bf16[4,1,2,1,1,6,2816]{6,2,5,1,0,4,3:T(2,128)(2,1)S(1)}, bf16[4,1,2,1,1,6,2816]{6,2,5,1,0,4,3:T(2,128)(2,1)S(1)}, u32[]{:S(2)}, u32[]{:S(2)}) %collective-permute-start.31) | collective-permute-done | bytes 270368 | tf_op jit(solution)/shard_map/ppermute | solution.py:29
  353.1 3.7 collective-permute-done.39
  360.0 6.5 %collective-permute-done.40 = bf16[1,2,2,1,1,22,768]{6,2,5,1,4,3,0:T(2,128)(2,1)S(1)} collective-permute-done((bf16[1,2,2,1,1,22,768]{6,2,5,1,4,3,0:T(2,128)(2,1)S(1)}, bf16[1,2,2,1,1,22,768]{6,2,5,1,4,3,0:T(2,128)(2,1)S(1)}, u32[]{:S(2)}, u32[]{:S(2)}) %collective-permute-start.40) | collective-permute-done | bytes 135200 | tf_op jit(solution)/shard_map/ppermute | solution.py:29
  366.8 3.0 collective-permute-start.41
  371.5 4.4 %collective-permute-done.41 = bf16[1,1,2,1,1,22,768]{6,2,5,1,4,3,0:T(2,128)(2,1)S(1)} collective-permute-done((bf16[1,1,2,1,1,22,768]{6,2,5,1,4,3,0:T(2,128)(2,1)S(1)}, bf16[1,1,2,1,1,22,768]{6,2,5,1,4,3,0:T(2,128)(2,1)S(1)}, u32[]{:S(2)}, u32[]{:S(2)}) %collective-permute-start.41) | collective-permute-done | bytes 67616 | tf_op jit(solution)/shard_map/ppermute | solution.py:29
  377.8 3.3 collective-permute-done.42
  381.5 2.7 collective-permute-done.35
  (465 shorter events, 82.7 us)
Async XLA Ops:
  0.6 11.9 %collective-permute-start.14 = (bf16[22,768]{1,0:T(8,128)(2,1)}, bf16[22,768]{1,0:T(8,128)(2,1)S(1)}, u32[]{:S(2)}, u32[]{:S(2)}) collective-permute-start(bf16[22,768]{1,0:T(8,128)(2,1)} %param.10), channel_id=1, source_target_pairs={{0,2},{2,0},{1,3},{3,1},{4,6},{6,4},{5,7},{7,5},{8,10},{10,8},{9,1... | collective-permute-start | bytes 101384 | tf_op jit(solution)/shard_map/ppermute | solution.py:45
  0.7 13.7 %collective-permute-start.2 = (bf16[6,2816]{1,0:T(8,128)(2,1)}, bf16[6,2816]{1,0:T(8,128)(2,1)S(1)}, u32[]{:S(2)}, u32[]{:S(2)}) collective-permute-start(bf16[6,2816]{1,0:T(8,128)(2,1)} %param.9), channel_id=1, source_target_pairs={{0,2},{2,0},{1,3},{3,1},{4,6},{6,4},{5,7},{7,5},{8,10},{10,8},{9,1... | collective-permute-start | bytes 101384 | tf_op jit(solution)/shard_map/ppermute | solution.py:45
  4.5 21.5 %collective-permute-start = (bf16[1,3,32,768]{3,2,1,0:T(8,128)(2,1)S(1)}, bf16[1,3,32,768]{3,2,1,0:T(8,128)(2,1)S(1)}, u32[]{:S(2)}, u32[]{:S(2)}) collective-permute-start(bf16[1,3,32,768]{3,2,1,0:T(8,128)(2,1)S(1)} %get-tuple-element.112), channel_id=1, source_target_pairs={{0,1},{2,3},{4,5},{6,7},{8,9},{10,11},{12,13},{14,15},{16,17},{18,... | collective-permute-start | bytes 442376 | tf_op jit(solution)/shard_map/ppermute | solution.py:84
  8.7 17.9 %collective-permute-start.1 = (bf16[1,3,32,768]{3,2,1,0:T(8,128)(2,1)S(1)}, bf16[1,3,32,768]{3,2,1,0:T(8,128)(2,1)S(1)}, u32[]{:S(2)}, u32[]{:S(2)}) collective-permute-start(bf16[1,3,32,768]{3,2,1,0:T(8,128)(2,1)S(1)} %get-tuple-element.113), channel_id=1, source_target_pairs={{1,0},{3,2},{5,4},{7,6},{9,8},{11,10},{13,12},{15,14},{17,16},{19,... | collective-permute-start | bytes 442376 | tf_op jit(solution)/shard_map/ppermute | solution.py:87
  14.8 6.7 %collective-permute-start.3 = (bf16[12,2816]{1,0:T(8,128)(2,1)S(1)}, bf16[12,2816]{1,0:T(8,128)(2,1)S(1)}, u32[]{:S(2)}, u32[]{:S(2)}) collective-permute-start(bf16[12,2816]{1,0:T(8,128)(2,1)S(1)} %dynamic_update_slice.97), channel_id=1, source_target_pairs={{0,4},{4,0},{1,5},{5,1},{2,6},{6,2},{3,7},{7,3},{8,12},{12,8},{9,1... | collective-permute-start | bytes 202760 | tf_op jit(solution)/shard_map/ppermute | solution.py:45
  18.4 31.9 %collective-permute-start.18 = (bf16[88,768]{1,0:T(8,128)(2,1)S(1)}, bf16[88,768]{1,0:T(8,128)(2,1)}, u32[]{:S(2)}, u32[]{:S(2)}) collective-permute-start(bf16[88,768]{1,0:T(8,128)(2,1)S(1)} %dynamic_update_slice.115), channel_id=1, source_target_pairs={{0,192},{64,0},{128,64},{192,128},{1,193},{65,1},{129,65},{193,129... | collective-permute-start | bytes 405512 | tf_op jit(solution)/shard_map/ppermute | solution.py:49
  21.5 22.3 %collective-permute-start.16 = (bf16[88,768]{1,0:T(8,128)(2,1)S(1)}, bf16[88,768]{1,0:T(8,128)(2,1)}, u32[]{:S(2)}, u32[]{:S(2)}) collective-permute-start(bf16[88,768]{1,0:T(8,128)(2,1)S(1)} %dynamic_update_slice.115), channel_id=1, source_target_pairs={{0,64},{64,128},{128,192},{192,0},{1,65},{65,129},{129,193},{193,1... | collective-permute-start | bytes 405512 | tf_op jit(solution)/shard_map/ppermute | solution.py:45
  22.2 31.1 %collective-permute-start.6 = (bf16[24,2816]{1,0:T(8,128)(2,1)S(1)}, bf16[24,2816]{1,0:T(8,128)(2,1)S(1)}, u32[]{:S(2)}, u32[]{:S(2)}) collective-permute-start(bf16[24,2816]{1,0:T(8,128)(2,1)S(1)} %dynamic_update_slice.99), channel_id=1, source_target_pairs={{0,192},{64,0},{128,64},{192,128},{1,193},{65,1},{129,65},{193,129... | collective-permute-start | bytes 405512 | tf_op jit(solution)/shard_map/ppermute | solution.py:49
  26.0 17.9 %collective-permute-start.4 = (bf16[24,2816]{1,0:T(8,128)(2,1)S(1)}, bf16[24,2816]{1,0:T(8,128)(2,1)S(1)}, u32[]{:S(2)}, u32[]{:S(2)}) collective-permute-start(bf16[24,2816]{1,0:T(8,128)(2,1)S(1)} %dynamic_update_slice.99), channel_id=1, source_target_pairs={{0,64},{64,128},{128,192},{192,0},{1,65},{65,129},{129,193},{193,1... | collective-permute-start | bytes 405512 | tf_op jit(solution)/shard_map/ppermute | solution.py:45
  43.8 6.5 %collective-permute-start.17 = (bf16[88,768]{1,0:T(8,128)(2,1)}, bf16[88,768]{1,0:T(8,128)(2,1)S(1)}, u32[]{:S(2)}, u32[]{:S(2)}) collective-permute-start(bf16[88,768]{1,0:T(8,128)(2,1)} %collective-permute-done.16), channel_id=1, source_target_pairs={{0,64},{64,128},{128,192},{192,0},{1,65},{65,129},{129,193},{193,1... | collective-permute-start | bytes 405512 | tf_op jit(solution)/shard_map/ppermute | solution.py:45
  43.9 9.4 %collective-permute-start.5 = (bf16[24,2816]{1,0:T(8,128)(2,1)S(1)}, bf16[24,2816]{1,0:T(8,128)(2,1)S(1)}, u32[]{:S(2)}, u32[]{:S(2)}) collective-permute-start(bf16[24,2816]{1,0:T(8,128)(2,1)S(1)} %collective-permute-done.4), channel_id=1, source_target_pairs={{0,64},{64,128},{128,192},{192,0},{1,65},{65,129},{129,193},{193,1... | collective-permute-start | bytes 405512 | tf_op jit(solution)/shard_map/ppermute | solution.py:45
  51.3 19.1 %collective-permute-start.19 = (bf16[352,768]{1,0:T(8,128)(2,1)S(1)}, bf16[352,768]{1,0:T(8,128)(2,1)S(1)}, u32[]{:S(2)}, u32[]{:S(2)}) collective-permute-start(bf16[352,768]{1,0:T(8,128)(2,1)S(1)} %constant_dynamic-update-slice_fusion.8), channel_id=1, source_target_pairs={{0,8},{8,16},{16,24},{24,32},{32,40},{40,48},{48,56},{56,0},{1,9},... | collective-permute-start | bytes 1622024 | tf_op jit(solution)/shard_map/ppermute | solution.py:45
  53.3 28.7 %collective-permute-start.7 = (bf16[96,2816]{1,0:T(8,128)(2,1)S(1)}, bf16[96,2816]{1,0:T(8,128)(2,1)S(1)}, u32[]{:S(2)}, u32[]{:S(2)}) collective-permute-start(bf16[96,2816]{1,0:T(8,128)(2,1)S(1)} %constant_dynamic-update-slice_fusion.20), channel_id=1, source_target_pairs={{0,8},{8,16},{16,24},{24,32},{32,40},{40,48},{48,56},{56,0},{1,9},... | collective-permute-start | bytes 1622024 | tf_op jit(solution)/shard_map/ppermute | solution.py:45
  55.6 26.7 %collective-permute-start.11 = (bf16[96,2816]{1,0:T(8,128)(2,1)S(1)}, bf16[96,2816]{1,0:T(8,128)(2,1)S(1)}, u32[]{:S(2)}, u32[]{:S(2)}) collective-permute-start(bf16[96,2816]{1,0:T(8,128)(2,1)S(1)} %constant_dynamic-update-slice_fusion.20), channel_id=1, source_target_pairs={{0,56},{8,0},{16,8},{24,16},{32,24},{40,32},{48,40},{56,48},{1,57}... | collective-permute-start | bytes 1622024 | tf_op jit(solution)/shard_map/ppermute | solution.py:49
  58.2 27.7 %collective-permute-start.23 = (bf16[352,768]{1,0:T(8,128)(2,1)S(1)}, bf16[352,768]{1,0:T(8,128)(2,1)S(1)}, u32[]{:S(2)}, u32[]{:S(2)}) collective-permute-start(bf16[352,768]{1,0:T(8,128)(2,1)S(1)} %constant_dynamic-update-slice_fusion.8), channel_id=1, source_target_pairs={{0,56},{8,0},{16,8},{24,16},{32,24},{40,32},{48,40},{56,48},{1,57}... | collective-permute-start | bytes 1622024 | tf_op jit(solution)/shard_map/ppermute | solution.py:49
  70.4 23.2 %collective-permute-start.20 = (bf16[352,768]{1,0:T(8,128)(2,1)S(1)}, bf16[352,768]{1,0:T(8,128)(2,1)S(1)}, u32[]{:S(2)}, u32[]{:S(2)}) collective-permute-start(bf16[352,768]{1,0:T(8,128)(2,1)S(1)} %collective-permute-done.19), channel_id=1, source_target_pairs={{0,8},{8,16},{16,24},{24,32},{32,40},{40,48},{48,56},{56,0},{1,9},... | collective-permute-start | bytes 1622024 | tf_op jit(solution)/shard_map/ppermute | solution.py:45
  82.0 23.2 %collective-permute-start.8 = (bf16[96,2816]{1,0:T(8,128)(2,1)S(1)}, bf16[96,2816]{1,0:T(8,128)(2,1)S(1)}, u32[]{:S(2)}, u32[]{:S(2)}) collective-permute-start(bf16[96,2816]{1,0:T(8,128)(2,1)S(1)} %collective-permute-done.7), channel_id=1, source_target_pairs={{0,8},{8,16},{16,24},{24,32},{32,40},{40,48},{48,56},{56,0},{1,9},... | collective-permute-start | bytes 1622024 | tf_op jit(solution)/shard_map/ppermute | solution.py:45
  82.3 22.9 %collective-permute-start.12 = (bf16[96,2816]{1,0:T(8,128)(2,1)S(1)}, bf16[96,2816]{1,0:T(8,128)(2,1)S(1)}, u32[]{:S(2)}, u32[]{:S(2)}) collective-permute-start(bf16[96,2816]{1,0:T(8,128)(2,1)S(1)} %collective-permute-done.11), channel_id=1, source_target_pairs={{0,56},{8,0},{16,8},{24,16},{32,24},{40,32},{48,40},{56,48},{1,57}... | collective-permute-start | bytes 1622024 | tf_op jit(solution)/shard_map/ppermute | solution.py:49
  85.8 22.7 %collective-permute-start.24 = (bf16[352,768]{1,0:T(8,128)(2,1)S(1)}, bf16[352,768]{1,0:T(8,128)(2,1)S(1)}, u32[]{:S(2)}, u32[]{:S(2)}) collective-permute-start(bf16[352,768]{1,0:T(8,128)(2,1)S(1)} %collective-permute-done.23), channel_id=1, source_target_pairs={{0,56},{8,0},{16,8},{24,16},{32,24},{40,32},{48,40},{56,48},{1,57}... | collective-permute-start | bytes 1622024 | tf_op jit(solution)/shard_map/ppermute | solution.py:49
  93.6 23.2 %collective-permute-start.21 = (bf16[352,768]{1,0:T(8,128)(2,1)S(1)}, bf16[352,768]{1,0:T(8,128)(2,1)S(1)}, u32[]{:S(2)}, u32[]{:S(2)}) collective-permute-start(bf16[352,768]{1,0:T(8,128)(2,1)S(1)} %collective-permute-done.20), channel_id=1, source_target_pairs={{0,8},{8,16},{16,24},{24,32},{32,40},{40,48},{48,56},{56,0},{1,9},... | collective-permute-start | bytes 1622024 | tf_op jit(solution)/shard_map/ppermute | solution.py:45
  105.2 23.2 %collective-permute-start.9 = (bf16[96,2816]{1,0:T(8,128)(2,1)S(1)}, bf16[96,2816]{1,0:T(8,128)(2,1)S(1)}, u32[]{:S(2)}, u32[]{:S(2)}) collective-permute-start(bf16[96,2816]{1,0:T(8,128)(2,1)S(1)} %collective-permute-done.8), channel_id=1, source_target_pairs={{0,8},{8,16},{16,24},{24,32},{32,40},{40,48},{48,56},{56,0},{1,9},... | collective-permute-start | bytes 1622024 | tf_op jit(solution)/shard_map/ppermute | solution.py:45
  105.2 42.5 %collective-permute-start.13 = (bf16[96,2816]{1,0:T(8,128)(2,1)S(1)}, bf16[96,2816]{1,0:T(8,128)(2,1)S(1)}, u32[]{:S(2)}, u32[]{:S(2)}) collective-permute-start(bf16[96,2816]{1,0:T(8,128)(2,1)S(1)} %collective-permute-done.12), channel_id=1, source_target_pairs={{0,56},{8,0},{16,8},{24,16},{32,24},{40,32},{48,40},{56,48},{1,57}... | collective-permute-start | bytes 1622024 | tf_op jit(solution)/shard_map/ppermute | solution.py:49
  108.5 31.5 %collective-permute-start.25 = (bf16[352,768]{1,0:T(8,128)(2,1)S(1)}, bf16[352,768]{1,0:T(8,128)(2,1)S(1)}, u32[]{:S(2)}, u32[]{:S(2)}) collective-permute-start(bf16[352,768]{1,0:T(8,128)(2,1)S(1)} %collective-permute-done.24), channel_id=1, source_target_pairs={{0,56},{8,0},{16,8},{24,16},{32,24},{40,32},{48,40},{56,48},{1,57}... | collective-permute-start | bytes 1622024 | tf_op jit(solution)/shard_map/ppermute | solution.py:49
  116.8 23.2 %collective-permute-start.22 = (bf16[352,768]{1,0:T(8,128)(2,1)S(1)}, bf16[352,768]{1,0:T(8,128)(2,1)S(1)}, u32[]{:S(2)}, u32[]{:S(2)}) collective-permute-start(bf16[352,768]{1,0:T(8,128)(2,1)S(1)} %collective-permute-done.21), channel_id=1, source_target_pairs={{0,8},{8,16},{16,24},{24,32},{32,40},{40,48},{48,56},{56,0},{1,9},... | collective-permute-start | bytes 1622024 | tf_op jit(solution)/shard_map/ppermute | solution.py:45
  128.3 19.2 %collective-permute-start.10 = (bf16[96,2816]{1,0:T(8,128)(2,1)S(1)}, bf16[96,2816]{1,0:T(8,128)(2,1)S(1)}, u32[]{:S(2)}, u32[]{:S(2)}) collective-permute-start(bf16[96,2816]{1,0:T(8,128)(2,1)S(1)} %collective-permute-done.9), channel_id=1, source_target_pairs={{0,8},{8,16},{16,24},{24,32},{32,40},{40,48},{48,56},{56,0},{1,9},... | collective-permute-start | bytes 1622024 | tf_op jit(solution)/shard_map/ppermute | solution.py:45
  180.0 22.4 %collective-permute-start.44 = (f32[7,7,768]{2,1,0:T(8,128)S(1)}, f32[7,7,768]{2,1,0:T(8,128)S(1)}, u32[]{:S(2)}, u32[]{:S(2)}) collective-permute-start(f32[7,7,768]{2,1,0:T(8,128)S(1)} %broadcast_multiply_fusion), channel_id=1, source_target_pairs={{0,64},{64,0},{128,192},{192,128},{1,65},{65,1},{129,193},{193,129... | collective-permute-start | bytes 451592 | tf_op jit(solution)/shard_map/ppermute | solution.py:74
  180.5 76.3 %collective-permute-start.26 = (bf16[1,3,32,768]{3,2,1,0:T(8,128)(2,1)S(1)}, bf16[1,3,32,768]{3,2,1,0:T(8,128)(2,1)S(1)}, u32[]{:S(2)}, u32[]{:S(2)}) collective-permute-start(bf16[1,3,32,768]{3,2,1,0:T(8,128)(2,1)S(1)} %get-tuple-element.110), channel_id=1, source_target_pairs={{0,1},{2,3},{4,5},{6,7},{8,9},{10,11},{12,13},{14,15},{16,17},{18,... | collective-permute-start | bytes 442376 | tf_op jit(solution)/shard_map/ppermute | solution.py:84
  186.3 70.5 %collective-permute-start.27 = (bf16[1,3,32,768]{3,2,1,0:T(8,128)(2,1)S(1)}, bf16[1,3,32,768]{3,2,1,0:T(8,128)(2,1)S(1)}, u32[]{:S(2)}, u32[]{:S(2)}) collective-permute-start(bf16[1,3,32,768]{3,2,1,0:T(8,128)(2,1)S(1)} %get-tuple-element.111), channel_id=1, source_target_pairs={{1,0},{3,2},{5,4},{7,6},{9,8},{11,10},{13,12},{15,14},{17,16},{19,... | collective-permute-start | bytes 442376 | tf_op jit(solution)/shard_map/ppermute | solution.py:87
  202.3 60.1 %collective-permute-start.28 = (bf16[4,8,2,1,1,6,2816]{6,1,5,4,3,2,0:T(8,128)(2,1)}, bf16[4,8,2,1,1,6,2816]{6,1,5,4,3,2,0:T(8,128)(2,1)}, u32[]{:S(2)}, u32[]{:S(2)}) collective-permute-start(bf16[4,8,2,1,1,6,2816]{6,1,5,4,3,2,0:T(8,128)(2,1)} %copy.28), channel_id=1, source_target_pairs={{0,2},{2,0},{1,3},{3,1},{4,6},{6,4},{5,7},{7,5},{8,10},{10,8},{9,1... | collective-permute-start | bytes 6488072 | tf_op jit(solution)/shard_map/ppermute | solution.py:29
  202.4 18.5 %collective-permute-start.45 = (f32[7,7,768]{2,1,0:T(8,128)S(1)}, f32[7,7,768]{2,1,0:T(8,128)S(1)}, u32[]{:S(2)}, u32[]{:S(2)}) collective-permute-start(f32[7,7,768]{2,1,0:T(8,128)S(1)} %fusion.218), channel_id=1, source_target_pairs={{0,128},{64,192},{128,0},{192,64},{1,129},{65,193},{129,1},{193,65... | collective-permute-start | bytes 451592 | tf_op jit(solution)/shard_map/ppermute | solution.py:74
  220.9 6.6 %collective-permute-start.46 = (f32[7,7,768]{2,1,0:T(8,128)S(1)}, f32[7,7,768]{2,1,0:T(8,128)S(1)}, u32[]{:S(2)}, u32[]{:S(2)}) collective-permute-start(f32[7,7,768]{2,1,0:T(8,128)S(1)} %add.877), channel_id=1, source_target_pairs={{0,8},{8,0},{16,24},{24,16},{32,40},{40,32},{48,56},{56,48},{1,9},... | collective-permute-start | bytes 451592 | tf_op jit(solution)/shard_map/ppermute | solution.py:74
  225.8 69.2 %collective-permute-start.36 = (bf16[4,8,2,1,1,22,768]{6,1,5,4,3,2,0:T(8,128)(2,1)}, bf16[4,8,2,1,1,22,768]{6,1,5,4,3,2,0:T(8,128)(2,1)}, u32[]{:S(2)}, u32[]{:S(2)}) collective-permute-start(bf16[4,8,2,1,1,22,768]{6,1,5,4,3,2,0:T(8,128)(2,1)} %copy.32), channel_id=1, source_target_pairs={{0,2},{2,0},{1,3},{3,1},{4,6},{6,4},{5,7},{7,5},{8,10},{10,8},{9,1... | collective-permute-start | bytes 6488072 | tf_op jit(solution)/shard_map/ppermute | solution.py:29
  227.5 10.4 %collective-permute-start.47 = (f32[7,7,768]{2,1,0:T(8,128)S(1)}, f32[7,7,768]{2,1,0:T(8,128)S(1)}, u32[]{:S(2)}, u32[]{:S(2)}) collective-permute-start(f32[7,7,768]{2,1,0:T(8,128)S(1)} %add.878), channel_id=1, source_target_pairs={{0,16},{8,24},{16,0},{24,8},{32,48},{40,56},{48,32},{56,40},{1,17}... | collective-permute-start | bytes 451592 | tf_op jit(solution)/shard_map/ppermute | solution.py:74
  237.9 13.1 %collective-permute-start.48 = (f32[7,7,768]{2,1,0:T(8,128)S(1)}, f32[7,7,768]{2,1,0:T(8,128)S(1)}, u32[]{:S(2)}, u32[]{:S(2)}) collective-permute-start(f32[7,7,768]{2,1,0:T(8,128)S(1)} %add.879), channel_id=1, source_target_pairs={{0,32},{8,40},{16,48},{24,56},{32,0},{40,8},{48,16},{56,24},{1,33}... | collective-permute-start | bytes 451592 | tf_op jit(solution)/shard_map/ppermute | solution.py:74
  251.0 5.5 %collective-permute-start.49 = (f32[7,7,768]{2,1,0:T(8,128)S(1)}, f32[7,7,768]{2,1,0:T(8,128)S(1)}, u32[]{:S(2)}, u32[]{:S(2)}) collective-permute-start(f32[7,7,768]{2,1,0:T(8,128)S(1)} %add.880), channel_id=1, source_target_pairs={{0,4},{4,0},{1,5},{5,1},{2,6},{6,2},{3,7},{7,3},{8,12},{12,8},{9,1... | collective-permute-start | bytes 451592 | tf_op jit(solution)/shard_map/ppermute | solution.py:74
  258.2 36.0 %collective-permute-start.51 = (f32[7,7,768]{2,1,0:T(8,128)S(1)}, f32[7,7,768]{2,1,0:T(8,128)S(1)}, u32[]{:S(2)}, u32[]{:S(2)}) collective-permute-start(f32[7,7,768]{2,1,0:T(8,128)S(1)} %add.882), channel_id=1, source_target_pairs={{0,1},{1,0},{2,3},{3,2},{4,5},{5,4},{6,7},{7,6},{8,9},{9,8},{10,11... | collective-permute-start | bytes 451592 | tf_op jit(solution)/shard_map/ppermute | solution.py:74
  280.4 25.9 %collective-permute-start.29 = (bf16[4,4,2,1,1,6,2816]{6,2,5,1,0,4,3:T(2,128)(2,1)S(1)}, bf16[4,4,2,1,1,6,2816]{6,2,5,1,0,4,3:T(2,128)(2,1)S(1)}, u32[]{:S(2)}, u32[]{:S(2)}) collective-permute-start(bf16[4,4,2,1,1,6,2816]{6,2,5,1,0,4,3:T(2,128)(2,1)S(1)} %bitcast.127), channel_id=1, source_target_pairs={{0,8},{8,0},{16,24},{24,16},{32,40},{40,32},{48,56},{56,48},{1,9},... | collective-permute-start | bytes 3244040 | tf_op jit(solution)/shard_map/ppermute | solution.py:29
  301.9 25.7 %collective-permute-start.37 = (bf16[2,8,2,1,1,22,768]{6,2,5,1,4,3,0:T(2,128)(2,1)S(1)}, bf16[2,8,2,1,1,22,768]{6,2,5,1,4,3,0:T(2,128)(2,1)S(1)}, u32[]{:S(2)}, u32[]{:S(2)}) collective-permute-start(bf16[2,8,2,1,1,22,768]{6,2,5,1,4,3,0:T(2,128)(2,1)S(1)} %bitcast.128), channel_id=1, source_target_pairs={{0,64},{64,0},{128,192},{192,128},{1,65},{65,1},{129,193},{193,129... | collective-permute-start | bytes 3244040 | tf_op jit(solution)/shard_map/ppermute | solution.py:29
  308.2 26.0 %collective-permute-start.30 = (bf16[4,2,2,1,1,6,2816]{6,2,5,1,0,4,3:T(2,128)(2,1)S(1)}, bf16[4,2,2,1,1,6,2816]{6,2,5,1,0,4,3:T(2,128)(2,1)S(1)}, u32[]{:S(2)}, u32[]{:S(2)}) collective-permute-start(bf16[4,2,2,1,1,6,2816]{6,2,5,1,0,4,3:T(2,128)(2,1)S(1)} %fusion.212), channel_id=1, source_target_pairs={{0,16},{8,24},{16,0},{24,8},{32,48},{40,56},{48,32},{56,40},{1,17}... | collective-permute-start | bytes 1622024 | tf_op jit(solution)/shard_map/ppermute | solution.py:29
  330.3 14.8 %collective-permute-start.38 = (bf16[1,8,2,1,1,22,768]{6,2,5,1,4,3,0:T(2,128)(2,1)S(1)}, bf16[1,8,2,1,1,22,768]{6,2,5,1,4,3,0:T(2,128)(2,1)S(1)}, u32[]{:S(2)}, u32[]{:S(2)}) collective-permute-start(bf16[1,8,2,1,1,22,768]{6,2,5,1,4,3,0:T(2,128)(2,1)S(1)} %dynamic-slice_convert_fusion.3), channel_id=1, source_target_pairs={{0,128},{64,192},{128,0},{192,64},{1,129},{65,193},{129,1},{193,65... | collective-permute-start | bytes 1622024 | tf_op jit(solution)/shard_map/ppermute | solution.py:29
  335.0 17.5 %collective-permute-start.31 = (bf16[4,1,2,1,1,6,2816]{6,2,5,1,0,4,3:T(2,128)(2,1)S(1)}, bf16[4,1,2,1,1,6,2816]{6,2,5,1,0,4,3:T(2,128)(2,1)S(1)}, u32[]{:S(2)}, u32[]{:S(2)}) collective-permute-start(bf16[4,1,2,1,1,6,2816]{6,2,5,1,0,4,3:T(2,128)(2,1)S(1)} %dynamic-slice_convert_fusion.6), channel_id=1, source_target_pairs={{0,32},{8,40},{16,48},{24,56},{32,0},{40,8},{48,16},{56,24},{1,33}... | collective-permute-start | bytes 811016 | tf_op jit(solution)/shard_map/ppermute | solution.py:29
  345.9 10.9 %collective-permute-start.39 = (bf16[1,4,2,1,1,22,768]{6,2,5,1,4,3,0:T(2,128)(2,1)S(1)}, bf16[1,4,2,1,1,22,768]{6,2,5,1,4,3,0:T(2,128)(2,1)S(1)}, u32[]{:S(2)}, u32[]{:S(2)}) collective-permute-start(bf16[1,4,2,1,1,22,768]{6,2,5,1,4,3,0:T(2,128)(2,1)S(1)} %fusion.213), channel_id=1, source_target_pairs={{0,8},{8,0},{16,24},{24,16},{32,40},{40,32},{48,56},{56,48},{1,9},... | collective-permute-start | bytes 811016 | tf_op jit(solution)/shard_map/ppermute | solution.py:29
  357.2 9.4 %collective-permute-start.40 = (bf16[1,2,2,1,1,22,768]{6,2,5,1,4,3,0:T(2,128)(2,1)S(1)}, bf16[1,2,2,1,1,22,768]{6,2,5,1,4,3,0:T(2,128)(2,1)S(1)}, u32[]{:S(2)}, u32[]{:S(2)}) collective-permute-start(bf16[1,2,2,1,1,22,768]{6,2,5,1,4,3,0:T(2,128)(2,1)S(1)} %fusion.215), channel_id=1, source_target_pairs={{0,16},{8,24},{16,0},{24,8},{32,48},{40,56},{48,32},{56,40},{1,17}... | collective-permute-start | bytes 405512 | tf_op jit(solution)/shard_map/ppermute | solution.py:29
  358.7 11.2 %collective-permute-start.33 = (bf16[1,1,2,1,1,6,2816]{6,2,5,0,4,3,1:T(2,128)(2,1)S(1)}, bf16[1,1,2,1,1,6,2816]{6,2,5,0,4,3,1:T(2,128)(2,1)S(1)}, u32[]{:S(2)}, u32[]{:S(2)}) collective-permute-start(bf16[1,1,2,1,1,6,2816]{6,2,5,0,4,3,1:T(2,128)(2,1)S(1)} %dynamic-slice_convert_fusion.10), channel_id=1, source_target_pairs={{0,128},{64,192},{128,0},{192,64},{1,129},{65,193},{129,1},{193,65... | collective-permute-start | bytes 202760 | tf_op jit(solution)/shard_map/ppermute | solution.py:29
  366.8 9.1 %collective-permute-start.41 = (bf16[1,1,2,1,1,22,768]{6,2,5,1,4,3,0:T(2,128)(2,1)S(1)}, bf16[1,1,2,1,1,22,768]{6,2,5,1,4,3,0:T(2,128)(2,1)S(1)}, u32[]{:S(2)}, u32[]{:S(2)}) collective-permute-start(bf16[1,1,2,1,1,22,768]{6,2,5,1,4,3,0:T(2,128)(2,1)S(1)} %dynamic-slice_convert_fusion.9), channel_id=1, source_target_pairs={{0,32},{8,40},{16,48},{24,56},{32,0},{40,8},{48,16},{56,24},{1,33}... | collective-permute-start | bytes 202760 | tf_op jit(solution)/shard_map/ppermute | solution.py:29
  370.0 7.6 %collective-permute-start.34 = (bf16[1,1,1,1,1,6,2816]{6,2,5,0,4,3,1:T(2,128)(2,1)S(1)}, bf16[1,1,1,1,1,6,2816]{6,2,5,0,4,3,1:T(2,128)(2,1)S(1)}, u32[]{:S(2)}, u32[]{:S(2)}) collective-permute-start(bf16[1,1,1,1,1,6,2816]{6,2,5,0,4,3,1:T(2,128)(2,1)S(1)} %dynamic-slice_convert_fusion.12), channel_id=1, source_target_pairs={{0,4},{4,0},{1,5},{5,1},{2,6},{6,2},{3,7},{7,3},{8,12},{12,8},{9,1... | collective-permute-start | bytes 101384 | tf_op jit(solution)/shard_map/ppermute | solution.py:29
  377.7 6.5 %collective-permute-start.35 = (f32[6,2816]{1,0:T(8,128)S(1)}, f32[6,2816]{1,0:T(8,128)S(1)}, u32[]{:S(2)}, u32[]{:S(2)}) collective-permute-start(f32[6,2816]{1,0:T(8,128)S(1)} %bitcast.129), channel_id=1, source_target_pairs={{0,1},{1,0},{2,3},{3,2},{4,5},{5,4},{6,7},{7,6},{8,9},{9,8},{10,11... | collective-permute-start | bytes 202760 | tf_op jit(solution)/shard_map/ppermute | solution.py:67
  381.1 5.9 %collective-permute-start.43 = (f32[22,768]{1,0:T(8,128)S(1)}, f32[22,768]{1,0:T(8,128)S(1)}, u32[]{:S(2)}, u32[]{:S(2)}) collective-permute-start(f32[22,768]{1,0:T(8,128)S(1)} %bitcast.130), channel_id=1, source_target_pairs={{0,1},{1,0},{2,3},{3,2},{4,5},{5,4},{6,7},{7,6},{8,9},{9,8},{10,11... | collective-permute-start | bytes 202760 | tf_op jit(solution)/shard_map/ppermute | solution.py:67
  (113 other events, 618.9 us)

commit v2 on v1

--- a/solution.py
+++ b/solution.py
@@ -59,11 +59,11 @@
 
 
 def reduce_weight_grad(term, order):
-    rows = term.shape[0] // 128
-    view = term.reshape(*SIZES[:4], 1, rows, term.shape[1])
+    rows = term.shape[1]
+    view = term.reshape(*SIZES[:4], 1, rows, term.shape[2])
     for axis in order:
         view = ring_scatter(view, axis, jnp.bfloat16)
-    tiles = view.reshape(rows, term.shape[1])
+    tiles = view.reshape(rows, term.shape[2])
     return tiles + lax.ppermute(tiles, "rows", [(0, 1), (1, 0)])
 
 
@@ -171,8 +171,9 @@
     pre_act = jnp.dot(tokens, up_full, preferred_element_type=jnp.float32)
     hidden, derivative = gelu_parts(pre_act)
     activation = hidden.astype(jnp.bfloat16)
+    blocks = 128
     down_term = lax.dot_general(
-        activation, cot_rows, (((0,), (0,)), ((), ())), preferred_element_type=jnp.float32
+        activation.reshape(activation.shape[0], blocks, -1), cot_rows, (((0,), (0,)), ((), ())), preferred_element_type=jnp.float32
     )
     down_grad = reduce_weight_grad(down_term * grad_scale, ("c", "y", "z", "xl"))
     branch = jnp.dot(activation, down_full, preferred_element_type=jnp.float32)
@@ -181,7 +182,7 @@
     )
     grad_pre = (grad_act * derivative).astype(jnp.bfloat16)
     up_term = lax.dot_general(
-        tokens, grad_pre, (((0,), (0,)), ((), ())), preferred_element_type=jnp.float32
+        tokens.reshape(tokens.shape[0], blocks, -1), grad_pre, (((0,), (0,)), ((), ())), preferred_element_type=jnp.float32
     )
     up_grad = reduce_weight_grad(up_term * grad_scale, ("c", "z", "y", "xl"))
     grad_rows = lax.dot_general(

time: 395 us -> 444 us (1.12)
  local copies, waits for them, and re-layouts: 59.4 us -> 140 us
  waiting for transfers between devices: 158 us -> 120 us
  starting transfers between devices: 70.4 us -> 75.6 us
    dynamic_slice x1 -> x3, local copies, waits for them, and re-layouts: 4.17 us -> 24.4 us  [ring_scatter(): send = lax.dynamic_index_in_dim(pairs, 1 - bit, dim + 1, keepdims=False)]
    dynamic_slice x4, local copies, waits for them, and re-layouts: 5.43 us -> 24 us  [ring_scatter(): keep = lax.dynamic_index_in_dim(pairs, bit, dim + 1, keepdims=False)]
    ppermute x16, waiting for transfers between devices: 81.6 us -> 64.6 us  [ring_gather_rows(): cur = lax.ppermute(cur, axis, [(i, (i + 1) % n) for i in range(n)])]
    ppermute x8, waiting for transfers between devices: 16.8 us -> 5.37 us  [butterfly_sum(): x = x + lax.ppermute(x, axis, [(i, i ^ d) for i in range(n)])]
    unnamed x228 -> x190, local copies, waits for them, and re-layouts: 2.47 us -> 12.4 us
    convert_element_type x0 -> x2, local copies, waits for them, and re-layouts: none -> 9.47 us  [the longest x1 4.85 us: on_device(): normed = unit_norm.astype(jnp.bfloat16)]
    ppermute x14, waiting for transfers between devices: 54.5 us -> 45.8 us  [ring_scatter(): got = lax.ppermute(send.astype(wire), axis, [(i, i ^ d) for i in range(n)])]
    convert_element_type x15 -> x11, local copies, waits for them, and re-layouts: 11.5 us -> 3.63 us  [ring_scatter(): got = lax.ppermute(send.astype(wire), axis, [(i, i ^ d) for i in range(n)])]
  transfers between devices with their start and end apart: 52 -> 52, of which waited for: 27 -> 22; matrix products, arithmetic and copies ran while one was open for 32% -> 48% of each run, Pallas kernels for 0% -> 0%
where the time goes in v2:
time: 444 us; the launch traced here: 436 us
  local copies, waits for them, and re-layouts  140 us (32%)
  waiting for transfers between devices  120 us (27%)
  starting transfers between devices  75.6 us (17%)
  other arithmetic  65.3 us (15%)
  matrix products  31.8 us (7%)
    ppermute x16, waiting for transfers between devices, ring_gather_rows(): cur = lax.ppermute(cur, axis, [(i, (i + 1) % n) for i in range(n)])  64.6 us
    ppermute x14, waiting for transfers between devices, ring_scatter(): got = lax.ppermute(send.astype(wire), axis, [(i, i ^ d) for i in range(n)])  45.8 us
    dynamic_slice x3, local copies, waits for them, and re-layouts, ring_scatter(): send = lax.dynamic_index_in_dim(pairs, 1 - bit, dim + 1, keepdims=False)  24.4 us
    dynamic_slice x4, local copies, waits for them, and re-layouts, ring_scatter(): keep = lax.dynamic_index_in_dim(pairs, bit, dim + 1, keepdims=False)  24 us
    another operation x2, local copies, waits for them, and re-layouts, ring_scatter(): pairs = x.reshape(shape)  21.5 us
    ppermute x8, starting transfers between devices, ring_gather_rows(): cur = lax.ppermute(cur, axis, [(i, (i - 1) % n) for i in range(n)])  19.3 us
    ppermute x14, starting transfers between devices, ring_scatter(): got = lax.ppermute(send.astype(wire), axis, [(i, i ^ d) for i in range(n)])  16.7 us
    add x14, other arithmetic, ring_scatter(): x = keep + got.astype(jnp.float32)  16 us
  transfers between devices with their start and end apart: 52, of which 22 were waited for; matrix products, arithmetic and copies ran while one was open for 48% of the time, Pallas kernels for 0%

profile of v2, /device:TPU:2, one launch (start us, length us, event | category | flops | bytes accessed | tf_op | source)
XLA Modules:
  0.0 435.8 jit_solution(6486925323795400656)
XLA Ops:
  4.5 4.2 collective-permute-start
  34.4 15.7 %fusion.222 = (f32[16,32]{1,0:T(8,128)S(1)}, f32[1,16,32,768]{3,2,1,0:T(8,128)S(1)}) fusion(bf16[1,22,38,768]{3,2,1,0:T(8,128)(2,1)S(1)} %fusion.207, f32[768]{0:T(1024)S(1)} %copy-done.80, f32[768]{0:T(1024)S(1)} %copy-done.82, f32[768]{0:T(1024)S(1)} %get-tuple-element.58, bf16[1,3,32,768]{3,2,1,0:T(8,128)(2,1)} %copy-done.14, ...), kind=kLoop, calls=%fused_computation.520 | loop fusion | flops 60554752 | bytes 35837440 | tf_op jit(solution)/shard_map/reduce_sum | solution.py:130
  53.2 3.8 collective-permute-done.17
  67.7 10.9 %collective-permute-done.19 = bf16[352,768]{1,0:T(8,128)(2,1)} collective-permute-done((bf16[352,768]{1,0:T(8,128)(2,1)}, bf16[352,768]{1,0:T(8,128)(2,1)}, u32[]{:S(2)}, u32[]{:S(2)}) %collective-permute-start.19) | collective-permute-done | bytes 540704 | tf_op jit(solution)/shard_map/ppermute | solution.py:45
  79.7 4.8 %copy.23 = bf16[1,16,32,768]{2,1,3,0:T(8,128)(2,1)} copy(bf16[1,16,32,768]{3,2,1,0:T(8,128)(2,1)} %fusion.208) | data formatting | bytes 1572864 | tf_op jit(solution)/shard_map/convert_element_type | solution.py:167
  84.5 5.1 %reshape_reshape.9 = bf16[512,128,6]{0,2,1:T(8,128)(2,1)} reshape(bf16[1,16,32,768]{2,1,3,0:T(8,128)(2,1)} %copy.23) | data formatting | bytes 1572864 | tf_op jit(solution)/shard_map/reshape;reshape | solution.py:185
  96.9 4.9 %collective-permute-done.20 = bf16[352,768]{1,0:T(8,128)(2,1)} collective-permute-done((bf16[352,768]{1,0:T(8,128)(2,1)}, bf16[352,768]{1,0:T(8,128)(2,1)}, u32[]{:S(2)}, u32[]{:S(2)}) %collective-permute-start.20) | collective-permute-done | bytes 540704 | tf_op jit(solution)/shard_map/ppermute | solution.py:45
  102.9 10.4 %collective-permute-done.8 = bf16[96,2816]{1,0:T(8,128)(2,1)S(1)} collective-permute-done((bf16[96,2816]{1,0:T(8,128)(2,1)}, bf16[96,2816]{1,0:T(8,128)(2,1)S(1)}, u32[]{:S(2)}, u32[]{:S(2)}) %collective-permute-start.8) | collective-permute-done | bytes 540704 | tf_op jit(solution)/shard_map/ppermute | solution.py:45
  118.5 6.3 %collective-permute-done.21 = bf16[352,768]{1,0:T(8,128)(2,1)S(1)} collective-permute-done((bf16[352,768]{1,0:T(8,128)(2,1)}, bf16[352,768]{1,0:T(8,128)(2,1)S(1)}, u32[]{:S(2)}, u32[]{:S(2)}) %collective-permute-start.21) | collective-permute-done | bytes 540704 | tf_op jit(solution)/shard_map/ppermute | solution.py:45
  125.9 10.5 %collective-permute-done.9 = bf16[96,2816]{1,0:T(8,128)(2,1)S(1)} collective-permute-done((bf16[96,2816]{1,0:T(8,128)(2,1)S(1)}, bf16[96,2816]{1,0:T(8,128)(2,1)S(1)}, u32[]{:S(2)}, u32[]{:S(2)}) %collective-permute-start.9) | collective-permute-done | bytes 540704 | tf_op jit(solution)/shard_map/ppermute | solution.py:45
  136.9 11.1 %collective-permute-done.22 = bf16[352,768]{1,0:T(8,128)(2,1)S(1)} collective-permute-done((bf16[352,768]{1,0:T(8,128)(2,1)S(1)}, bf16[352,768]{1,0:T(8,128)(2,1)S(1)}, u32[]{:S(2)}, u32[]{:S(2)}) %collective-permute-start.22) | collective-permute-done | bytes 540704 | tf_op jit(solution)/shard_map/ppermute | solution.py:45
  149.6 6.2 %collective-permute-done.10 = bf16[96,2816]{1,0:T(8,128)(2,1)S(1)} collective-permute-done((bf16[96,2816]{1,0:T(8,128)(2,1)S(1)}, bf16[96,2816]{1,0:T(8,128)(2,1)S(1)}, u32[]{:S(2)}, u32[]{:S(2)}) %collective-permute-start.10) | collective-permute-done | bytes 540704 | tf_op jit(solution)/shard_map/ppermute | solution.py:45
  158.2 4.3 multiply_convert_fusion
  162.5 3.7 fusion.5
  166.2 3.6 fusion.226
  171.8 4.7 %fusion.106 = (f32[768]{0:T(1024)S(1)}, f32[768]{0:T(1024)S(1)}, f32[768]{0:T(1024)S(1)}, f32[768]{0:T(1024)S(1)}, f32[768]{0:T(1024)S(1)}, /*index=5*/f32[768]{...) fusion(bf16[1,22,38,768]{3,2,1,0:T(8,128)(2,1)S(1)} %fusion.207, ...), kind=kLoop, calls=%fused_computation.262 | loop fusion | flops 23972352 | bytes 18938368 | tf_op jit(solution)/shard_map/reduce_sum | solution.py:124
  177.8 4.0 fusion.85
  185.1 5.8 %collective-permute-start.26 = (bf16[1,3,32,768]{3,2,1,0:T(8,128)(2,1)}, bf16[1,3,32,768]{3,2,1,0:T(8,128)(2,1)S(1)}, u32[]{:S(2)}, u32[]{:S(2)}) collective-permute-start(bf16[1,3,32,768]{3,2,1,0:T(8,128)(2,1)} %get-tuple-element.110), channel_id=1, source_target_pairs={{0,1},{2,3},{4,5},{6,7},{8,9},{10,11},{12,13},{14,15},{16,17},{18,... | collective-permute-start | bytes 442376 | tf_op jit(solution)/shard_map/ppermute | solution.py:84
  192.4 4.6 %copy.29 = bf16[512,2816]{0,1:T(8,128)(2,1)} copy(bf16[512,2816]{1,0:T(8,128)(2,1)} %get-tuple-element.116) | data formatting | bytes 5767168 | tf_op jit(solution)/shard_map/convert_element_type | solution.py:173
  197.0 5.5 %reshape.527 = bf16[512,128,22]{0,2,1:T(8,128)(2,1)} reshape(bf16[512,2816]{0,1:T(8,128)(2,1)} %copy.29) | data formatting | bytes 5767168 | tf_op jit(solution)/shard_map/reshape | solution.py:176
  202.5 8.7 %broadcast_multiply_fusion = f32[128,22,768]{2,0,1:T(8,128)} fusion(bf16[512,768,1]{1,0,2:T(8,128)(2,1)S(1)} %bitcast.139, bf16[512,128,22]{0,2,1:T(8,128)(2,1)} %reshape.527), kind=kOutput, calls=%fused_computation.56 | convolution fusion | flops 2216755200 | bytes 12320768 | tf_op jit(solution)/shard_map/dot_general | solution.py:175
  211.1 10.7 %reshape_reshape.11 = f32[4,8,2,1,2,1,22,768]{7,4,2,1,0,6,5,3:T(2,128)} reshape(f32[128,22,768]{2,0,1:T(8,128)} %broadcast_multiply_fusion) | data formatting | bytes 17301504 | tf_op jit(solution)/shard_map/reshape;reshape | solution.py:25
  221.8 10.1 %constant_dynamic-slice_fusion.1 = bf16[4,8,2,1,1,1,22,768]{7,4,2,1,0,6,5,3:T(2,128)(2,1)} fusion(f32[4,8,2,1,2,1,22,768]{7,4,2,1,0,6,5,3:T(2,128)} %reshape_reshape.11, s32[]{:T(128)S(6)} %select_n.378), kind=kLoop, calls=%fused_computation.431 | loop fusion | bytes 4325380 | tf_op jit(solution)/shard_map/jit(dynamic_index_in_dim)/dynamic_slice | solution.py:28
  231.9 4.1 copy.67
  236.1 3.3 collective-permute-start.45
  239.4 6.0 %convolution_multiply_fusion = f32[128,6,2816]{2,0,1:T(8,128)} fusion(bf16[512,2816]{1,0:T(8,128)(2,1)S(1)} %copy-done.11, bf16[512,128,6]{0,2,1:T(8,128)(2,1)S(1)} %copy-done.6), kind=kOutput, calls=%fused_computation.43 | convolution fusion | flops 2216755200 | bytes 12320768 | tf_op jit(solution)/shard_map/dot_general | solution.py:184
  245.4 10.8 %reshape_reshape.10 = f32[4,8,2,1,2,1,6,2816]{7,4,2,1,0,6,5,3:T(2,128)} reshape(f32[128,6,2816]{2,0,1:T(8,128)} %convolution_multiply_fusion) | data formatting | bytes 17301504 | tf_op jit(solution)/shard_map/reshape;reshape | solution.py:25
  256.3 10.0 %constant_dynamic-slice_fusion.5 = bf16[4,8,2,1,1,1,6,2816]{7,4,2,1,0,6,5,3:T(2,128)(2,1)} fusion(f32[4,8,2,1,2,1,6,2816]{7,4,2,1,0,6,5,3:T(2,128)} %reshape_reshape.10, s32[]{:T(128)S(6)} %select_n.378), kind=kLoop, calls=%fused_computation.435 | loop fusion | bytes 4325380 | tf_op jit(solution)/shard_map/jit(dynamic_index_in_dim)/dynamic_slice | solution.py:28
  266.3 4.0 copy.66
  272.2 5.5 %fusion.107 = bf16[1,16,32,768]{3,2,1,0:T(8,128)(2,1)} fusion(bf16[1,16,32,768]{3,2,1,0:T(8,128)(2,1)S(1)} %copy-done.1, bf16[16,32,2816]{2,1,0:T(8,128)(2,1)S(1)} %bitcast.131, bf16[2816,768,1]{1,0,2:T(8,128)(2,1)} %bitcast.125), kind=kOutput, calls=%fused_computation.263 | convolution fusion | flops 2215772160 | bytes 8781824 | tf_op jit(solution)/shard_map/dot_general | solution.py:179
  277.7 4.2 collective-permute-done.47
  281.9 4.8 %collective-permute-start.48 = (f32[7,7,768]{2,1,0:T(8,128)S(1)}, f32[7,7,768]{2,1,0:T(8,128)S(1)}, u32[]{:S(2)}, u32[]{:S(2)}) collective-permute-start(f32[7,7,768]{2,1,0:T(8,128)S(1)} %add.879), channel_id=1, source_target_pairs={{0,32},{8,40},{16,48},{24,56},{32,0},{40,8},{48,16},{56,24},{1,33}... | collective-permute-start | bytes 451592 | tf_op jit(solution)/shard_map/ppermute | solution.py:74
  286.7 10.1 %constant_dynamic-slice_fusion.2 = f32[4,8,2,1,1,1,22,768]{7,4,2,1,0,6,5,3:T(1,128)} fusion(f32[4,8,2,1,2,1,22,768]{7,4,2,1,0,6,5,3:T(2,128)} %reshape_reshape.11, s32[]{:T(128)S(6)} %select_n.377), kind=kLoop, calls=%fused_computation.432 | loop fusion | bytes 8650756 | tf_op jit(solution)/shard_map/jit(dynamic_index_in_dim)/dynamic_slice | solution.py:27
  298.3 10.0 %constant_dynamic-slice_fusion.6 = f32[4,8,2,1,1,1,6,2816]{7,4,2,1,0,6,5,3:T(1,128)} fusion(f32[4,8,2,1,2,1,6,2816]{7,4,2,1,0,6,5,3:T(2,128)} %reshape_reshape.10, s32[]{:T(128)S(6)} %select_n.377), kind=kLoop, calls=%fused_computation.436 | loop fusion | bytes 8650756 | tf_op jit(solution)/shard_map/jit(dynamic_index_in_dim)/dynamic_slice | solution.py:27
  309.8 3.8 collective-permute-start.51
  313.6 3.4 bitcast_add_fusion
  319.1 4.0 bitcast_add_fusion.1
  323.1 6.0 %reshape.523 = f32[4,4,2,2,1,1,6,2816]{7,2,1,6,3,0,5,4:T(2,128)} reshape(f32[4,8,2,1,1,6,2816]{6,1,5,4,3,2,0:T(8,128)} %bitcast_add_fusion.1) | data formatting | bytes 8650752 | tf_op jit(solution)/shard_map/reshape | solution.py:25
  329.1 4.3 constant_dynamic-slice_fusion.3
  338.9 5.9 %collective-permute-done.37 = bf16[2,8,2,1,1,22,768]{6,2,5,1,4,3,0:T(2,128)(2,1)} collective-permute-done((bf16[2,8,2,1,1,22,768]{6,2,5,1,4,3,0:T(2,128)(2,1)S(1)}, bf16[2,8,2,1,1,22,768]{6,2,5,1,4,3,0:T(2,128)(2,1)}, u32[]{:S(2)}, u32[]{:S(2)}) %collective-permute-start.37) | collective-permute-done | bytes 1081376 | tf_op jit(solution)/shard_map/ppermute | solution.py:29
  344.8 3.5 bitcast_add_fusion.2
  351.4 9.1 %collective-permute-done.29 = bf16[4,4,2,1,1,6,2816]{6,2,5,1,0,4,3:T(2,128)(2,1)S(1)} collective-permute-done((bf16[4,4,2,1,1,6,2816]{6,2,5,1,0,4,3:T(2,128)(2,1)S(1)}, bf16[4,4,2,1,1,6,2816]{6,2,5,1,0,4,3:T(2,128)(2,1)S(1)}, u32[]{:S(2)}, u32[]{:S(2)}) %collective-permute-start.29) | collective-permute-done | bytes 1081376 | tf_op jit(solution)/shard_map/ppermute | solution.py:29
  364.2 12.6 %fusion.198 = bf16[1,16,32,768]{3,2,1,0:T(8,128)(2,1)} fusion(f32[1,22,32,768]{3,2,1,0:T(8,128)S(1)} %maximum_convert_fusion, f32[768]{0:T(1024)S(1)} %copy-done.81, f32[768]{0:T(1024)S(1)} %copy-done.83, f32[768]{0:T(1024)S(1)} %copy-done.27, f32[768]{0:T(1024)S(1)} %copy-done.29, f32[768]{0:T(1024)S(1)} %copy-done.31, f32[768]{0:T(1024)S(1)} %copy-done.33, ...), kind=kLoop, calls=%fused_computation.354 | loop fusion | flops 40108032 | bytes 14948352 | tf_op jit(solution)/shard_map/convert_element_type | solution.py:205
  382.2 7.1 %collective-permute-done.30 = bf16[4,2,2,1,1,6,2816]{6,2,5,1,0,4,3:T(2,128)(2,1)S(1)} collective-permute-done((bf16[4,2,2,1,1,6,2816]{6,2,5,1,0,4,3:T(2,128)(2,1)}, bf16[4,2,2,1,1,6,2816]{6,2,5,1,0,4,3:T(2,128)(2,1)S(1)}, u32[]{:S(2)}, u32[]{:S(2)}) %collective-permute-start.30) | collective-permute-done | bytes 540704 | tf_op jit(solution)/shard_map/ppermute | solution.py:29
  391.8 5.0 %collective-permute-done.39 = bf16[1,4,2,1,1,22,768]{6,2,5,1,4,3,0:T(2,128)(2,1)S(1)} collective-permute-done((bf16[1,4,2,1,1,22,768]{6,2,5,1,4,3,0:T(2,128)(2,1)S(1)}, bf16[1,4,2,1,1,22,768]{6,2,5,1,4,3,0:T(2,128)(2,1)S(1)}, u32[]{:S(2)}, u32[]{:S(2)}) %collective-permute-start.39) | collective-permute-done | bytes 270368 | tf_op jit(solution)/shard_map/ppermute | solution.py:29
  397.5 7.9 %collective-permute-done.31 = bf16[4,1,2,1,1,6,2816]{6,2,5,1,0,4,3:T(2,128)(2,1)S(1)} collective-permute-done((bf16[4,1,2,1,1,6,2816]{6,2,5,1,0,4,3:T(2,128)(2,1)S(1)}, bf16[4,1,2,1,1,6,2816]{6,2,5,1,0,4,3:T(2,128)(2,1)S(1)}, u32[]{:S(2)}, u32[]{:S(2)}) %collective-permute-start.31) | collective-permute-done | bytes 270368 | tf_op jit(solution)/shard_map/ppermute | solution.py:29
  407.3 4.6 %collective-permute-done.40 = bf16[1,2,2,1,1,22,768]{6,2,5,1,4,3,0:T(2,128)(2,1)S(1)} collective-permute-done((bf16[1,2,2,1,1,22,768]{6,2,5,1,4,3,0:T(2,128)(2,1)S(1)}, bf16[1,2,2,1,1,22,768]{6,2,5,1,4,3,0:T(2,128)(2,1)S(1)}, u32[]{:S(2)}, u32[]{:S(2)}) %collective-permute-start.40) | collective-permute-done | bytes 135200 | tf_op jit(solution)/shard_map/ppermute | solution.py:29
  412.1 4.0 collective-permute-start.41
  (428 shorter events, 118.5 us)
Async XLA Ops:
  0.6 11.3 %collective-permute-start.14 = (bf16[22,768]{1,0:T(8,128)(2,1)}, bf16[22,768]{1,0:T(8,128)(2,1)S(1)}, u32[]{:S(2)}, u32[]{:S(2)}) collective-permute-start(bf16[22,768]{1,0:T(8,128)(2,1)} %param.10), channel_id=1, source_target_pairs={{0,2},{2,0},{1,3},{3,1},{4,6},{6,4},{5,7},{7,5},{8,10},{10,8},{9,1... | collective-permute-start | bytes 101384 | tf_op jit(solution)/shard_map/ppermute | solution.py:45
  0.7 13.1 %collective-permute-start.2 = (bf16[6,2816]{1,0:T(8,128)(2,1)}, bf16[6,2816]{1,0:T(8,128)(2,1)S(1)}, u32[]{:S(2)}, u32[]{:S(2)}) collective-permute-start(bf16[6,2816]{1,0:T(8,128)(2,1)} %param.9), channel_id=1, source_target_pairs={{0,2},{2,0},{1,3},{3,1},{4,6},{6,4},{5,7},{7,5},{8,10},{10,8},{9,1... | collective-permute-start | bytes 101384 | tf_op jit(solution)/shard_map/ppermute | solution.py:45
  4.5 28.8 %collective-permute-start = (bf16[1,3,32,768]{3,2,1,0:T(8,128)(2,1)S(1)}, bf16[1,3,32,768]{3,2,1,0:T(8,128)(2,1)S(1)}, u32[]{:S(2)}, u32[]{:S(2)}) collective-permute-start(bf16[1,3,32,768]{3,2,1,0:T(8,128)(2,1)S(1)} %get-tuple-element.112), channel_id=1, source_target_pairs={{0,1},{2,3},{4,5},{6,7},{8,9},{10,11},{12,13},{14,15},{16,17},{18,... | collective-permute-start | bytes 442376 | tf_op jit(solution)/shard_map/ppermute | solution.py:84
  8.7 24.8 %collective-permute-start.1 = (bf16[1,3,32,768]{3,2,1,0:T(8,128)(2,1)S(1)}, bf16[1,3,32,768]{3,2,1,0:T(8,128)(2,1)S(1)}, u32[]{:S(2)}, u32[]{:S(2)}) collective-permute-start(bf16[1,3,32,768]{3,2,1,0:T(8,128)(2,1)S(1)} %get-tuple-element.113), channel_id=1, source_target_pairs={{1,0},{3,2},{5,4},{7,6},{9,8},{11,10},{13,12},{15,14},{17,16},{19,... | collective-permute-start | bytes 442376 | tf_op jit(solution)/shard_map/ppermute | solution.py:87
  12.3 7.7 %collective-permute-start.15 = (bf16[44,768]{1,0:T(8,128)(2,1)S(1)}, bf16[44,768]{1,0:T(8,128)(2,1)S(1)}, u32[]{:S(2)}, u32[]{:S(2)}) collective-permute-start(bf16[44,768]{1,0:T(8,128)(2,1)S(1)} %dynamic_update_slice.113), channel_id=1, source_target_pairs={{0,4},{4,0},{1,5},{5,1},{2,6},{6,2},{3,7},{7,3},{8,12},{12,8},{9,1... | collective-permute-start | bytes 202760 | tf_op jit(solution)/shard_map/ppermute | solution.py:45
  14.2 10.5 %collective-permute-start.3 = (bf16[12,2816]{1,0:T(8,128)(2,1)S(1)}, bf16[12,2816]{1,0:T(8,128)(2,1)S(1)}, u32[]{:S(2)}, u32[]{:S(2)}) collective-permute-start(bf16[12,2816]{1,0:T(8,128)(2,1)S(1)} %dynamic_update_slice.97), channel_id=1, source_target_pairs={{0,4},{4,0},{1,5},{5,1},{2,6},{6,2},{3,7},{7,3},{8,12},{12,8},{9,1... | collective-permute-start | bytes 202760 | tf_op jit(solution)/shard_map/ppermute | solution.py:45
  21.7 36.0 %collective-permute-start.18 = (bf16[88,768]{1,0:T(8,128)(2,1)}, bf16[88,768]{1,0:T(8,128)(2,1)}, u32[]{:S(2)}, u32[]{:S(2)}) collective-permute-start(bf16[88,768]{1,0:T(8,128)(2,1)} %dynamic_update_slice.115), channel_id=1, source_target_pairs={{0,192},{64,0},{128,64},{192,128},{1,193},{65,1},{129,65},{193,129... | collective-permute-start | bytes 405512 | tf_op jit(solution)/shard_map/ppermute | solution.py:49
  24.7 25.4 %collective-permute-start.16 = (bf16[88,768]{1,0:T(8,128)(2,1)}, bf16[88,768]{1,0:T(8,128)(2,1)}, u32[]{:S(2)}, u32[]{:S(2)}) collective-permute-start(bf16[88,768]{1,0:T(8,128)(2,1)} %dynamic_update_slice.115), channel_id=1, source_target_pairs={{0,64},{64,128},{128,192},{192,0},{1,65},{65,129},{129,193},{193,1... | collective-permute-start | bytes 405512 | tf_op jit(solution)/shard_map/ppermute | solution.py:45
  26.4 34.8 %collective-permute-start.6 = (bf16[24,2816]{1,0:T(8,128)(2,1)}, bf16[24,2816]{1,0:T(8,128)(2,1)S(1)}, u32[]{:S(2)}, u32[]{:S(2)}) collective-permute-start(bf16[24,2816]{1,0:T(8,128)(2,1)} %dynamic_update_slice.99), channel_id=1, source_target_pairs={{0,192},{64,0},{128,64},{192,128},{1,193},{65,1},{129,65},{193,129... | collective-permute-start | bytes 405512 | tf_op jit(solution)/shard_map/ppermute | solution.py:49
  33.3 17.0 %collective-permute-start.4 = (bf16[24,2816]{1,0:T(8,128)(2,1)}, bf16[24,2816]{1,0:T(8,128)(2,1)S(1)}, u32[]{:S(2)}, u32[]{:S(2)}) collective-permute-start(bf16[24,2816]{1,0:T(8,128)(2,1)} %dynamic_update_slice.99), channel_id=1, source_target_pairs={{0,64},{64,128},{128,192},{192,0},{1,65},{65,129},{129,193},{193,1... | collective-permute-start | bytes 405512 | tf_op jit(solution)/shard_map/ppermute | solution.py:45
  50.1 6.9 %collective-permute-start.17 = (bf16[88,768]{1,0:T(8,128)(2,1)}, bf16[88,768]{1,0:T(8,128)(2,1)S(1)}, u32[]{:S(2)}, u32[]{:S(2)}) collective-permute-start(bf16[88,768]{1,0:T(8,128)(2,1)} %collective-permute-done.16), channel_id=1, source_target_pairs={{0,64},{64,128},{128,192},{192,0},{1,65},{65,129},{129,193},{193,1... | collective-permute-start | bytes 405512 | tf_op jit(solution)/shard_map/ppermute | solution.py:45
  50.2 10.9 %collective-permute-start.5 = (bf16[24,2816]{1,0:T(8,128)(2,1)S(1)}, bf16[24,2816]{1,0:T(8,128)(2,1)S(1)}, u32[]{:S(2)}, u32[]{:S(2)}) collective-permute-start(bf16[24,2816]{1,0:T(8,128)(2,1)S(1)} %collective-permute-done.4), channel_id=1, source_target_pairs={{0,64},{64,128},{128,192},{192,0},{1,65},{65,129},{129,193},{193,1... | collective-permute-start | bytes 405512 | tf_op jit(solution)/shard_map/ppermute | solution.py:45
  59.2 19.4 %collective-permute-start.19 = (bf16[352,768]{1,0:T(8,128)(2,1)}, bf16[352,768]{1,0:T(8,128)(2,1)}, u32[]{:S(2)}, u32[]{:S(2)}) collective-permute-start(bf16[352,768]{1,0:T(8,128)(2,1)} %constant_dynamic-update-slice_fusion.8), channel_id=1, source_target_pairs={{0,8},{8,16},{16,24},{24,32},{32,40},{40,48},{48,56},{56,0},{1,9},... | collective-permute-start | bytes 1622024 | tf_op jit(solution)/shard_map/ppermute | solution.py:45
  61.2 29.0 %collective-permute-start.7 = (bf16[96,2816]{1,0:T(8,128)(2,1)S(1)}, bf16[96,2816]{1,0:T(8,128)(2,1)}, u32[]{:S(2)}, u32[]{:S(2)}) collective-permute-start(bf16[96,2816]{1,0:T(8,128)(2,1)S(1)} %constant_dynamic-update-slice_fusion.20), channel_id=1, source_target_pairs={{0,8},{8,16},{16,24},{24,32},{32,40},{40,48},{48,56},{56,0},{1,9},... | collective-permute-start | bytes 1622024 | tf_op jit(solution)/shard_map/ppermute | solution.py:45
  63.5 27.2 %collective-permute-start.11 = (bf16[96,2816]{1,0:T(8,128)(2,1)S(1)}, bf16[96,2816]{1,0:T(8,128)(2,1)}, u32[]{:S(2)}, u32[]{:S(2)}) collective-permute-start(bf16[96,2816]{1,0:T(8,128)(2,1)S(1)} %constant_dynamic-update-slice_fusion.20), channel_id=1, source_target_pairs={{0,56},{8,0},{16,8},{24,16},{32,24},{40,32},{48,40},{56,48},{1,57}... | collective-permute-start | bytes 1622024 | tf_op jit(solution)/shard_map/ppermute | solution.py:49
  65.6 28.4 %collective-permute-start.23 = (bf16[352,768]{1,0:T(8,128)(2,1)}, bf16[352,768]{1,0:T(8,128)(2,1)}, u32[]{:S(2)}, u32[]{:S(2)}) collective-permute-start(bf16[352,768]{1,0:T(8,128)(2,1)} %constant_dynamic-update-slice_fusion.8), channel_id=1, source_target_pairs={{0,56},{8,0},{16,8},{24,16},{32,24},{40,32},{48,40},{56,48},{1,57}... | collective-permute-start | bytes 1622024 | tf_op jit(solution)/shard_map/ppermute | solution.py:49
  78.6 23.2 %collective-permute-start.20 = (bf16[352,768]{1,0:T(8,128)(2,1)}, bf16[352,768]{1,0:T(8,128)(2,1)}, u32[]{:S(2)}, u32[]{:S(2)}) collective-permute-start(bf16[352,768]{1,0:T(8,128)(2,1)} %collective-permute-done.19), channel_id=1, source_target_pairs={{0,8},{8,16},{16,24},{24,32},{32,40},{40,48},{48,56},{56,0},{1,9},... | collective-permute-start | bytes 1622024 | tf_op jit(solution)/shard_map/ppermute | solution.py:45
  90.2 23.1 %collective-permute-start.8 = (bf16[96,2816]{1,0:T(8,128)(2,1)}, bf16[96,2816]{1,0:T(8,128)(2,1)S(1)}, u32[]{:S(2)}, u32[]{:S(2)}) collective-permute-start(bf16[96,2816]{1,0:T(8,128)(2,1)} %collective-permute-done.7), channel_id=1, source_target_pairs={{0,8},{8,16},{16,24},{24,32},{32,40},{40,48},{48,56},{56,0},{1,9},... | collective-permute-start | bytes 1622024 | tf_op jit(solution)/shard_map/ppermute | solution.py:45
  90.7 23.6 %collective-permute-start.12 = (bf16[96,2816]{1,0:T(8,128)(2,1)}, bf16[96,2816]{1,0:T(8,128)(2,1)S(1)}, u32[]{:S(2)}, u32[]{:S(2)}) collective-permute-start(bf16[96,2816]{1,0:T(8,128)(2,1)} %collective-permute-done.11), channel_id=1, source_target_pairs={{0,56},{8,0},{16,8},{24,16},{32,24},{40,32},{48,40},{56,48},{1,57}... | collective-permute-start | bytes 1622024 | tf_op jit(solution)/shard_map/ppermute | solution.py:49
  94.0 23.6 %collective-permute-start.24 = (bf16[352,768]{1,0:T(8,128)(2,1)}, bf16[352,768]{1,0:T(8,128)(2,1)S(1)}, u32[]{:S(2)}, u32[]{:S(2)}) collective-permute-start(bf16[352,768]{1,0:T(8,128)(2,1)} %collective-permute-done.23), channel_id=1, source_target_pairs={{0,56},{8,0},{16,8},{24,16},{32,24},{40,32},{48,40},{56,48},{1,57}... | collective-permute-start | bytes 1622024 | tf_op jit(solution)/shard_map/ppermute | solution.py:49
  101.8 23.1 %collective-permute-start.21 = (bf16[352,768]{1,0:T(8,128)(2,1)}, bf16[352,768]{1,0:T(8,128)(2,1)S(1)}, u32[]{:S(2)}, u32[]{:S(2)}) collective-permute-start(bf16[352,768]{1,0:T(8,128)(2,1)} %collective-permute-done.20), channel_id=1, source_target_pairs={{0,8},{8,16},{16,24},{24,32},{32,40},{40,48},{48,56},{56,0},{1,9},... | collective-permute-start | bytes 1622024 | tf_op jit(solution)/shard_map/ppermute | solution.py:45
  113.3 23.2 %collective-permute-start.9 = (bf16[96,2816]{1,0:T(8,128)(2,1)S(1)}, bf16[96,2816]{1,0:T(8,128)(2,1)S(1)}, u32[]{:S(2)}, u32[]{:S(2)}) collective-permute-start(bf16[96,2816]{1,0:T(8,128)(2,1)S(1)} %collective-permute-done.8), channel_id=1, source_target_pairs={{0,8},{8,16},{16,24},{24,32},{32,40},{40,48},{48,56},{56,0},{1,9},... | collective-permute-start | bytes 1622024 | tf_op jit(solution)/shard_map/ppermute | solution.py:45
  114.4 42.6 %collective-permute-start.13 = (bf16[96,2816]{1,0:T(8,128)(2,1)S(1)}, bf16[96,2816]{1,0:T(8,128)(2,1)S(1)}, u32[]{:S(2)}, u32[]{:S(2)}) collective-permute-start(bf16[96,2816]{1,0:T(8,128)(2,1)S(1)} %collective-permute-done.12), channel_id=1, source_target_pairs={{0,56},{8,0},{16,8},{24,16},{32,24},{40,32},{48,40},{56,48},{1,57}... | collective-permute-start | bytes 1622024 | tf_op jit(solution)/shard_map/ppermute | solution.py:49
  117.7 31.5 %collective-permute-start.25 = (bf16[352,768]{1,0:T(8,128)(2,1)S(1)}, bf16[352,768]{1,0:T(8,128)(2,1)S(1)}, u32[]{:S(2)}, u32[]{:S(2)}) collective-permute-start(bf16[352,768]{1,0:T(8,128)(2,1)S(1)} %collective-permute-done.24), channel_id=1, source_target_pairs={{0,56},{8,0},{16,8},{24,16},{32,24},{40,32},{48,40},{56,48},{1,57}... | collective-permute-start | bytes 1622024 | tf_op jit(solution)/shard_map/ppermute | solution.py:49
  124.8 23.2 %collective-permute-start.22 = (bf16[352,768]{1,0:T(8,128)(2,1)S(1)}, bf16[352,768]{1,0:T(8,128)(2,1)S(1)}, u32[]{:S(2)}, u32[]{:S(2)}) collective-permute-start(bf16[352,768]{1,0:T(8,128)(2,1)S(1)} %collective-permute-done.21), channel_id=1, source_target_pairs={{0,8},{8,16},{16,24},{24,32},{32,40},{40,48},{48,56},{56,0},{1,9},... | collective-permute-start | bytes 1622024 | tf_op jit(solution)/shard_map/ppermute | solution.py:45
  136.4 19.3 %collective-permute-start.10 = (bf16[96,2816]{1,0:T(8,128)(2,1)S(1)}, bf16[96,2816]{1,0:T(8,128)(2,1)S(1)}, u32[]{:S(2)}, u32[]{:S(2)}) collective-permute-start(bf16[96,2816]{1,0:T(8,128)(2,1)S(1)} %collective-permute-done.9), channel_id=1, source_target_pairs={{0,8},{8,16},{16,24},{24,32},{32,40},{40,48},{48,56},{56,0},{1,9},... | collective-permute-start | bytes 1622024 | tf_op jit(solution)/shard_map/ppermute | solution.py:45
  184.2 51.8 %collective-permute-start.44 = (f32[7,7,768]{2,1,0:T(8,128)S(1)}, f32[7,7,768]{2,1,0:T(8,128)S(1)}, u32[]{:S(2)}, u32[]{:S(2)}) collective-permute-start(f32[7,7,768]{2,1,0:T(8,128)S(1)} %broadcast_multiply_fusion.1), channel_id=1, source_target_pairs={{0,64},{64,0},{128,192},{192,128},{1,65},{65,1},{129,193},{193,129... | collective-permute-start | bytes 451592 | tf_op jit(solution)/shard_map/ppermute | solution.py:74
  185.1 123.3 %collective-permute-start.26 = (bf16[1,3,32,768]{3,2,1,0:T(8,128)(2,1)}, bf16[1,3,32,768]{3,2,1,0:T(8,128)(2,1)S(1)}, u32[]{:S(2)}, u32[]{:S(2)}) collective-permute-start(bf16[1,3,32,768]{3,2,1,0:T(8,128)(2,1)} %get-tuple-element.110), channel_id=1, source_target_pairs={{0,1},{2,3},{4,5},{6,7},{8,9},{10,11},{12,13},{14,15},{16,17},{18,... | collective-permute-start | bytes 442376 | tf_op jit(solution)/shard_map/ppermute | solution.py:84
  190.9 117.5 %collective-permute-start.27 = (bf16[1,3,32,768]{3,2,1,0:T(8,128)(2,1)}, bf16[1,3,32,768]{3,2,1,0:T(8,128)(2,1)S(1)}, u32[]{:S(2)}, u32[]{:S(2)}) collective-permute-start(bf16[1,3,32,768]{3,2,1,0:T(8,128)(2,1)} %get-tuple-element.111), channel_id=1, source_target_pairs={{1,0},{3,2},{5,4},{7,6},{9,8},{11,10},{13,12},{15,14},{17,16},{19,... | collective-permute-start | bytes 442376 | tf_op jit(solution)/shard_map/ppermute | solution.py:87
  236.0 77.6 %collective-permute-start.36 = (bf16[4,8,2,1,1,22,768]{6,1,5,4,3,2,0:T(8,128)(2,1)}, bf16[4,8,2,1,1,22,768]{6,1,5,4,3,2,0:T(8,128)(2,1)}, u32[]{:S(2)}, u32[]{:S(2)}) collective-permute-start(bf16[4,8,2,1,1,22,768]{6,1,5,4,3,2,0:T(8,128)(2,1)} %bitcast.108), channel_id=1, source_target_pairs={{0,2},{2,0},{1,3},{3,1},{4,6},{6,4},{5,7},{7,5},{8,10},{10,8},{9,1... | collective-permute-start | bytes 6488072 | tf_op jit(solution)/shard_map/ppermute | solution.py:29
  236.1 20.2 %collective-permute-start.45 = (f32[7,7,768]{2,1,0:T(8,128)S(1)}, f32[7,7,768]{2,1,0:T(8,128)S(1)}, u32[]{:S(2)}, u32[]{:S(2)}) collective-permute-start(f32[7,7,768]{2,1,0:T(8,128)S(1)} %fusion.221), channel_id=1, source_target_pairs={{0,128},{64,192},{128,0},{192,64},{1,129},{65,193},{129,1},{193,65... | collective-permute-start | bytes 451592 | tf_op jit(solution)/shard_map/ppermute | solution.py:74
  256.2 14.4 %collective-permute-start.46 = (f32[7,7,768]{2,1,0:T(8,128)S(1)}, f32[7,7,768]{2,1,0:T(8,128)S(1)}, u32[]{:S(2)}, u32[]{:S(2)}) collective-permute-start(f32[7,7,768]{2,1,0:T(8,128)S(1)} %add.877), channel_id=1, source_target_pairs={{0,8},{8,0},{16,24},{24,16},{32,40},{40,32},{48,56},{56,48},{1,9},... | collective-permute-start | bytes 451592 | tf_op jit(solution)/shard_map/ppermute | solution.py:74
  270.4 48.7 %collective-permute-start.28 = (bf16[4,8,2,1,1,6,2816]{6,1,5,4,3,2,0:T(8,128)(2,1)}, bf16[4,8,2,1,1,6,2816]{6,1,5,4,3,2,0:T(8,128)(2,1)}, u32[]{:S(2)}, u32[]{:S(2)}) collective-permute-start(bf16[4,8,2,1,1,6,2816]{6,1,5,4,3,2,0:T(8,128)(2,1)} %bitcast.107), channel_id=1, source_target_pairs={{0,2},{2,0},{1,3},{3,1},{4,6},{6,4},{5,7},{7,5},{8,10},{10,8},{9,1... | collective-permute-start | bytes 6488072 | tf_op jit(solution)/shard_map/ppermute | solution.py:29
  270.6 11.2 %collective-permute-start.47 = (f32[7,7,768]{2,1,0:T(8,128)S(1)}, f32[7,7,768]{2,1,0:T(8,128)S(1)}, u32[]{:S(2)}, u32[]{:S(2)}) collective-permute-start(f32[7,7,768]{2,1,0:T(8,128)S(1)} %add.878), channel_id=1, source_target_pairs={{0,16},{8,24},{16,0},{24,8},{32,48},{40,56},{48,32},{56,40},{1,17}... | collective-permute-start | bytes 451592 | tf_op jit(solution)/shard_map/ppermute | solution.py:74
  281.9 14.9 %collective-permute-start.48 = (f32[7,7,768]{2,1,0:T(8,128)S(1)}, f32[7,7,768]{2,1,0:T(8,128)S(1)}, u32[]{:S(2)}, u32[]{:S(2)}) collective-permute-start(f32[7,7,768]{2,1,0:T(8,128)S(1)} %add.879), channel_id=1, source_target_pairs={{0,32},{8,40},{16,48},{24,56},{32,0},{40,8},{48,16},{56,24},{1,33}... | collective-permute-start | bytes 451592 | tf_op jit(solution)/shard_map/ppermute | solution.py:74
  296.8 11.5 %collective-permute-start.49 = (f32[7,7,768]{2,1,0:T(8,128)S(1)}, f32[7,7,768]{2,1,0:T(8,128)S(1)}, u32[]{:S(2)}, u32[]{:S(2)}) collective-permute-start(f32[7,7,768]{2,1,0:T(8,128)S(1)} %add.880), channel_id=1, source_target_pairs={{0,4},{4,0},{1,5},{5,1},{2,6},{6,2},{3,7},{7,3},{8,12},{12,8},{9,1... | collective-permute-start | bytes 451592 | tf_op jit(solution)/shard_map/ppermute | solution.py:74
  309.8 67.0 %collective-permute-start.51 = (f32[7,7,768]{2,1,0:T(8,128)S(1)}, f32[7,7,768]{2,1,0:T(8,128)}, u32[]{:S(2)}, u32[]{:S(2)}) collective-permute-start(f32[7,7,768]{2,1,0:T(8,128)S(1)} %add.882), channel_id=1, source_target_pairs={{0,1},{1,0},{2,3},{3,2},{4,5},{5,4},{6,7},{7,6},{8,9},{9,8},{10,11... | collective-permute-start | bytes 451592 | tf_op jit(solution)/shard_map/ppermute | solution.py:74
  319.0 25.7 %collective-permute-start.37 = (bf16[2,8,2,1,1,22,768]{6,2,5,1,4,3,0:T(2,128)(2,1)S(1)}, bf16[2,8,2,1,1,22,768]{6,2,5,1,4,3,0:T(2,128)(2,1)}, u32[]{:S(2)}, u32[]{:S(2)}) collective-permute-start(bf16[2,8,2,1,1,22,768]{6,2,5,1,4,3,0:T(2,128)(2,1)S(1)} %bitcast.137), channel_id=1, source_target_pairs={{0,64},{64,0},{128,192},{192,128},{1,65},{65,1},{129,193},{193,129... | collective-permute-start | bytes 3244040 | tf_op jit(solution)/shard_map/ppermute | solution.py:29
  334.5 25.9 %collective-permute-start.29 = (bf16[4,4,2,1,1,6,2816]{6,2,5,1,0,4,3:T(2,128)(2,1)S(1)}, bf16[4,4,2,1,1,6,2816]{6,2,5,1,0,4,3:T(2,128)(2,1)S(1)}, u32[]{:S(2)}, u32[]{:S(2)}) collective-permute-start(bf16[4,4,2,1,1,6,2816]{6,2,5,1,0,4,3:T(2,128)(2,1)S(1)} %bitcast.136), channel_id=1, source_target_pairs={{0,8},{8,0},{16,24},{24,16},{32,40},{40,32},{48,56},{56,48},{1,9},... | collective-permute-start | bytes 3244040 | tf_op jit(solution)/shard_map/ppermute | solution.py:29
  350.0 28.4 %collective-permute-start.38 = (bf16[1,8,2,1,1,22,768]{6,2,5,1,4,3,0:T(2,128)(2,1)}, bf16[1,8,2,1,1,22,768]{6,2,5,1,4,3,0:T(2,128)(2,1)S(1)}, u32[]{:S(2)}, u32[]{:S(2)}) collective-permute-start(bf16[1,8,2,1,1,22,768]{6,2,5,1,4,3,0:T(2,128)(2,1)} %dynamic-slice_convert_fusion.1), channel_id=1, source_target_pairs={{0,128},{64,192},{128,0},{192,64},{1,129},{65,193},{129,1},{193,65... | collective-permute-start | bytes 1622024 | tf_op jit(solution)/shard_map/ppermute | solution.py:29
  363.1 26.2 %collective-permute-start.30 = (bf16[4,2,2,1,1,6,2816]{6,2,5,1,0,4,3:T(2,128)(2,1)}, bf16[4,2,2,1,1,6,2816]{6,2,5,1,0,4,3:T(2,128)(2,1)S(1)}, u32[]{:S(2)}, u32[]{:S(2)}) collective-permute-start(bf16[4,2,2,1,1,6,2816]{6,2,5,1,0,4,3:T(2,128)(2,1)} %fusion.215), channel_id=1, source_target_pairs={{0,16},{8,24},{16,0},{24,8},{32,48},{40,56},{48,32},{56,40},{1,17}... | collective-permute-start | bytes 1622024 | tf_op jit(solution)/shard_map/ppermute | solution.py:29
  380.4 16.5 %collective-permute-start.39 = (bf16[1,4,2,1,1,22,768]{6,2,5,1,4,3,0:T(2,128)(2,1)S(1)}, bf16[1,4,2,1,1,22,768]{6,2,5,1,4,3,0:T(2,128)(2,1)S(1)}, u32[]{:S(2)}, u32[]{:S(2)}) collective-permute-start(bf16[1,4,2,1,1,22,768]{6,2,5,1,4,3,0:T(2,128)(2,1)S(1)} %fusion.216), channel_id=1, source_target_pairs={{0,8},{8,0},{16,24},{24,16},{32,40},{40,32},{48,56},{56,48},{1,9},... | collective-permute-start | bytes 811016 | tf_op jit(solution)/shard_map/ppermute | solution.py:29
  390.1 15.3 %collective-permute-start.31 = (bf16[4,1,2,1,1,6,2816]{6,2,5,1,0,4,3:T(2,128)(2,1)S(1)}, bf16[4,1,2,1,1,6,2816]{6,2,5,1,0,4,3:T(2,128)(2,1)S(1)}, u32[]{:S(2)}, u32[]{:S(2)}) collective-permute-start(bf16[4,1,2,1,1,6,2816]{6,2,5,1,0,4,3:T(2,128)(2,1)S(1)} %dynamic-slice_convert_fusion.4), channel_id=1, source_target_pairs={{0,32},{8,40},{16,48},{24,56},{32,0},{40,8},{48,16},{56,24},{1,33}... | collective-permute-start | bytes 811016 | tf_op jit(solution)/shard_map/ppermute | solution.py:29
  397.3 14.6 %collective-permute-start.40 = (bf16[1,2,2,1,1,22,768]{6,2,5,1,4,3,0:T(2,128)(2,1)S(1)}, bf16[1,2,2,1,1,22,768]{6,2,5,1,4,3,0:T(2,128)(2,1)S(1)}, u32[]{:S(2)}, u32[]{:S(2)}) collective-permute-start(bf16[1,2,2,1,1,22,768]{6,2,5,1,4,3,0:T(2,128)(2,1)S(1)} %fusion.218), channel_id=1, source_target_pairs={{0,16},{8,24},{16,0},{24,8},{32,48},{40,56},{48,32},{56,40},{1,17}... | collective-permute-start | bytes 405512 | tf_op jit(solution)/shard_map/ppermute | solution.py:29
  405.8 10.3 %collective-permute-start.32 = (bf16[2,1,2,1,1,6,2816]{6,2,5,0,4,3,1:T(2,128)(2,1)S(1)}, bf16[2,1,2,1,1,6,2816]{6,2,5,0,4,3,1:T(2,128)(2,1)S(1)}, u32[]{:S(2)}, u32[]{:S(2)}) collective-permute-start(bf16[2,1,2,1,1,6,2816]{6,2,5,0,4,3,1:T(2,128)(2,1)S(1)} %fusion.217), channel_id=1, source_target_pairs={{0,64},{64,0},{128,192},{192,128},{1,65},{65,1},{129,193},{193,129... | collective-permute-start | bytes 405512 | tf_op jit(solution)/shard_map/ppermute | solution.py:29
  412.1 9.5 %collective-permute-start.41 = (bf16[1,1,2,1,1,22,768]{6,2,5,1,4,3,0:T(2,128)(2,1)S(1)}, bf16[1,1,2,1,1,22,768]{6,2,5,1,4,3,0:T(2,128)(2,1)S(1)}, u32[]{:S(2)}, u32[]{:S(2)}) collective-permute-start(bf16[1,1,2,1,1,22,768]{6,2,5,1,4,3,0:T(2,128)(2,1)S(1)} %dynamic-slice_convert_fusion.7), channel_id=1, source_target_pairs={{0,32},{8,40},{16,48},{24,56},{32,0},{40,8},{48,16},{56,24},{1,33}... | collective-permute-start | bytes 202760 | tf_op jit(solution)/shard_map/ppermute | solution.py:29
  416.3 7.3 %collective-permute-start.33 = (bf16[1,1,2,1,1,6,2816]{6,2,5,0,4,3,1:T(2,128)(2,1)S(1)}, bf16[1,1,2,1,1,6,2816]{6,2,5,0,4,3,1:T(2,128)(2,1)S(1)}, u32[]{:S(2)}, u32[]{:S(2)}) collective-permute-start(bf16[1,1,2,1,1,6,2816]{6,2,5,0,4,3,1:T(2,128)(2,1)S(1)} %dynamic-slice_convert_fusion.8), channel_id=1, source_target_pairs={{0,128},{64,192},{128,0},{192,64},{1,129},{65,193},{129,1},{193,65... | collective-permute-start | bytes 202760 | tf_op jit(solution)/shard_map/ppermute | solution.py:29
  428.8 6.1 %collective-permute-start.35 = (f32[6,2816]{1,0:T(8,128)S(1)}, f32[6,2816]{1,0:T(8,128)S(1)}, u32[]{:S(2)}, u32[]{:S(2)}) collective-permute-start(f32[6,2816]{1,0:T(8,128)S(1)} %bitcast.140), channel_id=1, source_target_pairs={{0,1},{1,0},{2,3},{3,2},{4,5},{5,4},{6,7},{7,6},{8,9},{9,8},{10,11... | collective-permute-start | bytes 202760 | tf_op jit(solution)/shard_map/ppermute | solution.py:67
  (93 other events, 826.8 us)

commit v3 on v1

--- a/solution.py
+++ b/solution.py
@@ -51,11 +51,17 @@
     return out
 
 
-def gather_weight(shard):
+def gather_weights(up_shard, down_shard):
+    lanes = 128
+    packed = jnp.concatenate([up_shard.reshape(-1, lanes), down_shard.reshape(-1, lanes)])
+    half = up_shard.size // lanes
     for axis in ("c", "xl", "y", "z"):
-        shard = ring_gather_rows(shard, axis)
-    shard = shard.reshape(SIZE["z"], SIZE["y"], -1, shard.shape[1]).transpose(1, 0, 2, 3)
-    return shard.reshape(-1, shard.shape[3])
+        packed = ring_gather_rows(packed, axis)
+    packed = packed.reshape(SIZE["z"], SIZE["y"], -1, packed.shape[0] // 128, lanes)
+    packed = packed.transpose(1, 0, 2, 3, 4).reshape(128, -1, lanes)
+    up_full = packed[:, :half].reshape(-1, up_shard.shape[1])
+    down_full = packed[:, half:].reshape(-1, down_shard.shape[1])
+    return up_full, down_full
 
 
 def reduce_weight_grad(term, order):
@@ -156,8 +162,7 @@
     inside_cells = inside[..., None]
     masked = jnp.where(inside_cells, features, jnp.zeros((), features.dtype))
     masked_cot = jnp.where(inside_cells, cotangent, jnp.zeros((), cotangent.dtype))
-    up_full = gather_weight(up_weight)
-    down_full = gather_weight(down_weight)
+    up_full, down_full = gather_weights(up_weight, down_weight)
     rimmed = padded_2(masked, (("rows", 1),), reach)
     padded = jnp.pad(rimmed, ((0, 0), (0, 0), (reach, reach), (0, 0)))
     convolved = jnp.where(

time: 395 us -> 456 us (1.15)
  the two profiles are of different devices: /device:TPU:2 before, /device:TPU:6 now
where the time goes in v3:
time: 456 us; the launch traced here: 447 us
  local copies, waits for them, and re-layouts  148 us (32%)
  waiting for transfers between devices  143 us (31%)
  other arithmetic  69 us (15%)
  starting transfers between devices  54.6 us (12%)
  matrix products  29.6 us (6%)
    ppermute x14, waiting for transfers between devices, ring_scatter(): got = lax.ppermute(send.astype(wire), axis, [(i, i ^ d) for i in range(n)])  54.4 us
    ppermute x8, waiting for transfers between devices, ring_gather_rows(): cur = lax.ppermute(cur, axis, [(i, (i + 1) % n) for i in range(n)])  50.2 us
    another operation x56, local copies, waits for them, and re-layouts, kernel_terms(): kernel_rows.append(jnp.stack(kernel_row))  33.4 us
    another operation x2, local copies, waits for them, and re-layouts, ring_scatter(): pairs = x.reshape(shape)  19.5 us
    add x14, other arithmetic, ring_scatter(): x = keep + got.astype(jnp.float32)  18.4 us
    ppermute x8, waiting for transfers between devices, butterfly_sum(): x = x + lax.ppermute(x, axis, [(i, i ^ d) for i in range(n)])  18.1 us
    reshape x2, local copies, waits for them, and re-layouts, gather_weights(): down_full = packed[:, half:].reshape(-1, down_shard.shape[1])  17 us
    reduce_sum x1, other arithmetic, layer_norm(): centered = convolved - jnp.mean(convolved, axis=-1, keepdims=True)  16.4 us
  transfers between devices with their start and end apart: 40, of which 29 were waited for; matrix products, arithmetic and copies ran while one was open for 37% of the time, Pallas kernels for 0%

profile of v3, /device:TPU:6, one launch (start us, length us, event | category | flops | bytes accessed | tf_op | source)
XLA Modules:
  0.0 447.1 jit_solution(5317986186367358217)
XLA Ops:
  4.7 4.7 %collective-permute-done.3 = bf16[528,128]{1,0:T(8,128)(2,1)S(1)} collective-permute-done((bf16[528,128]{1,0:T(8,128)(2,1)S(1)}, bf16[528,128]{1,0:T(8,128)(2,1)S(1)}, u32[]{:S(2)}, u32[]{:S(2)}) %collective-permute-start.3) | collective-permute-done | bytes 135200 | tf_op jit(solution)/shard_map/ppermute | solution.py:45
  12.9 5.6 %collective-permute-done.4 = bf16[1056,128]{1,0:T(8,128)(2,1)S(1)} collective-permute-done((bf16[1056,128]{1,0:T(8,128)(2,1)S(1)}, bf16[1056,128]{1,0:T(8,128)(2,1)S(1)}, u32[]{:S(2)}, u32[]{:S(2)}) %collective-permute-start.4) | collective-permute-done | bytes 270368 | tf_op jit(solution)/shard_map/ppermute | solution.py:45
  21.5 5.1 %collective-permute-done.5 = bf16[1056,128]{1,0:T(8,128)(2,1)S(1)} collective-permute-done((bf16[1056,128]{1,0:T(8,128)(2,1)S(1)}, bf16[1056,128]{1,0:T(8,128)(2,1)S(1)}, u32[]{:S(2)}, u32[]{:S(2)}) %collective-permute-start.5) | collective-permute-done | bytes 270368 | tf_op jit(solution)/shard_map/ppermute | solution.py:45
  31.1 3.3 collective-permute-start.1
  37.1 5.9 %collective-permute-done = bf16[1,3,32,768]{3,2,1,0:T(8,128)(2,1)S(1)} collective-permute-done((bf16[1,3,32,768]{3,2,1,0:T(8,128)(2,1)S(1)}, bf16[1,3,32,768]{3,2,1,0:T(8,128)(2,1)S(1)}, u32[]{:S(2)}, u32[]{:S(2)}) %collective-permute-start) | collective-permute-done | bytes 147488 | tf_op jit(solution)/shard_map/ppermute | solution.py:90
  43.6 4.0 collective-permute-start.11
  47.6 8.2 %collective-permute-done.7 = bf16[4224,128]{1,0:T(8,128)(2,1)} collective-permute-done((bf16[4224,128]{1,0:T(8,128)(2,1)}, bf16[4224,128]{1,0:T(8,128)(2,1)}, u32[]{:S(2)}, u32[]{:S(2)}) %collective-permute-start.7) | collective-permute-done | bytes 1081376 | tf_op jit(solution)/shard_map/ppermute | solution.py:45
  56.0 16.4 %fusion.219 = (f32[16,32]{1,0:T(8,128)S(1)}, f32[1,16,32,768]{3,2,1,0:T(8,128)S(1)}) fusion(bf16[1,22,38,768]{3,2,1,0:T(8,128)(2,1)S(1)} %fusion.205, f32[768]{0:T(1024)S(1)} %get-tuple-element.104, f32[768]{0:T(1024)S(1)} %get-tuple-element.105, f32[768]{0:T(1024)S(1)} %get-tuple-element.58, bf16[1,3,32,768]{3,2,1,0:T(8,128)(2,1)S(1)} %collective-permute-done.1, ...), kind=kLoop, calls=%fused_computation.508 | loop fusion | flops 60554752 | bytes 35837440 | tf_op jit(solution)/shard_map/reduce_sum | solution.py:136
  74.0 3.2 collective-permute-start.12
  80.2 4.4 broadcast_in_dim.58
  89.3 8.6 %collective-permute-done.12 = bf16[4224,128]{1,0:T(8,128)(2,1)S(1)} collective-permute-done((bf16[4224,128]{1,0:T(8,128)(2,1)S(1)}, bf16[4224,128]{1,0:T(8,128)(2,1)S(1)}, u32[]{:S(2)}, u32[]{:S(2)}) %collective-permute-start.12) | collective-permute-done | bytes 1081376 | tf_op jit(solution)/shard_map/ppermute | solution.py:49
  97.9 3.4 collective-permute-start.13
  106.4 20.0 %collective-permute-done.10 = bf16[4224,128]{1,0:T(8,128)(2,1)S(1)} collective-permute-done((bf16[4224,128]{1,0:T(8,128)(2,1)S(1)}, bf16[4224,128]{1,0:T(8,128)(2,1)S(1)}, u32[]{:S(2)}, u32[]{:S(2)}) %collective-permute-start.10) | collective-permute-done | bytes 1081376 | tf_op jit(solution)/shard_map/ppermute | solution.py:45
  130.7 7.6 %copy.23 = bf16[4,8,4,264,128]{4,3,2,1,0:T(8,128)(2,1)} copy(bf16[4,8,4,264,128]{4,3,2,0,1:T(8,128)(2,1)} %bitcast.4) | data formatting | bytes 17301504 | tf_op jit(solution)/shard_map/transpose | solution.py:61
  138.3 9.1 %fusion.221 = (bf16[128,132,128]{2,1,0:T(8,128)(2,1)}, bf16[128,132,128]{2,1,0:T(8,128)(2,1)}) fusion(bf16[128,264,128]{2,1,0:T(8,128)(2,1)} %bitcast.93), kind=kLoop, calls=%fused_computation.509 | loop fusion | bytes 17301504 | tf_op jit(solution)/shard_map/slice | solution.py:63
  147.4 8.6 %reshape.536 = bf16[2816,768,1]{1,0,2:T(8,128)(2,1)} reshape(bf16[128,132,128]{2,1,0:T(8,128)(2,1)} %get-tuple-element.111) | data formatting | bytes 8650752 | tf_op jit(solution)/shard_map/reshape | solution.py:63
  156.1 8.3 %reshape.525 = bf16[2816,768]{1,0:T(8,128)(2,1)} reshape(bf16[128,132,128]{2,1,0:T(8,128)(2,1)} %get-tuple-element.111) | data formatting | bytes 8650752 | tf_op jit(solution)/shard_map/reshape | solution.py:63
  164.4 8.8 %reshape.523 = bf16[768,2816]{1,0:T(8,128)(2,1)} reshape(bf16[128,132,128]{2,1,0:T(8,128)(2,1)} %get-tuple-element.112) | data formatting | bytes 8650752 | tf_op jit(solution)/shard_map/reshape | solution.py:62
  173.2 6.1 %multiply_convert_fusion = (bf16[512,2816]{1,0:T(8,128)(2,1)}, f32[512,2816]{1,0:T(8,128)S(1)}) fusion(bf16[512,768]{1,0:T(8,128)(2,1)} %bitcast.111, bf16[768,2816]{1,0:T(8,128)(2,1)} %reshape.523), kind=kOutput, calls=%fused_computation.52 | convolution fusion | flops 2221801472 | bytes 13762560 | tf_op jit(solution)/shard_map/dot_general | solution.py:176
  179.3 3.7 fusion.5
  185.6 5.8 %convolution_multiply_fusion.1 = f32[768,2816]{1,0:T(8,128)} fusion(bf16[512,768]{1,0:T(8,128)(2,1)S(1)} %bitcast.112, bf16[512,2816]{1,0:T(8,128)(2,1)S(1)} %fusion.5), kind=kOutput, calls=%fused_computation.44 | convolution fusion | flops 2216755200 | bytes 12320768 | tf_op jit(solution)/shard_map/dot_general | solution.py:188
  191.9 6.4 %fusion.104 = (f32[768]{0:T(1024)}, f32[768]{0:T(1024)}, f32[768]{0:T(1024)}, f32[768]{0:T(1024)}, f32[768]{0:T(1024)}, /*index=5*/f32[768]{0:T(1024)}, f32[768]...) fusion(bf16[1,22,38,768]{3,2,1,0:T(8,128)(2,1)S(1)} %fusion.205, ...), kind=kLoop, calls=%fused_computation.260 | loop fusion | flops 23972352 | bytes 18938368 | tf_op jit(solution)/shard_map/reduce_sum | solution.py:130
  198.2 4.6 %fusion.83 = (f32[768]{0:T(1024)}, f32[768]{0:T(1024)}, f32[768]{0:T(1024)}, f32[768]{0:T(1024)}, f32[768]{0:T(1024)}, /*index=5*/f32[768]{0:T(1024)}, f32[768]{...) fusion(f32[1,16,32,768]{3,2,1,0:T(8,128)S(1)} %get-tuple-elemen, ...), kind=kLoop, calls=%fused_computation.239 | loop fusion | flops 21613056 | bytes 16570368 | tf_op jit(solution)/shard_map/reduce_sum | solution.py:130
  205.5 4.0 collective-permute-start.15
  210.9 10.2 %reshape_reshape.6 = f32[4,8,2,1,2,1,6,2816]{7,6,4,2,1,0,5,3:T(8,128)} reshape(f32[768,2816]{1,0:T(8,128)} %convolution_multiply_fusion.1) | data formatting | bytes 17301504 | tf_op jit(solution)/shard_map/reshape;reshape | solution.py:25
  256.6 3.0 fusion.6
  263.6 5.8 %convolution_multiply_fusion = f32[2816,768]{1,0:T(8,128)} fusion(bf16[512,2816]{1,0:T(8,128)(2,1)S(1)} %copy-done.11, bf16[512,768]{1,0:T(8,128)(2,1)S(1)} %bitcast.110), kind=kOutput, calls=%fused_computation.43 | convolution fusion | flops 2216755200 | bytes 12320768 | tf_op jit(solution)/shard_map/dot_general | solution.py:179
  269.4 9.4 %reshape_reshape.7 = f32[4,8,2,1,2,1,22,768]{7,6,4,2,1,0,5,3:T(8,128)} reshape(f32[2816,768]{1,0:T(8,128)} %convolution_multiply_fusion) | data formatting | bytes 17301504 | tf_op jit(solution)/shard_map/reshape;reshape | solution.py:25
  285.6 5.7 %fusion.105 = bf16[1,16,32,768]{3,2,1,0:T(8,128)(2,1)} fusion(bf16[1,16,32,768]{3,2,1,0:T(8,128)(2,1)S(1)} %copy-done.3, bf16[16,32,2816]{2,1,0:T(8,128)(2,1)S(1)} %bitcast.113, bf16[2816,768,1]{1,0,2:T(8,128)(2,1)} %reshape.536), kind=kOutput, calls=%fused_computation.261 | convolution fusion | flops 2215772160 | bytes 8781824 | tf_op jit(solution)/shard_map/dot_general | solution.py:183
  291.2 4.5 %collective-permute-done.35 = f32[7,7,768]{2,1,0:T(8,128)S(1)} collective-permute-done((f32[7,7,768]{2,1,0:T(8,128)S(1)}, f32[7,7,768]{2,1,0:T(8,128)S(1)}, u32[]{:S(2)}, u32[]{:S(2)}) %collective-permute-start.35) | collective-permute-done | bytes 150560 | tf_op jit(solution)/shard_map/ppermute | solution.py:80
  295.8 4.3 collective-permute-start.36
  300.6 8.5 %collective-permute-done.36 = f32[7,7,768]{2,1,0:T(8,128)S(1)} collective-permute-done((f32[7,7,768]{2,1,0:T(8,128)S(1)}, f32[7,7,768]{2,1,0:T(8,128)S(1)}, u32[]{:S(2)}, u32[]{:S(2)}) %collective-permute-start.36) | collective-permute-done | bytes 150560 | tf_op jit(solution)/shard_map/ppermute | solution.py:80
  311.8 3.0 collective-permute-done.37
  316.3 4.8 %collective-permute-start.39 = (f32[7,7,768]{2,1,0:T(8,128)S(1)}, f32[7,7,768]{2,1,0:T(8,128)S(1)}, u32[]{:S(2)}, u32[]{:S(2)}) collective-permute-start(f32[7,7,768]{2,1,0:T(8,128)S(1)} %add.802), channel_id=1, source_target_pairs={{0,1},{1,0},{2,3},{3,2},{4,5},{5,4},{6,7},{7,6},{8,9},{9,8},{10,11... | collective-permute-start | bytes 451592 | tf_op jit(solution)/shard_map/ppermute | solution.py:80
  321.1 6.2 %bitcast_add_fusion.1 = f32[4,8,2,1,1,6,2816]{6,1,5,4,3,2,0:T(8,128)} fusion(f32[4,8,2,1,1,1,6,2816]{7,6,4,2,1,0,5,3:T(8,128)S(1)} %constant_dynamic-slice_fusion.4, bf16[4,8,2,1,1,6,2816]{6,1,5,4,3,2,0:T(8,128)(2,1)} %collective-permute-done.16), kind=kLoop, calls=%fused_computation.56 | loop fusion | flops 2162688 | bytes 10813440 | tf_op jit(solution)/shard_map/add | solution.py:30
  327.4 6.0 %reshape.528 = f32[4,4,2,2,1,1,6,2816]{7,2,1,6,3,0,5,4:T(2,128)} reshape(f32[4,8,2,1,1,6,2816]{6,1,5,4,3,2,0:T(8,128)} %bitcast_add_fusion.1) | data formatting | bytes 8650752 | tf_op jit(solution)/shard_map/reshape | solution.py:25
  333.4 4.2 constant_dynamic-slice_fusion.2
  339.5 12.6 %fusion.196 = bf16[1,16,32,768]{3,2,1,0:T(8,128)(2,1)} fusion(f32[1,22,32,768]{3,2,1,0:T(8,128)S(1)} %maximum_convert_fusion, f32[768]{0:T(1024)S(1)} %copy-done.18, f32[768]{0:T(1024)S(1)} %copy-done.20, f32[768]{0:T(1024)S(1)} %get-tuple-element.58, f32[768]{0:T(1024)S(1)} %get-tuple-element.59, f32[768]{0:T(1024)S(1)} %get-tuple-element.60, ...), kind=kLoop, calls=%fused_computation.352 | loop fusion | flops 40108032 | bytes 14948352 | tf_op jit(solution)/shard_map/convert_element_type | solution.py:209
  352.8 6.0 %bitcast_add_fusion = f32[4,8,2,1,1,22,768]{6,1,5,4,3,2,0:T(8,128)S(1)} fusion(f32[4,8,2,1,1,1,22,768]{7,6,4,2,1,0,5,3:T(8,128)} %constant_dynamic-slice_fusion.1, bf16[4,8,2,1,1,22,768]{6,1,5,4,3,2,0:T(8,128)(2,1)} %collective-permute-done.24), kind=kLoop, calls=%fused_computation.55 | loop fusion | flops 2162688 | bytes 10813440 | tf_op jit(solution)/shard_map/add | solution.py:30
  367.5 18.1 %collective-permute-done.25 = bf16[2,8,2,1,1,22,768]{6,2,5,1,4,3,0:T(2,128)(2,1)S(1)} collective-permute-done((bf16[2,8,2,1,1,22,768]{6,2,5,1,4,3,0:T(2,128)(2,1)S(1)}, bf16[2,8,2,1,1,22,768]{6,2,5,1,4,3,0:T(2,128)(2,1)S(1)}, u32[]{:S(2)}, u32[]{:S(2)}) %collective-permute-start.25) | collective-permute-done | bytes 1081376 | tf_op jit(solution)/shard_map/ppermute | solution.py:29
  396.7 6.4 %collective-permute-done.26 = bf16[1,8,2,1,1,22,768]{6,2,5,1,4,3,0:T(2,128)(2,1)S(1)} collective-permute-done((bf16[1,8,2,1,1,22,768]{6,2,5,1,4,3,0:T(2,128)(2,1)S(1)}, bf16[1,8,2,1,1,22,768]{6,2,5,1,4,3,0:T(2,128)(2,1)S(1)}, u32[]{:S(2)}, u32[]{:S(2)}) %collective-permute-start.26) | collective-permute-done | bytes 540704 | tf_op jit(solution)/shard_map/ppermute | solution.py:29
  405.4 6.1 %collective-permute-done.19 = bf16[4,1,2,1,1,6,2816]{6,2,5,1,0,4,3:T(2,128)(2,1)S(1)} collective-permute-done((bf16[4,1,2,1,1,6,2816]{6,2,5,1,0,4,3:T(2,128)(2,1)S(1)}, bf16[4,1,2,1,1,6,2816]{6,2,5,1,0,4,3:T(2,128)(2,1)S(1)}, u32[]{:S(2)}, u32[]{:S(2)}) %collective-permute-start.19) | collective-permute-done | bytes 270368 | tf_op jit(solution)/shard_map/ppermute | solution.py:29
  412.1 3.6 collective-permute-done.27
  420.3 5.2 %collective-permute-done.28 = bf16[1,2,2,1,1,22,768]{6,2,5,1,4,3,0:T(2,128)(2,1)S(1)} collective-permute-done((bf16[1,2,2,1,1,22,768]{6,2,5,1,4,3,0:T(2,128)(2,1)S(1)}, bf16[1,2,2,1,1,22,768]{6,2,5,1,4,3,0:T(2,128)(2,1)S(1)}, u32[]{:S(2)}, u32[]{:S(2)}) %collective-permute-start.28) | collective-permute-done | bytes 135200 | tf_op jit(solution)/shard_map/ppermute | solution.py:29
  425.7 3.1 collective-permute-start.29
  429.0 5.8 %collective-permute-done.29 = bf16[1,1,2,1,1,22,768]{6,2,5,1,4,3,0:T(2,128)(2,1)S(1)} collective-permute-done((bf16[1,1,2,1,1,22,768]{6,2,5,1,4,3,0:T(2,128)(2,1)S(1)}, bf16[1,1,2,1,1,22,768]{6,2,5,1,4,3,0:T(2,128)(2,1)S(1)}, u32[]{:S(2)}, u32[]{:S(2)}) %collective-permute-start.29) | collective-permute-done | bytes 67616 | tf_op jit(solution)/shard_map/ppermute | solution.py:29
  436.4 3.5 collective-permute-done.30
  442.0 4.0 collective-permute-done.31
  (353 shorter events, 127.6 us)
Async XLA Ops:
  2.4 1.3 collective-permute-start.2
  3.7 5.7 %collective-permute-start.3 = (bf16[528,128]{1,0:T(8,128)(2,1)S(1)}, bf16[528,128]{1,0:T(8,128)(2,1)S(1)}, u32[]{:S(2)}, u32[]{:S(2)}) collective-permute-start(bf16[528,128]{1,0:T(8,128)(2,1)S(1)} %constant_dynamic-update-slice_fusion.14), channel_id=1, source_target_pairs={{0,4},{4,0},{1,5},{5,1},{2,6},{6,2},{3,7},{7,3},{8,12},{12,8},{9,1... | collective-permute-start | bytes 405512 | tf_op jit(solution)/shard_map/ppermute | solution.py:45
  9.5 9.1 %collective-permute-start.4 = (bf16[1056,128]{1,0:T(8,128)(2,1)S(1)}, bf16[1056,128]{1,0:T(8,128)(2,1)S(1)}, u32[]{:S(2)}, u32[]{:S(2)}) collective-permute-start(bf16[1056,128]{1,0:T(8,128)(2,1)S(1)} %constant_dynamic-update-slice_fusion.12), channel_id=1, source_target_pairs={{0,64},{64,128},{128,192},{192,0},{1,65},{65,129},{129,193},{193,1... | collective-permute-start | bytes 811016 | tf_op jit(solution)/shard_map/ppermute | solution.py:45
  11.2 16.1 %collective-permute-start.6 = (bf16[1056,128]{1,0:T(8,128)(2,1)S(1)}, bf16[1056,128]{1,0:T(8,128)(2,1)S(1)}, u32[]{:S(2)}, u32[]{:S(2)}) collective-permute-start(bf16[1056,128]{1,0:T(8,128)(2,1)S(1)} %constant_dynamic-update-slice_fusion.12), channel_id=1, source_target_pairs={{0,192},{64,0},{128,64},{192,128},{1,193},{65,1},{129,65},{193,129... | collective-permute-start | bytes 811016 | tf_op jit(solution)/shard_map/ppermute | solution.py:49
  18.6 8.1 %collective-permute-start.5 = (bf16[1056,128]{1,0:T(8,128)(2,1)S(1)}, bf16[1056,128]{1,0:T(8,128)(2,1)S(1)}, u32[]{:S(2)}, u32[]{:S(2)}) collective-permute-start(bf16[1056,128]{1,0:T(8,128)(2,1)S(1)} %collective-permute-done.4), channel_id=1, source_target_pairs={{0,64},{64,128},{128,192},{192,0},{1,65},{65,129},{129,193},{193,1... | collective-permute-start | bytes 811016 | tf_op jit(solution)/shard_map/ppermute | solution.py:45
  28.1 27.7 %collective-permute-start.7 = (bf16[4224,128]{1,0:T(8,128)(2,1)}, bf16[4224,128]{1,0:T(8,128)(2,1)}, u32[]{:S(2)}, u32[]{:S(2)}) collective-permute-start(bf16[4224,128]{1,0:T(8,128)(2,1)} %constant_dynamic-update-slice_fusion.8), channel_id=1, source_target_pairs={{0,8},{8,16},{16,24},{24,32},{32,40},{40,48},{48,56},{56,0},{1,9},... | collective-permute-start | bytes 3244040 | tf_op jit(solution)/shard_map/ppermute | solution.py:45
  31.1 6.0 %collective-permute-start.1 = (bf16[1,3,32,768]{3,2,1,0:T(8,128)(2,1)S(1)}, bf16[1,3,32,768]{3,2,1,0:T(8,128)(2,1)S(1)}, u32[]{:S(2)}, u32[]{:S(2)}) collective-permute-start(bf16[1,3,32,768]{3,2,1,0:T(8,128)(2,1)S(1)} %get-tuple-element.117), channel_id=1, source_target_pairs={{1,0},{3,2},{5,4},{7,6},{9,8},{11,10},{13,12},{15,14},{17,16},{19,... | collective-permute-start | bytes 442376 | tf_op jit(solution)/shard_map/ppermute | solution.py:93
  34.4 8.5 %collective-permute-start = (bf16[1,3,32,768]{3,2,1,0:T(8,128)(2,1)S(1)}, bf16[1,3,32,768]{3,2,1,0:T(8,128)(2,1)S(1)}, u32[]{:S(2)}, u32[]{:S(2)}) collective-permute-start(bf16[1,3,32,768]{3,2,1,0:T(8,128)(2,1)S(1)} %get-tuple-element.116), channel_id=1, source_target_pairs={{0,1},{2,3},{4,5},{6,7},{8,9},{10,11},{12,13},{14,15},{16,17},{18,... | collective-permute-start | bytes 442376 | tf_op jit(solution)/shard_map/ppermute | solution.py:90
  36.5 35.9 %copy-start.21 = (f32[768]{0:T(1024)}, f32[768]{0:T(1024)S(1)}, u32[]{:S(2)}) copy-start(f32[768]{0:T(1024)S(1)} %get-tuple-element.76) | copy-start | bytes 9220
  36.5 35.9 %copy-start.23 = (f32[768]{0:T(1024)}, f32[768]{0:T(1024)S(1)}, u32[]{:S(2)}) copy-start(f32[768]{0:T(1024)S(1)} %get-tuple-element.77) | copy-start | bytes 9220
  36.5 35.9 %copy-start.25 = (f32[768]{0:T(1024)}, f32[768]{0:T(1024)S(1)}, u32[]{:S(2)}) copy-start(f32[768]{0:T(1024)S(1)} %get-tuple-element.78) | copy-start | bytes 9220
  36.5 35.9 %copy-start.27 = (f32[768]{0:T(1024)}, f32[768]{0:T(1024)S(1)}, u32[]{:S(2)}) copy-start(f32[768]{0:T(1024)S(1)} %get-tuple-element.79) | copy-start | bytes 9220
  36.6 35.9 %copy-start.29 = (f32[768]{0:T(1024)}, f32[768]{0:T(1024)S(1)}, u32[]{:S(2)}) copy-start(f32[768]{0:T(1024)S(1)} %get-tuple-element.80) | copy-start | bytes 9220
  36.6 35.9 %copy-start.31 = (f32[768]{0:T(1024)}, f32[768]{0:T(1024)S(1)}, u32[]{:S(2)}) copy-start(f32[768]{0:T(1024)S(1)} %get-tuple-element.81) | copy-start | bytes 9220
  36.6 35.9 %copy-start.33 = (f32[768]{0:T(1024)}, f32[768]{0:T(1024)S(1)}, u32[]{:S(2)}) copy-start(f32[768]{0:T(1024)S(1)} %get-tuple-element.82) | copy-start | bytes 9220
  36.6 35.9 %copy-start.35 = (f32[768]{0:T(1024)}, f32[768]{0:T(1024)S(1)}, u32[]{:S(2)}) copy-start(f32[768]{0:T(1024)S(1)} %get-tuple-element.83) | copy-start | bytes 9220
  43.6 30.5 %collective-permute-start.11 = (bf16[4224,128]{1,0:T(8,128)(2,1)}, bf16[4224,128]{1,0:T(8,128)(2,1)S(1)}, u32[]{:S(2)}, u32[]{:S(2)}) collective-permute-start(bf16[4224,128]{1,0:T(8,128)(2,1)} %constant_dynamic-update-slice_fusion.8), channel_id=1, source_target_pairs={{0,56},{8,0},{16,8},{24,16},{32,24},{40,32},{48,40},{56,48},{1,57}... | collective-permute-start | bytes 3244040 | tf_op jit(solution)/shard_map/ppermute | solution.py:49
  55.8 24.4 %collective-permute-start.8 = (bf16[4224,128]{1,0:T(8,128)(2,1)}, bf16[4224,128]{1,0:T(8,128)(2,1)S(1)}, u32[]{:S(2)}, u32[]{:S(2)}) collective-permute-start(bf16[4224,128]{1,0:T(8,128)(2,1)} %collective-permute-done.7), channel_id=1, source_target_pairs={{0,8},{8,16},{16,24},{24,32},{32,40},{40,48},{48,56},{56,0},{1,9},... | collective-permute-start | bytes 3244040 | tf_op jit(solution)/shard_map/ppermute | solution.py:45
  74.0 23.9 %collective-permute-start.12 = (bf16[4224,128]{1,0:T(8,128)(2,1)S(1)}, bf16[4224,128]{1,0:T(8,128)(2,1)S(1)}, u32[]{:S(2)}, u32[]{:S(2)}) collective-permute-start(bf16[4224,128]{1,0:T(8,128)(2,1)S(1)} %collective-permute-done.11), channel_id=1, source_target_pairs={{0,56},{8,0},{16,8},{24,16},{32,24},{40,32},{48,40},{56,48},{1,57}... | collective-permute-start | bytes 3244040 | tf_op jit(solution)/shard_map/ppermute | solution.py:49
  80.2 24.0 %collective-permute-start.9 = (bf16[4224,128]{1,0:T(8,128)(2,1)S(1)}, bf16[4224,128]{1,0:T(8,128)(2,1)S(1)}, u32[]{:S(2)}, u32[]{:S(2)}) collective-permute-start(bf16[4224,128]{1,0:T(8,128)(2,1)S(1)} %collective-permute-done.8), channel_id=1, source_target_pairs={{0,8},{8,16},{16,24},{24,32},{32,40},{40,48},{48,56},{56,0},{1,9},... | collective-permute-start | bytes 3244040 | tf_op jit(solution)/shard_map/ppermute | solution.py:45
  97.9 31.7 %collective-permute-start.13 = (bf16[4224,128]{1,0:T(8,128)(2,1)S(1)}, bf16[4224,128]{1,0:T(8,128)(2,1)S(1)}, u32[]{:S(2)}, u32[]{:S(2)}) collective-permute-start(bf16[4224,128]{1,0:T(8,128)(2,1)S(1)} %collective-permute-done.12), channel_id=1, source_target_pairs={{0,56},{8,0},{16,8},{24,16},{32,24},{40,32},{48,40},{56,48},{1,57}... | collective-permute-start | bytes 3244040 | tf_op jit(solution)/shard_map/ppermute | solution.py:49
  104.2 22.2 %collective-permute-start.10 = (bf16[4224,128]{1,0:T(8,128)(2,1)S(1)}, bf16[4224,128]{1,0:T(8,128)(2,1)S(1)}, u32[]{:S(2)}, u32[]{:S(2)}) collective-permute-start(bf16[4224,128]{1,0:T(8,128)(2,1)S(1)} %collective-permute-done.9), channel_id=1, source_target_pairs={{0,8},{8,16},{16,24},{24,32},{32,40},{40,48},{48,56},{56,0},{1,9},... | collective-permute-start | bytes 3244040 | tf_op jit(solution)/shard_map/ppermute | solution.py:45
  205.5 109.4 %collective-permute-start.15 = (bf16[1,3,32,768]{3,2,1,0:T(8,128)(2,1)}, bf16[1,3,32,768]{3,2,1,0:T(8,128)(2,1)}, u32[]{:S(2)}, u32[]{:S(2)}) collective-permute-start(bf16[1,3,32,768]{3,2,1,0:T(8,128)(2,1)} %get-tuple-element.115), channel_id=1, source_target_pairs={{1,0},{3,2},{5,4},{7,6},{9,8},{11,10},{13,12},{15,14},{17,16},{19,... | collective-permute-start | bytes 442376 | tf_op jit(solution)/shard_map/ppermute | solution.py:93
  209.4 105.5 %collective-permute-start.14 = (bf16[1,3,32,768]{3,2,1,0:T(8,128)(2,1)}, bf16[1,3,32,768]{3,2,1,0:T(8,128)(2,1)}, u32[]{:S(2)}, u32[]{:S(2)}) collective-permute-start(bf16[1,3,32,768]{3,2,1,0:T(8,128)(2,1)} %get-tuple-element.114), channel_id=1, source_target_pairs={{0,1},{2,3},{4,5},{6,7},{8,9},{10,11},{12,13},{14,15},{16,17},{18,... | collective-permute-start | bytes 442376 | tf_op jit(solution)/shard_map/ppermute | solution.py:90
  256.5 5.5 %collective-permute-start.32 = (f32[7,7,768]{2,1,0:T(8,128)S(1)}, f32[7,7,768]{2,1,0:T(8,128)S(1)}, u32[]{:S(2)}, u32[]{:S(2)}) collective-permute-start(f32[7,7,768]{2,1,0:T(8,128)S(1)} %broadcast_multiply_fusion), channel_id=1, source_target_pairs={{0,64},{64,0},{128,192},{192,128},{1,65},{65,1},{129,193},{193,129... | collective-permute-start | bytes 451592 | tf_op jit(solution)/shard_map/ppermute | solution.py:80
  261.6 59.5 %collective-permute-start.16 = (bf16[4,8,2,1,1,6,2816]{6,1,5,4,3,2,0:T(8,128)(2,1)}, bf16[4,8,2,1,1,6,2816]{6,1,5,4,3,2,0:T(8,128)(2,1)}, u32[]{:S(2)}, u32[]{:S(2)}) collective-permute-start(bf16[4,8,2,1,1,6,2816]{6,1,5,4,3,2,0:T(8,128)(2,1)} %copy.25), channel_id=1, source_target_pairs={{0,2},{2,0},{1,3},{3,1},{4,6},{6,4},{5,7},{7,5},{8,10},{10,8},{9,1... | collective-permute-start | bytes 6488072 | tf_op jit(solution)/shard_map/ppermute | solution.py:29
  262.0 16.7 %collective-permute-start.33 = (f32[7,7,768]{2,1,0:T(8,128)S(1)}, f32[7,7,768]{2,1,0:T(8,128)S(1)}, u32[]{:S(2)}, u32[]{:S(2)}) collective-permute-start(f32[7,7,768]{2,1,0:T(8,128)S(1)} %fusion.218), channel_id=1, source_target_pairs={{0,128},{64,192},{128,0},{192,64},{1,129},{65,193},{129,1},{193,65... | collective-permute-start | bytes 451592 | tf_op jit(solution)/shard_map/ppermute | solution.py:80
  278.8 6.6 %collective-permute-start.34 = (f32[7,7,768]{2,1,0:T(8,128)S(1)}, f32[7,7,768]{2,1,0:T(8,128)S(1)}, u32[]{:S(2)}, u32[]{:S(2)}) collective-permute-start(f32[7,7,768]{2,1,0:T(8,128)S(1)} %add.797), channel_id=1, source_target_pairs={{0,8},{8,0},{16,24},{24,16},{32,40},{40,32},{48,56},{56,48},{1,9},... | collective-permute-start | bytes 451592 | tf_op jit(solution)/shard_map/ppermute | solution.py:80
  283.7 69.0 %collective-permute-start.24 = (bf16[4,8,2,1,1,22,768]{6,1,5,4,3,2,0:T(8,128)(2,1)}, bf16[4,8,2,1,1,22,768]{6,1,5,4,3,2,0:T(8,128)(2,1)}, u32[]{:S(2)}, u32[]{:S(2)}) collective-permute-start(bf16[4,8,2,1,1,22,768]{6,1,5,4,3,2,0:T(8,128)(2,1)} %copy.29), channel_id=1, source_target_pairs={{0,2},{2,0},{1,3},{3,1},{4,6},{6,4},{5,7},{7,5},{8,10},{10,8},{9,1... | collective-permute-start | bytes 6488072 | tf_op jit(solution)/shard_map/ppermute | solution.py:29
  285.4 10.4 %collective-permute-start.35 = (f32[7,7,768]{2,1,0:T(8,128)S(1)}, f32[7,7,768]{2,1,0:T(8,128)S(1)}, u32[]{:S(2)}, u32[]{:S(2)}) collective-permute-start(f32[7,7,768]{2,1,0:T(8,128)S(1)} %add.798), channel_id=1, source_target_pairs={{0,16},{8,24},{16,0},{24,8},{32,48},{40,56},{48,32},{56,40},{1,17}... | collective-permute-start | bytes 451592 | tf_op jit(solution)/shard_map/ppermute | solution.py:80
  295.8 13.2 %collective-permute-start.36 = (f32[7,7,768]{2,1,0:T(8,128)S(1)}, f32[7,7,768]{2,1,0:T(8,128)S(1)}, u32[]{:S(2)}, u32[]{:S(2)}) collective-permute-start(f32[7,7,768]{2,1,0:T(8,128)S(1)} %add.799), channel_id=1, source_target_pairs={{0,32},{8,40},{16,48},{24,56},{32,0},{40,8},{48,16},{56,24},{1,33}... | collective-permute-start | bytes 451592 | tf_op jit(solution)/shard_map/ppermute | solution.py:80
  309.1 5.7 %collective-permute-start.37 = (f32[7,7,768]{2,1,0:T(8,128)S(1)}, f32[7,7,768]{2,1,0:T(8,128)S(1)}, u32[]{:S(2)}, u32[]{:S(2)}) collective-permute-start(f32[7,7,768]{2,1,0:T(8,128)S(1)} %add.800), channel_id=1, source_target_pairs={{0,4},{4,0},{1,5},{5,1},{2,6},{6,2},{3,7},{7,3},{8,12},{12,8},{9,1... | collective-permute-start | bytes 451592 | tf_op jit(solution)/shard_map/ppermute | solution.py:80
  314.8 1.5 collective-permute-start.38
  316.3 35.7 %collective-permute-start.39 = (f32[7,7,768]{2,1,0:T(8,128)S(1)}, f32[7,7,768]{2,1,0:T(8,128)S(1)}, u32[]{:S(2)}, u32[]{:S(2)}) collective-permute-start(f32[7,7,768]{2,1,0:T(8,128)S(1)} %add.802), channel_id=1, source_target_pairs={{0,1},{1,0},{2,3},{3,2},{4,5},{5,4},{6,7},{7,6},{8,9},{9,8},{10,11... | collective-permute-start | bytes 451592 | tf_op jit(solution)/shard_map/ppermute | solution.py:80
  338.9 26.1 %collective-permute-start.17 = (bf16[4,4,2,1,1,6,2816]{6,2,5,1,0,4,3:T(2,128)(2,1)S(1)}, bf16[4,4,2,1,1,6,2816]{6,2,5,1,0,4,3:T(2,128)(2,1)S(1)}, u32[]{:S(2)}, u32[]{:S(2)}) collective-permute-start(bf16[4,4,2,1,1,6,2816]{6,2,5,1,0,4,3:T(2,128)(2,1)S(1)} %bitcast.118), channel_id=1, source_target_pairs={{0,8},{8,0},{16,24},{24,16},{32,40},{40,32},{48,56},{56,48},{1,9},... | collective-permute-start | bytes 3244040 | tf_op jit(solution)/shard_map/ppermute | solution.py:29
  359.7 25.9 %collective-permute-start.25 = (bf16[2,8,2,1,1,22,768]{6,2,5,1,4,3,0:T(2,128)(2,1)S(1)}, bf16[2,8,2,1,1,22,768]{6,2,5,1,4,3,0:T(2,128)(2,1)S(1)}, u32[]{:S(2)}, u32[]{:S(2)}) collective-permute-start(bf16[2,8,2,1,1,22,768]{6,2,5,1,4,3,0:T(2,128)(2,1)S(1)} %bitcast.119), channel_id=1, source_target_pairs={{0,64},{64,0},{128,192},{192,128},{1,65},{65,1},{129,193},{193,129... | collective-permute-start | bytes 3244040 | tf_op jit(solution)/shard_map/ppermute | solution.py:29
  366.9 26.1 %collective-permute-start.18 = (bf16[4,2,2,1,1,6,2816]{6,2,5,1,0,4,3:T(2,128)(2,1)S(1)}, bf16[4,2,2,1,1,6,2816]{6,2,5,1,0,4,3:T(2,128)(2,1)S(1)}, u32[]{:S(2)}, u32[]{:S(2)}) collective-permute-start(bf16[4,2,2,1,1,6,2816]{6,2,5,1,0,4,3:T(2,128)(2,1)S(1)} %fusion.212), channel_id=1, source_target_pairs={{0,16},{8,24},{16,0},{24,8},{32,48},{40,56},{48,32},{56,40},{1,17}... | collective-permute-start | bytes 1622024 | tf_op jit(solution)/shard_map/ppermute | solution.py:29
  388.2 14.9 %collective-permute-start.26 = (bf16[1,8,2,1,1,22,768]{6,2,5,1,4,3,0:T(2,128)(2,1)S(1)}, bf16[1,8,2,1,1,22,768]{6,2,5,1,4,3,0:T(2,128)(2,1)S(1)}, u32[]{:S(2)}, u32[]{:S(2)}) collective-permute-start(bf16[1,8,2,1,1,22,768]{6,2,5,1,4,3,0:T(2,128)(2,1)S(1)} %dynamic-slice_convert_fusion.3), channel_id=1, source_target_pairs={{0,128},{64,192},{128,0},{192,64},{1,129},{65,193},{129,1},{193,65... | collective-permute-start | bytes 1622024 | tf_op jit(solution)/shard_map/ppermute | solution.py:29
  393.8 17.7 %collective-permute-start.19 = (bf16[4,1,2,1,1,6,2816]{6,2,5,1,0,4,3:T(2,128)(2,1)S(1)}, bf16[4,1,2,1,1,6,2816]{6,2,5,1,0,4,3:T(2,128)(2,1)S(1)}, u32[]{:S(2)}, u32[]{:S(2)}) collective-permute-start(bf16[4,1,2,1,1,6,2816]{6,2,5,1,0,4,3:T(2,128)(2,1)S(1)} %dynamic-slice_convert_fusion.6), channel_id=1, source_target_pairs={{0,32},{8,40},{16,48},{24,56},{32,0},{40,8},{48,16},{56,24},{1,33}... | collective-permute-start | bytes 811016 | tf_op jit(solution)/shard_map/ppermute | solution.py:29
  403.9 11.7 %collective-permute-start.27 = (bf16[1,4,2,1,1,22,768]{6,2,5,1,4,3,0:T(2,128)(2,1)S(1)}, bf16[1,4,2,1,1,22,768]{6,2,5,1,4,3,0:T(2,128)(2,1)S(1)}, u32[]{:S(2)}, u32[]{:S(2)}) collective-permute-start(bf16[1,4,2,1,1,22,768]{6,2,5,1,4,3,0:T(2,128)(2,1)S(1)} %fusion.213), channel_id=1, source_target_pairs={{0,8},{8,0},{16,24},{24,16},{32,40},{40,32},{48,56},{56,48},{1,9},... | collective-permute-start | bytes 811016 | tf_op jit(solution)/shard_map/ppermute | solution.py:29
  411.9 5.5 %collective-permute-start.20 = (bf16[2,1,2,1,1,6,2816]{6,2,5,0,4,3,1:T(2,128)(2,1)S(1)}, bf16[2,1,2,1,1,6,2816]{6,2,5,0,4,3,1:T(2,128)(2,1)S(1)}, u32[]{:S(2)}, u32[]{:S(2)}) collective-permute-start(bf16[2,1,2,1,1,6,2816]{6,2,5,0,4,3,1:T(2,128)(2,1)S(1)} %fusion.214), channel_id=1, source_target_pairs={{0,64},{64,0},{128,192},{192,128},{1,65},{65,1},{129,193},{193,129... | collective-permute-start | bytes 405512 | tf_op jit(solution)/shard_map/ppermute | solution.py:29
  416.1 9.4 %collective-permute-start.28 = (bf16[1,2,2,1,1,22,768]{6,2,5,1,4,3,0:T(2,128)(2,1)S(1)}, bf16[1,2,2,1,1,22,768]{6,2,5,1,4,3,0:T(2,128)(2,1)S(1)}, u32[]{:S(2)}, u32[]{:S(2)}) collective-permute-start(bf16[1,2,2,1,1,22,768]{6,2,5,1,4,3,0:T(2,128)(2,1)S(1)} %fusion.215), channel_id=1, source_target_pairs={{0,16},{8,24},{16,0},{24,8},{32,48},{40,56},{48,32},{56,40},{1,17}... | collective-permute-start | bytes 405512 | tf_op jit(solution)/shard_map/ppermute | solution.py:29
  417.6 11.2 %collective-permute-start.21 = (bf16[1,1,2,1,1,6,2816]{6,2,5,0,4,3,1:T(2,128)(2,1)S(1)}, bf16[1,1,2,1,1,6,2816]{6,2,5,0,4,3,1:T(2,128)(2,1)S(1)}, u32[]{:S(2)}, u32[]{:S(2)}) collective-permute-start(bf16[1,1,2,1,1,6,2816]{6,2,5,0,4,3,1:T(2,128)(2,1)S(1)} %dynamic-slice_convert_fusion.10), channel_id=1, source_target_pairs={{0,128},{64,192},{128,0},{192,64},{1,129},{65,193},{129,1},{193,65... | collective-permute-start | bytes 202760 | tf_op jit(solution)/shard_map/ppermute | solution.py:29
  425.7 9.1 %collective-permute-start.29 = (bf16[1,1,2,1,1,22,768]{6,2,5,1,4,3,0:T(2,128)(2,1)S(1)}, bf16[1,1,2,1,1,22,768]{6,2,5,1,4,3,0:T(2,128)(2,1)S(1)}, u32[]{:S(2)}, u32[]{:S(2)}) collective-permute-start(bf16[1,1,2,1,1,22,768]{6,2,5,1,4,3,0:T(2,128)(2,1)S(1)} %dynamic-slice_convert_fusion.9), channel_id=1, source_target_pairs={{0,32},{8,40},{16,48},{24,56},{32,0},{40,8},{48,16},{56,24},{1,33}... | collective-permute-start | bytes 202760 | tf_op jit(solution)/shard_map/ppermute | solution.py:29
  428.9 6.1 %collective-permute-start.22 = (bf16[1,1,1,1,1,6,2816]{6,2,5,0,4,3,1:T(2,128)(2,1)S(1)}, bf16[1,1,1,1,1,6,2816]{6,2,5,0,4,3,1:T(2,128)(2,1)S(1)}, u32[]{:S(2)}, u32[]{:S(2)}) collective-permute-start(bf16[1,1,1,1,1,6,2816]{6,2,5,0,4,3,1:T(2,128)(2,1)S(1)} %dynamic-slice_convert_fusion.12), channel_id=1, source_target_pairs={{0,4},{4,0},{1,5},{5,1},{2,6},{6,2},{3,7},{7,3},{8,12},{12,8},{9,1... | collective-permute-start | bytes 101384 | tf_op jit(solution)/shard_map/ppermute | solution.py:29
  435.0 5.0 %collective-permute-start.30 = (bf16[1,1,1,1,1,22,768]{6,2,5,1,4,3,0:T(2,128)(2,1)S(1)}, bf16[1,1,1,1,1,22,768]{6,2,5,1,4,3,0:T(2,128)(2,1)S(1)}, u32[]{:S(2)}, u32[]{:S(2)}) collective-permute-start(bf16[1,1,1,1,1,22,768]{6,2,5,1,4,3,0:T(2,128)(2,1)S(1)} %dynamic-slice_convert_fusion.11), channel_id=1, source_target_pairs={{0,4},{4,0},{1,5},{5,1},{2,6},{6,2},{3,7},{7,3},{8,12},{12,8},{9,1... | collective-permute-start | bytes 101384 | tf_op jit(solution)/shard_map/ppermute | solution.py:29
  435.2 6.1 %collective-permute-start.23 = (f32[6,2816]{1,0:T(8,128)S(1)}, f32[6,2816]{1,0:T(8,128)S(1)}, u32[]{:S(2)}, u32[]{:S(2)}) collective-permute-start(f32[6,2816]{1,0:T(8,128)S(1)} %bitcast.120), channel_id=1, source_target_pairs={{0,1},{1,0},{2,3},{3,2},{4,5},{5,4},{6,7},{7,6},{8,9},{9,8},{10,11... | collective-permute-start | bytes 202760 | tf_op jit(solution)/shard_map/ppermute | solution.py:73
  440.1 5.9 %collective-permute-start.31 = (f32[22,768]{1,0:T(8,128)S(1)}, f32[22,768]{1,0:T(8,128)S(1)}, u32[]{:S(2)}, u32[]{:S(2)}) collective-permute-start(f32[22,768]{1,0:T(8,128)S(1)} %bitcast.121), channel_id=1, source_target_pairs={{0,1},{1,0},{2,3},{3,2},{4,5},{5,4},{6,7},{7,6},{8,9},{9,8},{10,11... | collective-permute-start | bytes 202760 | tf_op jit(solution)/shard_map/ppermute | solution.py:73
  (64 other events, 774.5 us)
